TPU v7x, 512 devices: a whole 4x8x8 slice. The times are simulated.
512 devices in a mesh: snap: 4 (over x), space: 128 (over z, y, core).
Axes of the slice: x: 4, y: 8, z: 8, core: 2. Of those that a mesh axis runs over, the one named last changes fastest.
Arguments:
- field_in: bfloat16 [4, 128, 32, 32, 256], P('snap', 'space'), may hold values from -6 to 6
- ocean_mask: int32 [128, 32, 32], P('space'), may hold values 0 or 1
- cotangent: bfloat16 [4, 128, 32, 32, 256], P('snap', 'space'), may hold values from -6 to 6
- w_first: bfloat16 [3, 3, 256, 128], replicated, may hold values from -0.125 to 0.125
- b_first: float32 [128], replicated, may hold values from -3 to 3
- w_second: bfloat16 [3, 3, 128, 256], replicated, may hold values from -0.1875 to 0.1875
- b_second: float32 [256], replicated, may hold values from -3 to 3
Outputs:
- field_out: bfloat16 [4, 128, 32, 32, 256], P('snap', 'space')
- grad_field: bfloat16 [4, 128, 32, 32, 256], P('snap', 'space')
- grad_w_first: float32 [3, 3, 256, 128], P(None, None, 'space')
- grad_w_second: float32 [3, 3, 128, 256], P(None, None, 'space')
- grad_b_first: float32 [128], P('space')
- grad_b_second: float32 [256], P('space')
All inputs are finite; a program needn't handle non-finite values. No bound on the sum of `ocean_mask` on one device may be relied on, other than what follows from the above.
Results may differ from a plain program's by a relative error of at most 0.014.
Values may be sent and summed in bfloat16 or wider, within the bound.
No kernel may reach another device: no remote copies, remote signals or barrier semaphores. Data moves between devices by JAX's collectives and lax.ppermute only.
A program may use at most 64 MiB of HBM per device.

v0:
```python
import math

import jax
import jax.numpy as jnp
from jax import lax
from jax.sharding import PartitionSpec as P

DEV_COLS = 4


ROOT_HALF = 0.7071067811865476
INV_ROOT_TWO_PI = 0.3989422804014327


def from_behind(array, axis, by):
    length = lax.axis_size(axis)
    return lax.ppermute(array, axis, [(i, (i + by) % length) for i in range(length)])


def gelu_value(pre):
    return 0.5 * pre * (1.0 + lax.erf(pre * ROOT_HALF))


def gelu_slope(pre):
    return (
        0.5 * (1.0 + lax.erf(pre * ROOT_HALF)) + pre * jnp.exp(-0.5 * pre * pre) * INV_ROOT_TWO_PI
    )


def dilated(padded, kernel):
    return lax.conv_general_dilated(
        padded[None],
        kernel,
        (1, 1),
        "VALID",
        rhs_dilation=(2, 2),
        dimension_numbers=("NHWC", "HWIO", "NHWC"),
        preferred_element_type=jnp.float32,
    )[0]


def flipped(kernel):
    return jnp.swapaxes(kernel[::-1, ::-1], 2, 3)


def tap_sums(padded, grad_out):
    span_y = grad_out.shape[0]
    span_x = grad_out.shape[1]
    flat_out = grad_out.reshape(span_y * span_x, grad_out.shape[2])
    tap_rows = []
    for tap_y in range(3):
        tap_line = []
        for tap_x in range(3):
            window = padded[2 * tap_y : 2 * tap_y + span_y, 2 * tap_x : 2 * tap_x + span_x].reshape(
                span_y * span_x, padded.shape[2]
            )
            tap_line.append(
                lax.dot_general(
                    window, flat_out, (((0,), (0,)), ((), ())), preferred_element_type=jnp.float32
                )
            )
        tap_rows.append(jnp.stack(tap_line))
    return jnp.stack(tap_rows)


def grid_halo(region):
    count = lax.axis_size("space")
    position = (lax.axis_index("space") + 1) % count
    column = position % DEV_COLS
    line = position // DEV_COLS
    last_line = count // DEV_COLS - 1
    strips = []
    for offset in (1, -1):
        edge_cells = region[:, -2:] if offset == 1 else region[:, :2]
        arrived = from_behind(edge_cells, "space", offset)
        inside = column != 0 if offset == 1 else column != DEV_COLS - 1
        strips.append(jnp.where(inside, arrived, jnp.zeros_like(arrived)))
    widened = jnp.concatenate([strips[0], region, strips[1]], axis=1)
    row_bands = []
    for offset in (DEV_COLS, -DEV_COLS):
        edge_cells = widened[-2:] if offset > 0 else widened[:2]
        arrived = from_behind(edge_cells, "space", offset)
        inside = line != 0 if offset > 0 else line != last_line
        row_bands.append(jnp.where(inside, arrived, jnp.zeros_like(arrived)))
    return jnp.concatenate([row_bands[0], widened, row_bands[1]], axis=0)


def local(field_in, ocean_mask, cotangent, w_first, b_first, w_second, b_second):
    region = field_in[0, 0]
    upstream = cotangent[0, 0]
    ocean = ocean_mask[0].astype(jnp.float32)[:, :, None]
    total = (
        field_in.shape[0]
        * lax.axis_size("snap")
        * lax.axis_size("space")
        * region.shape[0]
        * region.shape[1]
    )
    scale = 1.0 / math.sqrt(float(total))
    source_pad = grid_halo(region)
    pre = dilated(source_pad, w_first) + b_first
    hidden = (ocean * gelu_value(pre)).astype(jnp.bfloat16)
    hidden_pad = grid_halo(hidden)
    mixed = dilated(hidden_pad, w_second) + b_second
    field_out = (region.astype(jnp.float32) + ocean * mixed).astype(jnp.bfloat16)
    g_mixed = (ocean * upstream.astype(jnp.float32)).astype(jnp.bfloat16)
    grad_wb = tap_sums(hidden_pad, g_mixed)
    grad_bb = jnp.sum(g_mixed.astype(jnp.float32), axis=(0, 1))
    mixed_pad = grid_halo(g_mixed)
    g_hidden = dilated(mixed_pad, flipped(w_second))
    g_pre = (ocean * g_hidden * gelu_slope(pre)).astype(jnp.bfloat16)
    pre_pad = grid_halo(g_pre)
    g_input = (upstream.astype(jnp.float32) + dilated(pre_pad, flipped(w_first))).astype(
        jnp.bfloat16
    )
    grad_wa = tap_sums(source_pad, g_pre)
    grad_ba = jnp.sum(g_pre.astype(jnp.float32), axis=(0, 1))
    shares = (
        lax.psum_scatter(grad_wa, "space", scatter_dimension=2, tiled=True),
        lax.psum_scatter(grad_wb, "space", scatter_dimension=2, tiled=True),
        lax.psum_scatter(grad_ba, "space", scatter_dimension=0, tiled=True),
        lax.psum_scatter(grad_bb, "space", scatter_dimension=0, tiled=True),
    )
    summed = lax.psum((shares[0], shares[1], shares[2], shares[3]), "snap")
    return (
        field_out[None, None],
        g_input[None, None],
        summed[0] * scale,
        summed[1] * scale,
        summed[2] * scale,
        summed[3] * scale,
    )


def solution(mesh):
    placed = (
        P("snap", "space", None, None, None),
        P("space", None, None),
        P("snap", "space", None, None, None),
        P(),
        P(),
        P(),
        P(),
    )
    return jax.shard_map(
        local,
        mesh=mesh,
        in_specs=placed,
        out_specs=(
            P("snap", "space", None, None, None),
            P("snap", "space", None, None, None),
            P(None, None, "space", None),
            P(None, None, "space", None),
            P("space"),
            P("space"),
        ),
        check_vma=False,
    )
```

profile of v0, /device:TPU:6, one launch (start us, length us, event | category | flops | bytes accessed | tf_op | source)
XLA Modules:
  0.0 390.8 jit_solution(18005717857024186461)
XLA Ops:
  7.2 0.8 convert_bitcast_fusion.1
  8.1 1.3 convert_reduce_fusion
  9.4 1.9 collective-permute-start.8
  11.3 1.0 fusion.102
  12.3 3.6 collective-permute-start
  15.9 11.6 %collective-permute-start.1 = (bf16[32,2,256]{2,1,0:T(2,128)(2,1)S(1)}, bf16[32,2,256]{2,1,0:T(2,128)(2,1)S(1)}, u32[]{:S(2)}, u32[]{:S(2)}) collective-permute-start(bf16[32,2,256]{2,1,0:T(2,128)(2,1)S(1)} %get-tuple-element.32), channel_id=1, source_target_pairs={{0,127},{1,0},{2,1},{3,2},{4,3},{5,4},{6,5},{7,6},{8,7},{9,8},{10,... | collective-permute-start | bytes 98312 | tf_op jit(solution)/shard_map/ppermute | solution.py:17
  27.6 2.6 collective-permute-start.9
  30.3 1.4 collective-permute-done.9
  31.8 1.9 collective-permute-start.10
  33.9 1.9 collective-permute-start.2
  35.8 8.1 %collective-permute-start.3 = (bf16[2,36,256]{2,1,0:T(8,128)(2,1)S(1)}, bf16[2,36,256]{2,1,0:T(8,128)(2,1)S(1)}, u32[]{:S(2)}, u32[]{:S(2)}) collective-permute-start(bf16[2,36,256]{2,1,0:T(8,128)(2,1)S(1)} %get-tuple-element.25), channel_id=1, source_target_pairs={{0,124},{1,125},{2,126},{3,127},{4,0},{5,1},{6,2},{7,3},{8,4},{9,5... | collective-permute-start | bytes 110600 | tf_op jit(solution)/shard_map/ppermute | solution.py:17
  44.0 4.8 %collective-permute-start.11 = (bf16[2,36,256]{2,1,0:T(8,128)(2,1)S(1)}, bf16[2,36,256]{2,1,0:T(8,128)(2,1)S(1)}, u32[]{:S(2)}, u32[]{:S(2)}) collective-permute-start(bf16[2,36,256]{2,1,0:T(8,128)(2,1)S(1)} %get-tuple-element.23), channel_id=1, source_target_pairs={{0,124},{1,125},{2,126},{3,127},{4,0},{5,1},{6,2},{7,3},{8,4},{9,5... | collective-permute-start | bytes 110600 | tf_op jit(solution)/shard_map/ppermute | solution.py:17
  48.8 1.9 collective-permute-done.11
  50.8 0.4 maximum_bitcast_fusion.1
  51.7 0.7 copy-done.5
  52.5 1.7 fusion.18
  54.4 0.4 maximum_bitcast_fusion
  55.7 1.8 multiply_multiply_fusion.2
  57.7 0.8 convert_reduce_fusion.1
  59.3 0.4 maximum_maximum_fusion
  61.9 0.6 fusion.67
  62.6 1.9 collective-permute-start.4
  64.5 7.0 %collective-permute-start.5 = (bf16[32,2,128]{2,1,0:T(2,128)(2,1)S(1)}, bf16[32,2,128]{2,1,0:T(2,128)(2,1)S(1)}, u32[]{:S(2)}, u32[]{:S(2)}) collective-permute-start(bf16[32,2,128]{2,1,0:T(2,128)(2,1)S(1)} %get-tuple-element.42), channel_id=1, source_target_pairs={{0,127},{1,0},{2,1},{3,2},{4,3},{5,4},{6,5},{7,6},{8,7},{9,8},{10,... | collective-permute-start | bytes 49160 | tf_op jit(solution)/shard_map/ppermute | solution.py:17
  71.5 1.9 collective-permute-start.12
  73.4 7.1 %collective-permute-start.13 = (bf16[32,2,128]{2,1,0:T(2,128)(2,1)S(1)}, bf16[32,2,128]{2,1,0:T(2,128)(2,1)S(1)}, u32[]{:S(2)}, u32[]{:S(2)}) collective-permute-start(bf16[32,2,128]{2,1,0:T(2,128)(2,1)S(1)} %get-tuple-element.40), channel_id=1, source_target_pairs={{0,127},{1,0},{2,1},{3,2},{4,3},{5,4},{6,5},{7,6},{8,7},{9,8},{10,... | collective-permute-start | bytes 49160 | tf_op jit(solution)/shard_map/ppermute | solution.py:17
  81.0 1.1 pad_maximum_fusion
  82.9 1.9 collective-permute-start.6
  85.0 1.9 collective-permute-start.14
  86.9 8.1 %collective-permute-start.15 = (bf16[2,36,128]{2,1,0:T(8,128)(2,1)S(1)}, bf16[2,36,128]{2,1,0:T(8,128)(2,1)S(1)}, u32[]{:S(2)}, u32[]{:S(2)}) collective-permute-start(bf16[2,36,128]{2,1,0:T(8,128)(2,1)S(1)} %get-tuple-element.36), channel_id=1, source_target_pairs={{0,124},{1,125},{2,126},{3,127},{4,0},{5,1},{6,2},{7,3},{8,4},{9,5... | collective-permute-start | bytes 55304 | tf_op jit(solution)/shard_map/ppermute | solution.py:17
  95.0 4.8 %collective-permute-start.7 = (bf16[2,36,128]{2,1,0:T(8,128)(2,1)S(1)}, bf16[2,36,128]{2,1,0:T(8,128)(2,1)S(1)}, u32[]{:S(2)}, u32[]{:S(2)}) collective-permute-start(bf16[2,36,128]{2,1,0:T(8,128)(2,1)S(1)} %get-tuple-element.38), channel_id=1, source_target_pairs={{0,124},{1,125},{2,126},{3,127},{4,0},{5,1},{6,2},{7,3},{8,4},{9,5... | collective-permute-start | bytes 55304 | tf_op jit(solution)/shard_map/ppermute | solution.py:17
  99.9 1.7 collective-permute-done.7
  104.4 1.0 convolution_select_fusion.1
  105.4 0.4 copy.48
  105.9 1.1 convolution_select_fusion
  107.0 0.4 copy.58
  107.6 0.9 copy-done.2
  108.5 2.2 fusion.56
  110.7 0.6 convolution_bitcast_fusion.4
  111.4 1.1 pad_maximum_fusion.1
  112.5 1.3 dynamic-slice
  114.4 247.2 %all-reduce.4 = (f32[128]{0:T(128)S(1)}, f32[256]{0:T(256)S(1)}) all-reduce(f32[128]{0:T(128)S(1)} %get-tuple-element.16, f32[256]{0:T(256)S(1)} %get-tuple-element.14), channel_id=4, replica_groups=mesh['snap'=4,'space'=128] {'space'}, use_global_device_ids=true, to_apply=%region_5.6.clone | all-reduce | flops 384 | bytes 3072
  361.7 1.2 dynamic-slice.5
  363.0 0.8 constant_dynamic-slice_fusion.1
  363.8 1.5 constant_dynamic-slice_fusion
  365.3 15.1 %all-reduce.6 = (f32[3,3,2,128]{3,2,1,0:T(2,128)S(1)}, f32[3,3,1,256]{3,2,1,0:T(1,128)S(1)}, f32[1]{0:T(128)}, f32[2]{0:T(128)S(1)}) all-reduce(f32[3,3,2,128]{3,2,1,0:T(2,128)S(1)} %constant_dynamic-slice_fusion.1, f32[3,3,1,256]{3,2,1,0:T(1,128)S(1)} %constant_dynamic-slice_fusion, ...), channel_id=1, replica_groups=mesh['snap'=4,'space'=128] {'snap'}, use_global_device_ids=true, to_apply=%region_1.2 | all-reduce | flops 4611 | bytes 36888 | tf_op jit(solution)/shard_map/psum | solution.py:124
  380.5 0.6 broadcast_multiply_fusion.1
  381.1 0.5 broadcast_multiply_fusion.2
  381.6 0.6 broadcast_multiply_fusion
  (102 shorter events, 9.3 us)
Async XLA Ops:
  7.2 48.2 %copy-start = (bf16[3,3,256,128]{3,2,1,0:T(8,128)(2,1)S(1)}, bf16[3,3,256,128]{3,2,1,0:T(8,128)(2,1)}, u32[]{:S(2)}) copy-start(bf16[3,3,256,128]{3,2,1,0:T(8,128)(2,1)} %param.10) | copy-start | bytes 1769476
  7.2 26.7 %copy-start.1 = (bf16[1,1,32,32,256]{4,3,2,1,0:T(8,128)(2,1)S(1)}, bf16[1,1,32,32,256]{4,3,2,1,0:T(8,128)(2,1)}, u32[]{:S(2)}) copy-start(bf16[1,1,32,32,256]{4,3,2,1,0:T(8,128)(2,1)} %param.7) | copy-start | bytes 1572868
  7.2 355.8 %all-reduce.9.cloned.1.call-start = ((), (), s32[]{:S(2)}) async-start(), calls=%async_computation | async-start | bytes 4718592
  9.4 20.9 %collective-permute-start.8 = (bf16[32,2,256]{2,1,0:T(2,128)(2,1)S(1)}, bf16[32,2,256]{2,1,0:T(2,128)(2,1)S(1)}, u32[]{:S(2)}, u32[]{:S(2)}) collective-permute-start(bf16[32,2,256]{2,1,0:T(2,128)(2,1)S(1)} %get-tuple-element.29), channel_id=1, source_target_pairs={{0,1},{1,2},{2,3},{3,4},{4,5},{5,6},{6,7},{7,8},{8,9},{9,10},{10,1... | collective-permute-start | bytes 98312 | tf_op jit(solution)/shard_map/ppermute | solution.py:17
  12.3 21.4 %collective-permute-start = (bf16[32,2,256]{2,1,0:T(2,128)(2,1)S(1)}, bf16[32,2,256]{2,1,0:T(2,128)(2,1)S(1)}, u32[]{:S(2)}, u32[]{:S(2)}) collective-permute-start(bf16[32,2,256]{2,1,0:T(2,128)(2,1)S(1)} %get-tuple-element.31), channel_id=1, source_target_pairs={{0,1},{1,2},{2,3},{3,4},{4,5},{5,6},{6,7},{7,8},{8,9},{9,10},{10,1... | collective-permute-start | bytes 98312 | tf_op jit(solution)/shard_map/ppermute | solution.py:17
  15.9 17.9 %collective-permute-start.1 = (bf16[32,2,256]{2,1,0:T(2,128)(2,1)S(1)}, bf16[32,2,256]{2,1,0:T(2,128)(2,1)S(1)}, u32[]{:S(2)}, u32[]{:S(2)}) collective-permute-start(bf16[32,2,256]{2,1,0:T(2,128)(2,1)S(1)} %get-tuple-element.32), channel_id=1, source_target_pairs={{0,127},{1,0},{2,1},{3,2},{4,3},{5,4},{6,5},{7,6},{8,7},{9,8},{10,... | collective-permute-start | bytes 98312 | tf_op jit(solution)/shard_map/ppermute | solution.py:17
  27.6 4.2 %collective-permute-start.9 = (bf16[32,2,256]{2,1,0:T(2,128)(2,1)S(1)}, bf16[32,2,256]{2,1,0:T(2,128)(2,1)S(1)}, u32[]{:S(2)}, u32[]{:S(2)}) collective-permute-start(bf16[32,2,256]{2,1,0:T(2,128)(2,1)S(1)} %get-tuple-element.30), channel_id=1, source_target_pairs={{0,127},{1,0},{2,1},{3,2},{4,3},{5,4},{6,5},{7,6},{8,7},{9,8},{10,... | collective-permute-start | bytes 98312 | tf_op jit(solution)/shard_map/ppermute | solution.py:17
  31.8 17.0 %collective-permute-start.10 = (bf16[2,36,256]{2,1,0:T(8,128)(2,1)S(1)}, bf16[2,36,256]{2,1,0:T(8,128)(2,1)S(1)}, u32[]{:S(2)}, u32[]{:S(2)}) collective-permute-start(bf16[2,36,256]{2,1,0:T(8,128)(2,1)S(1)} %get-tuple-element.22), channel_id=1, source_target_pairs={{0,4},{1,5},{2,6},{3,7},{4,8},{5,9},{6,10},{7,11},{8,12},{9,13},{1... | collective-permute-start | bytes 110600 | tf_op jit(solution)/shard_map/ppermute | solution.py:17
  33.9 20.3 %collective-permute-start.2 = (bf16[2,36,256]{2,1,0:T(8,128)(2,1)S(1)}, bf16[2,36,256]{2,1,0:T(8,128)(2,1)S(1)}, u32[]{:S(2)}, u32[]{:S(2)}) collective-permute-start(bf16[2,36,256]{2,1,0:T(8,128)(2,1)S(1)} %get-tuple-element.24), channel_id=1, source_target_pairs={{0,4},{1,5},{2,6},{3,7},{4,8},{5,9},{6,10},{7,11},{8,12},{9,13},{1... | collective-permute-start | bytes 110600 | tf_op jit(solution)/shard_map/ppermute | solution.py:17
  35.8 18.6 %collective-permute-start.3 = (bf16[2,36,256]{2,1,0:T(8,128)(2,1)S(1)}, bf16[2,36,256]{2,1,0:T(8,128)(2,1)S(1)}, u32[]{:S(2)}, u32[]{:S(2)}) collective-permute-start(bf16[2,36,256]{2,1,0:T(8,128)(2,1)S(1)} %get-tuple-element.25), channel_id=1, source_target_pairs={{0,124},{1,125},{2,126},{3,127},{4,0},{5,1},{6,2},{7,3},{8,4},{9,5... | collective-permute-start | bytes 110600 | tf_op jit(solution)/shard_map/ppermute | solution.py:17
  44.0 6.8 %collective-permute-start.11 = (bf16[2,36,256]{2,1,0:T(8,128)(2,1)S(1)}, bf16[2,36,256]{2,1,0:T(8,128)(2,1)S(1)}, u32[]{:S(2)}, u32[]{:S(2)}) collective-permute-start(bf16[2,36,256]{2,1,0:T(8,128)(2,1)S(1)} %get-tuple-element.23), channel_id=1, source_target_pairs={{0,124},{1,125},{2,126},{3,127},{4,0},{5,1},{6,2},{7,3},{8,4},{9,5... | collective-permute-start | bytes 110600 | tf_op jit(solution)/shard_map/ppermute | solution.py:17
  51.4 1.1 copy-start.5
  51.4 1.1 copy-start.6
  55.1 0.7 copy-start.4
  62.6 20.0 %collective-permute-start.4 = (bf16[32,2,128]{2,1,0:T(2,128)(2,1)S(1)}, bf16[32,2,128]{2,1,0:T(2,128)(2,1)S(1)}, u32[]{:S(2)}, u32[]{:S(2)}) collective-permute-start(bf16[32,2,128]{2,1,0:T(2,128)(2,1)S(1)} %get-tuple-element.41), channel_id=1, source_target_pairs={{0,1},{1,2},{2,3},{3,4},{4,5},{5,6},{6,7},{7,8},{8,9},{9,10},{10,1... | collective-permute-start | bytes 49160 | tf_op jit(solution)/shard_map/ppermute | solution.py:17
  64.5 17.7 %collective-permute-start.5 = (bf16[32,2,128]{2,1,0:T(2,128)(2,1)S(1)}, bf16[32,2,128]{2,1,0:T(2,128)(2,1)S(1)}, u32[]{:S(2)}, u32[]{:S(2)}) collective-permute-start(bf16[32,2,128]{2,1,0:T(2,128)(2,1)S(1)} %get-tuple-element.42), channel_id=1, source_target_pairs={{0,127},{1,0},{2,1},{3,2},{4,3},{5,4},{6,5},{7,6},{8,7},{9,8},{10,... | collective-permute-start | bytes 49160 | tf_op jit(solution)/shard_map/ppermute | solution.py:17
  71.5 13.4 %collective-permute-start.12 = (bf16[32,2,128]{2,1,0:T(2,128)(2,1)S(1)}, bf16[32,2,128]{2,1,0:T(2,128)(2,1)S(1)}, u32[]{:S(2)}, u32[]{:S(2)}) collective-permute-start(bf16[32,2,128]{2,1,0:T(2,128)(2,1)S(1)} %get-tuple-element.39), channel_id=1, source_target_pairs={{0,1},{1,2},{2,3},{3,4},{4,5},{5,6},{6,7},{7,8},{8,9},{9,10},{10,1... | collective-permute-start | bytes 49160 | tf_op jit(solution)/shard_map/ppermute | solution.py:17
  73.4 11.5 %collective-permute-start.13 = (bf16[32,2,128]{2,1,0:T(2,128)(2,1)S(1)}, bf16[32,2,128]{2,1,0:T(2,128)(2,1)S(1)}, u32[]{:S(2)}, u32[]{:S(2)}) collective-permute-start(bf16[32,2,128]{2,1,0:T(2,128)(2,1)S(1)} %get-tuple-element.40), channel_id=1, source_target_pairs={{0,127},{1,0},{2,1},{3,2},{4,3},{5,4},{6,5},{7,6},{8,7},{9,8},{10,... | collective-permute-start | bytes 49160 | tf_op jit(solution)/shard_map/ppermute | solution.py:17
  82.9 16.9 %collective-permute-start.6 = (bf16[2,36,128]{2,1,0:T(8,128)(2,1)S(1)}, bf16[2,36,128]{2,1,0:T(8,128)(2,1)S(1)}, u32[]{:S(2)}, u32[]{:S(2)}) collective-permute-start(bf16[2,36,128]{2,1,0:T(8,128)(2,1)S(1)} %get-tuple-element.37), channel_id=1, source_target_pairs={{0,4},{1,5},{2,6},{3,7},{4,8},{5,9},{6,10},{7,11},{8,12},{9,13},{1... | collective-permute-start | bytes 55304 | tf_op jit(solution)/shard_map/ppermute | solution.py:17
  85.0 18.5 %collective-permute-start.14 = (bf16[2,36,128]{2,1,0:T(8,128)(2,1)S(1)}, bf16[2,36,128]{2,1,0:T(8,128)(2,1)S(1)}, u32[]{:S(2)}, u32[]{:S(2)}) collective-permute-start(bf16[2,36,128]{2,1,0:T(8,128)(2,1)S(1)} %get-tuple-element.35), channel_id=1, source_target_pairs={{0,4},{1,5},{2,6},{3,7},{4,8},{5,9},{6,10},{7,11},{8,12},{9,13},{1... | collective-permute-start | bytes 55304 | tf_op jit(solution)/shard_map/ppermute | solution.py:17
  86.9 16.8 %collective-permute-start.15 = (bf16[2,36,128]{2,1,0:T(8,128)(2,1)S(1)}, bf16[2,36,128]{2,1,0:T(8,128)(2,1)S(1)}, u32[]{:S(2)}, u32[]{:S(2)}) collective-permute-start(bf16[2,36,128]{2,1,0:T(8,128)(2,1)S(1)} %get-tuple-element.36), channel_id=1, source_target_pairs={{0,124},{1,125},{2,126},{3,127},{4,0},{5,1},{6,2},{7,3},{8,4},{9,5... | collective-permute-start | bytes 55304 | tf_op jit(solution)/shard_map/ppermute | solution.py:17
  95.0 6.6 %collective-permute-start.7 = (bf16[2,36,128]{2,1,0:T(8,128)(2,1)S(1)}, bf16[2,36,128]{2,1,0:T(8,128)(2,1)S(1)}, u32[]{:S(2)}, u32[]{:S(2)}) collective-permute-start(bf16[2,36,128]{2,1,0:T(8,128)(2,1)S(1)} %get-tuple-element.38), channel_id=1, source_target_pairs={{0,124},{1,125},{2,126},{3,127},{4,0},{5,1},{6,2},{7,3},{8,4},{9,5... | collective-permute-start | bytes 55304 | tf_op jit(solution)/shard_map/ppermute | solution.py:17
  107.4 1.0 copy-start.2
  107.4 1.0 copy-start.3
Sparse Core Ops, SparseCore 0:
  112.6 196.5 all-reduce.8
where the time goes:
time: 393 us; the launch traced here: 391 us
  blocking collectives  262 us (67%)
  starting transfers between devices  71.3 us (18%)
  between operations  17.4 us (4%)
  other arithmetic  12 us (3%)
  matrix products  11.4 us (3%)
  local copies, waits for them, and re-layouts  11.2 us (3%)
  waiting for transfers between devices  5.13 us (1%)
    unnamed x1, blocking collectives  247 us
    ppermute x16, starting transfers between devices, from_behind(): lax.ppermute(array, axis, [(i, (i + by) % length) for i in range(length)])  71.3 us
    psum x1, blocking collectives, local(): summed = lax.psum((shares[0], shares[1], shares[2], shares[3]), 'snap')  15.1 us
  transfers between devices with their start and end apart: 17, of which 3 were waited for; matrix products, arithmetic and copies ran while one was open for 3% of the time, Pallas kernels for 0%

commit v1 on v0

v1 whole, which is shorter than its diff:
```python
import math

import jax
import jax.numpy as jnp
import numpy as np
from jax import lax
from jax.sharding import Mesh
from jax.sharding import PartitionSpec as P

DEV_COLS = 4
HALO = 4
SPACE = ("z", "y", "core")


ROOT_HALF = 0.7071067811865476
INV_ROOT_TWO_PI = 0.3989422804014327


def from_behind(array, axis, by):
    length = lax.axis_size(axis)
    return lax.ppermute(array, axis, [(i, (i + by) % length) for i in range(length)])


def gelu_value(pre):
    return 0.5 * pre * (1.0 + lax.erf(pre * ROOT_HALF))


def gelu_slope(pre):
    return (
        0.5 * (1.0 + lax.erf(pre * ROOT_HALF)) + pre * jnp.exp(-0.5 * pre * pre) * INV_ROOT_TWO_PI
    )


def dilated(padded, kernel):
    return lax.conv_general_dilated(
        padded[None],
        kernel,
        (1, 1),
        "VALID",
        rhs_dilation=(2, 2),
        dimension_numbers=("NHWC", "HWIO", "NHWC"),
        preferred_element_type=jnp.float32,
    )[0]


def flipped(kernel):
    return jnp.swapaxes(kernel[::-1, ::-1], 2, 3)


def tap_sums(padded, grad_out):
    span_y = grad_out.shape[0]
    span_x = grad_out.shape[1]
    flat_out = grad_out.reshape(span_y * span_x, grad_out.shape[2])
    tap_rows = []
    for tap_y in range(3):
        tap_line = []
        for tap_x in range(3):
            window = padded[2 * tap_y : 2 * tap_y + span_y, 2 * tap_x : 2 * tap_x + span_x].reshape(
                span_y * span_x, padded.shape[2]
            )
            tap_line.append(
                lax.dot_general(
                    window, flat_out, (((0,), (0,)), ((), ())), preferred_element_type=jnp.float32
                )
            )
        tap_rows.append(jnp.stack(tap_line))
    return jnp.stack(tap_rows)


def grid_halo(region, width):
    count = lax.axis_size(SPACE)
    position = (lax.axis_index(SPACE) + 1) % count
    column = position % DEV_COLS
    line = position // DEV_COLS
    last_line = count // DEV_COLS - 1
    strips = []
    for offset in (1, -1):
        edge_cells = region[:, -width:] if offset == 1 else region[:, :width]
        arrived = from_behind(edge_cells, SPACE, offset)
        inside = column != 0 if offset == 1 else column != DEV_COLS - 1
        strips.append(jnp.where(inside, arrived, jnp.zeros_like(arrived)))
    widened = jnp.concatenate([strips[0], region, strips[1]], axis=1)
    row_bands = []
    for offset in (DEV_COLS, -DEV_COLS):
        edge_cells = widened[-width:] if offset > 0 else widened[:width]
        arrived = from_behind(edge_cells, SPACE, offset)
        inside = line != 0 if offset > 0 else line != last_line
        row_bands.append(jnp.where(inside, arrived, jnp.zeros_like(arrived)))
    return jnp.concatenate([row_bands[0], widened, row_bands[1]], axis=0)


def swap(value, axis, bit):
    size = lax.axis_size(axis)
    return lax.ppermute(value, axis, [(i, i ^ bit) for i in range(size)])


def halve(block, axis, bit):
    half = block.shape[0] // 2
    upper = (lax.axis_index(axis) // bit) % 2
    keep = lax.dynamic_slice_in_dim(block, upper * half, half, axis=0)
    send = lax.dynamic_slice_in_dim(block, (1 - upper) * half, half, axis=0)
    return keep + swap(send, axis, bit)


def reduce_shards(rows, sizes):
    names = ("z", "y", "core")
    counts = [len(_bits(size)) for size in sizes]
    steps = [("core", b) for b in _bits(sizes[2])]
    steps += [("y", b) for b in _bits(sizes[1])]
    steps += [("z", b) for b in _bits(sizes[0])]
    starts = dict(zip(names, np.cumsum([0] + counts[:-1]).tolist()))
    total = dict(zip(names, counts))
    order = [starts[axis] + total[axis] - 1 - int(math.log2(bit)) for axis, bit in steps]
    width = rows.shape[1]
    block = rows.reshape((2,) * len(order) + (width,))
    block = jnp.transpose(block, order + [len(order)]).reshape(rows.shape)
    for axis, bit in steps:
        block = halve(block, axis, bit)
    snap_size = lax.axis_size("snap")
    bit = 1
    while bit < snap_size:
        block = block + swap(block, "snap", bit)
        bit *= 2
    return block


def _bits(size):
    out = []
    bit = 1
    while bit < size:
        out.append(bit)
        bit *= 2
    return out


def local(sizes, field_in, ocean_mask, cotangent, w_first, b_first, w_second, b_second):
    region = field_in[0, 0]
    upstream = cotangent[0, 0]
    channels = region.shape[-1]
    hidden_channels = w_first.shape[-1]
    ocean = ocean_mask[0].astype(jnp.float32)[:, :, None]
    space_count = lax.axis_size(SPACE)
    total = (
        field_in.shape[0]
        * lax.axis_size("snap")
        * space_count
        * region.shape[0]
        * region.shape[1]
    )
    scale = 1.0 / math.sqrt(float(total))
    g_mixed = (ocean * upstream.astype(jnp.float32)).astype(jnp.bfloat16)
    mask_lanes = jnp.broadcast_to(ocean.astype(jnp.bfloat16), region.shape[:2] + (128,))
    packed = jnp.concatenate([region, g_mixed, mask_lanes], axis=-1)
    wide = grid_halo(packed, HALO)
    source_wide = wide[..., :channels]
    mixed_wide = wide[..., channels : 2 * channels]
    ocean_wide = wide[2:-2, 2:-2, 2 * channels : 2 * channels + 1].astype(jnp.float32)
    source_pad = source_wide[2:-2, 2:-2]
    pre = dilated(source_wide, w_first) + b_first
    hidden = (ocean_wide * gelu_value(pre)).astype(jnp.bfloat16)
    mixed = dilated(hidden, w_second) + b_second
    field_out = (region.astype(jnp.float32) + ocean * mixed).astype(jnp.bfloat16)
    grad_wb = tap_sums(hidden, g_mixed)
    grad_bb = jnp.sum(g_mixed.astype(jnp.float32), axis=(0, 1))
    g_hidden = dilated(mixed_wide, flipped(w_second))
    g_pre = (ocean_wide * g_hidden * gelu_slope(pre)).astype(jnp.bfloat16)
    g_input = (upstream.astype(jnp.float32) + dilated(g_pre, flipped(w_first))).astype(
        jnp.bfloat16
    )
    g_pre_inner = g_pre[2:-2, 2:-2]
    grad_wa = tap_sums(source_pad, g_pre_inner)
    grad_ba = jnp.sum(g_pre_inner.astype(jnp.float32), axis=(0, 1))
    per_a = channels // space_count
    per_b = hidden_channels // space_count
    rows = jnp.concatenate(
        [
            jnp.moveaxis(grad_wa.reshape(3, 3, space_count, per_a, hidden_channels), 2, 0).reshape(
                space_count, -1
            ),
            jnp.moveaxis(grad_wb.reshape(3, 3, space_count, per_b, channels), 2, 0).reshape(
                space_count, -1
            ),
            grad_ba.reshape(space_count, per_b),
            grad_bb.reshape(space_count, per_a),
        ],
        axis=1,
    )
    width = rows.shape[1]
    padded_width = -(-width // 128) * 128
    rows = jnp.pad(rows, ((0, 0), (0, padded_width - width)))
    mine = reduce_shards(rows, sizes)[0] * scale
    cut_a = 9 * per_a * hidden_channels
    cut_b = cut_a + 9 * per_b * channels
    return (
        field_out[None, None],
        g_input[None, None],
        mine[:cut_a].reshape(3, 3, per_a, hidden_channels),
        mine[cut_a:cut_b].reshape(3, 3, per_b, channels),
        mine[cut_b : cut_b + per_b],
        mine[cut_b + per_b : cut_b + per_b + per_a],
    )


def solution(mesh):
    snap = mesh.shape["snap"]
    space = mesh.shape["space"]
    core_size = 2
    y_size = 8 if space % 16 == 0 else space // core_size
    z_size = space // (core_size * y_size)
    sizes = (z_size, y_size, core_size)
    grid = Mesh(mesh.devices.reshape(snap, z_size, y_size, core_size), ("snap",) + SPACE)
    placed = (
        P("snap", SPACE, None, None, None),
        P(SPACE, None, None),
        P("snap", SPACE, None, None, None),
        P(),
        P(),
        P(),
        P(),
    )

    def run(*args):
        return local(sizes, *args)

    return jax.shard_map(
        run,
        mesh=grid,
        in_specs=placed,
        out_specs=(
            P("snap", SPACE, None, None, None),
            P("snap", SPACE, None, None, None),
            P(None, None, SPACE, None),
            P(None, None, SPACE, None),
            P(SPACE),
            P(SPACE),
        ),
        check_vma=False,
    )
```

time: 393 us -> 191 us (0.49)
  blocking collectives: 262 us -> 0 us
  waiting for transfers between devices: 5.13 us -> 75.8 us
  starting transfers between devices: 71.3 us -> 44.2 us
  local copies, waits for them, and re-layouts: 11.2 us -> 33 us
  between operations: 17.4 us -> 1.68 us
  matrix products: 11.4 us -> 18.7 us
    unnamed x1 -> x0, blocking collectives: 247 us -> none
    ppermute x0 -> x9, waiting for transfers between devices: none -> 58.4 us  [swap(): return lax.ppermute(value, axis, [(i, i ^ bit) for i in range(size)])]
    ppermute x16 -> x4, starting transfers between devices: 71.3 us -> 21.9 us  [from_behind(): lax.ppermute(array, axis, [(i, (i + by) % length) for i in range(length)])]
    ppermute x0 -> x9, starting transfers between devices: none -> 22.3 us  [swap(): return lax.ppermute(value, axis, [(i, i ^ bit) for i in range(size)])]
    psum x1 -> x0, blocking collectives: 15.1 us -> none  [local(): summed = lax.psum((shares[0], shares[1], shares[2], shares[3]), 'snap')]
    ppermute x16 -> x4, waiting for transfers between devices: 5.12 us -> 17.4 us  [from_behind(): lax.ppermute(array, axis, [(i, (i + by) % length) for i in range(length)])]
    reshape x0 -> x4, local copies, waits for them, and re-layouts: none -> 6.99 us  [the longest x1 3.17 us: reduce_shards(): block = jnp.transpose(block, order + [len(order)]).reshape(rows.shape)]
    concatenate x0 -> x1, local copies, waits for them, and re-layouts: none -> 6.75 us  [local(): jnp.concatenate([jnp.moveaxis(grad_wa.reshape(3, 3, space_count, per_a, h...]
  transfers between devices with their start and end apart: 17 -> 13, of which waited for: 3 -> 13; matrix products, arithmetic and copies ran while one was open for 3% -> 4% of each run, Pallas kernels for 0% -> 0%
where the time goes in v1:
time: 191 us; the launch traced here: 189 us
  waiting for transfers between devices  75.8 us (40%)
  starting transfers between devices  44.2 us (23%)
  local copies, waits for them, and re-layouts  33 us (17%)
  matrix products  18.7 us (10%)
  other arithmetic  15.6 us (8%)
    ppermute x9, waiting for transfers between devices, swap(): return lax.ppermute(value, axis, [(i, i ^ bit) for i in range(size)])  58.4 us
    ppermute x9, starting transfers between devices, swap(): return lax.ppermute(value, axis, [(i, i ^ bit) for i in range(size)])  22.3 us
    ppermute x4, starting transfers between devices, from_behind(): lax.ppermute(array, axis, [(i, (i + by) % length) for i in range(length)])  21.9 us
    ppermute x4, waiting for transfers between devices, from_behind(): lax.ppermute(array, axis, [(i, (i + by) % length) for i in range(length)])  17.4 us
    dot_general x18, matrix products, tap_sums(): lax.dot_general(window, flat_out, (((0,), (0,)), ((), ())), preferred_ele...  11.6 us
    conv_general_dilated x4, matrix products, dilated(): lax.conv_general_dilated(padded[None], kernel, (1, 1), 'VALID', rhs_dilat...  7.09 us
    concatenate x1, local copies, waits for them, and re-layouts, local(): jnp.concatenate([jnp.moveaxis(grad_wa.reshape(3, 3, space_count, per_a, h...  6.75 us
    unnamed x40, local copies, waits for them, and re-layouts  5.85 us
  transfers between devices with their start and end apart: 13, of which 13 were waited for; matrix products, arithmetic and copies ran while one was open for 4% of the time, Pallas kernels for 0%

profile of v1, /device:TPU:6, one launch (start us, length us, event | category | flops | bytes accessed | tf_op | source)
XLA Modules:
  0.0 189.0 jit_solution(12896170516978141191)
XLA Ops:
  1.5 1.3 convert_reduce_fusion
  3.1 13.3 %collective-permute-start.1 = (bf16[32,4,640]{2,1,0:T(4,128)(2,1)S(1)}, bf16[32,4,640]{2,1,0:T(4,128)(2,1)S(1)}, u32[]{:S(2)}, u32[]{:S(2)}) collective-permute-start(bf16[32,4,640]{2,1,0:T(4,128)(2,1)S(1)} %get-tuple-element.36), channel_id=1, source_target_pairs={{0,127},{1,0},{2,1},{3,2},{4,3},{5,4},{6,5},{7,6},{8,7},{9,8},{10,... | collective-permute-start | bytes 491528 | tf_op jit(solution)/shard_map/ppermute | solution.py:21
  16.4 1.9 %collective-permute-start = (bf16[32,4,640]{2,1,0:T(4,128)(2,1)S(1)}, bf16[32,4,640]{2,1,0:T(4,128)(2,1)S(1)}, u32[]{:S(2)}, u32[]{:S(2)}) collective-permute-start(bf16[32,4,640]{2,1,0:T(4,128)(2,1)S(1)} %get-tuple-element.35), channel_id=1, source_target_pairs={{0,1},{1,2},{2,3},{3,4},{4,5},{5,6},{6,7},{7,8},{8,9},{9,10},{10,1... | collective-permute-start | bytes 491528 | tf_op jit(solution)/shard_map/ppermute | solution.py:21
  19.3 7.1 %collective-permute-done = bf16[32,4,640]{2,1,0:T(4,128)(2,1)S(1)} collective-permute-done((bf16[32,4,640]{2,1,0:T(4,128)(2,1)S(1)}, bf16[32,4,640]{2,1,0:T(4,128)(2,1)S(1)}, u32[]{:S(2)}, u32[]{:S(2)}) %collective-permute-start) | collective-permute-done | bytes 163872 | tf_op jit(solution)/shard_map/ppermute | solution.py:21
  26.6 1.9 %collective-permute-start.3 = (bf16[4,40,640]{2,1,0:T(8,128)(2,1)S(1)}, bf16[4,40,640]{2,1,0:T(8,128)(2,1)S(1)}, u32[]{:S(2)}, u32[]{:S(2)}) collective-permute-start(bf16[4,40,640]{2,1,0:T(8,128)(2,1)S(1)} %get-tuple-element.34), channel_id=1, source_target_pairs={{0,124},{1,125},{2,126},{3,127},{4,0},{5,1},{6,2},{7,3},{8,4},{9,5... | collective-permute-start | bytes 614408 | tf_op jit(solution)/shard_map/ppermute | solution.py:21
  29.3 4.8 %collective-permute-start.2 = (bf16[4,40,640]{2,1,0:T(8,128)(2,1)S(1)}, bf16[4,40,640]{2,1,0:T(8,128)(2,1)S(1)}, u32[]{:S(2)}, u32[]{:S(2)}) collective-permute-start(bf16[4,40,640]{2,1,0:T(8,128)(2,1)S(1)} %get-tuple-element.33), channel_id=1, source_target_pairs={{0,4},{1,5},{2,6},{3,7},{4,8},{5,9},{6,10},{7,11},{8,12},{9,13},{1... | collective-permute-start | bytes 614408 | tf_op jit(solution)/shard_map/ppermute | solution.py:21
  34.1 1.1 collective-permute-done.3
  35.3 8.4 %collective-permute-done.2 = bf16[4,40,640]{2,1,0:T(8,128)(2,1)S(1)} collective-permute-done((bf16[4,40,640]{2,1,0:T(8,128)(2,1)S(1)}, bf16[4,40,640]{2,1,0:T(8,128)(2,1)S(1)}, u32[]{:S(2)}, u32[]{:S(2)}) %collective-permute-start.2) | collective-permute-done | bytes 204832 | tf_op jit(solution)/shard_map/ppermute | solution.py:21
  43.7 3.3 %pad_maximum_fusion = (bf16[40,40,256]{2,1,0:T(8,128)(2,1)S(1)}, bf16[40,40,256]{2,1,0:T(8,128)(2,1)S(1)}) fusion(bf16[4,40,640]{2,1,0:T(8,128)(2,1)S(1)} %broadcast_select_fusion, bf16[4,40,640]{2,1,0:T(8,128)(2,1)S(1)} %broadcast_select_fusion.1, bf16[32,4,640]{2,1,0:T(4,128)(2,1)S(1)} %broadcast_select_fusion.2, ...), kind=kLoop, calls=%fused_computation.49 | loop fusion | flops 11468800 | bytes 3686400 | tf_op jit(solution)/shard_map/concatenate | solution.py:89
  49.0 1.9 %fusion.18 = f32[36,8,5,128]{3,1,2,0:T(8,128)S(1)} fusion(bf16[3,3,128,256]{3,2,1,0:T(8,128)(2,1)S(1)} %copy-done.14, bf16[40,1,7,4,256]{4,2,3,0,1:T(8,128)(2,1)S(1)} %slice.164, bf16[40,1,8,5,256]{4,2,3,0,1:T(8,128)(2,1)S(1)} %copy.89, pred[8,5]{0,1:T(8,128)(4,1)S(1)} %copy-done.17), kind=kOutput, calls=%fused_computation.23 | convolution fusion | flops 853954560 | bytes 2719784 | tf_op jit(solution)/shard_map/conv_general_dilated | solution.py:35
  51.6 3.1 %fusion.34 = (f32[36,8,5,128]{3,1,2,0:T(8,128)}, f32[36,8,5,128]{3,1,2,0:T(8,128)}, f32[36,8,5,128]{3,1,2,0:T(8,128)S(1)}) fusion(f32[128]{0:T(128)S(1)} %copy-done.13, bf16[3,3,256,128]{3,2,1,0:T(8,128)(2,1)S(1)} %copy-done, bf16[40,1,7,4,256]{4,2,3,0,1:T(8,128)(2,1)S(1)} %slice.160, bf16[40,1,8,5,256]{4,2,3,0,1:T(8,128)(2,1)S(1)} %copy.82, ...), kind=kOutput, calls=%fused_computation.59 | convolution fusion | flops 855982080 | bytes 4194856 | tf_op jit(solution)/shard_map/conv_general_dilated | solution.py:35
  63.4 0.9 convolution_bitcast_fusion.7
  66.2 0.9 convolution_bitcast_fusion.4
  69.5 1.1 maximum_bitcast_fusion.4
  70.5 1.3 maximum_bitcast_fusion.2
  72.0 1.4 copy.103
  73.4 6.8 %concatenate.39 = f32[128,4611]{0,1:T(8,128)} concatenate(f32[128,2304]{0,1:T(8,128)S(1)} %bitcast.192, f32[128,2304]{0,1:T(8,128)} %bitcast.193, f32[128,1]{0,1:T(1,128)S(1)} %bitcast.216, f32[128,2]{0,1:T(2,128)S(1)} %copy-done.10), dimensions={1} | concatenate | bytes 4721664 | tf_op jit(solution)/shard_map/concatenate | solution.py:175
  80.1 2.3 %copy.114 = f32[128,4611]{1,0:T(8,128)S(1)} copy(f32[128,4611]{0,1:T(8,128)} %concatenate.39) | data formatting | bytes 4721664
  82.5 1.6 pad.4.clone
  84.0 3.0 %reshape.126 = f32[2,2,2,2,2,2,2,4736]{7,6,5,4,3,2,1,0:T(2,128)S(1)} reshape(f32[128,4736]{1,0:T(8,128)} %pad.4.clone) | data formatting | bytes 4849664 | tf_op jit(solution)/shard_map/reshape | solution.py:115
  87.1 3.3 %copy.106 = f32[2,2,2,2,2,2,2,4736]{7,6,5,4,3,2,1,0:T(2,128)} copy(f32[2,2,2,2,2,2,2,4736]{7,0,1,2,3,4,5,6:T(2,128)S(1)} %bitcast.191) | data formatting | bytes 4849664 | tf_op jit(solution)/shard_map/transpose | solution.py:116
  90.4 3.2 %reshape.127 = f32[128,4736]{1,0:T(8,128)S(1)} reshape(f32[2,2,2,2,2,2,2,4736]{7,6,5,4,3,2,1,0:T(2,128)} %copy.106) | data formatting | bytes 4849664 | tf_op jit(solution)/shard_map/reshape | solution.py:116
  93.6 1.1 constant_dynamic-slice_fusion.6
  94.7 1.9 %collective-permute-start.4 = (f32[64,4736]{1,0:T(8,128)}, f32[64,4736]{1,0:T(8,128)}, u32[]{:S(2)}, u32[]{:S(2)}) collective-permute-start(f32[64,4736]{1,0:T(8,128)} %constant_dynamic-slice_fusion.6), channel_id=1, source_target_pairs={{0,1},{1,0},{2,3},{3,2},{4,5},{5,4},{6,7},{7,6},{8,9},{9,8},{10,11... | collective-permute-start | bytes 3637256 | tf_op jit(solution)/shard_map/ppermute | solution.py:94
  96.7 3.2 %collective-permute-done.4 = f32[64,4736]{1,0:T(8,128)} collective-permute-done((f32[64,4736]{1,0:T(8,128)}, f32[64,4736]{1,0:T(8,128)}, u32[]{:S(2)}, u32[]{:S(2)}) %collective-permute-start.4) | collective-permute-done | bytes 1212448 | tf_op jit(solution)/shard_map/ppermute | solution.py:94
  99.8 1.4 dynamic-slice_add_fusion
  101.3 1.0 copy-done.4
  102.4 4.7 %collective-permute-start.5 = (f32[32,4736]{1,0:T(8,128)S(1)}, f32[32,4736]{1,0:T(8,128)S(1)}, u32[]{:S(2)}, u32[]{:S(2)}) collective-permute-start(f32[32,4736]{1,0:T(8,128)S(1)} %constant_dynamic-slice_fusion.5), channel_id=1, source_target_pairs={{0,2},{2,0},{4,6},{6,4},{8,10},{10,8},{12,14},{14,12},{1,3},{3,1},... | collective-permute-start | bytes 1818632 | tf_op jit(solution)/shard_map/ppermute | solution.py:94
  107.1 13.9 %collective-permute-done.5 = f32[32,4736]{1,0:T(8,128)S(1)} collective-permute-done((f32[32,4736]{1,0:T(8,128)S(1)}, f32[32,4736]{1,0:T(8,128)S(1)}, u32[]{:S(2)}, u32[]{:S(2)}) %collective-permute-start.5) | collective-permute-done | bytes 606240 | tf_op jit(solution)/shard_map/ppermute | solution.py:94
  121.0 1.1 dynamic-slice_add_fusion.1
  122.2 1.9 %collective-permute-start.6 = (f32[16,4736]{1,0:T(8,128)S(1)}, f32[16,4736]{1,0:T(8,128)S(1)}, u32[]{:S(2)}, u32[]{:S(2)}) collective-permute-start(f32[16,4736]{1,0:T(8,128)S(1)} %constant_dynamic-slice_fusion.4), channel_id=1, source_target_pairs={{0,4},{2,6},{4,0},{6,2},{8,12},{10,14},{12,8},{14,10},{1,5},{3,7},... | collective-permute-start | bytes 909320 | tf_op jit(solution)/shard_map/ppermute | solution.py:94
  124.5 15.7 %collective-permute-done.6 = f32[16,4736]{1,0:T(8,128)S(1)} collective-permute-done((f32[16,4736]{1,0:T(8,128)S(1)}, f32[16,4736]{1,0:T(8,128)S(1)}, u32[]{:S(2)}, u32[]{:S(2)}) %collective-permute-start.6) | collective-permute-done | bytes 303136 | tf_op jit(solution)/shard_map/ppermute | solution.py:94
  140.3 1.9 %collective-permute-start.7 = (f32[8,4736]{1,0:T(8,128)S(1)}, f32[8,4736]{1,0:T(8,128)S(1)}, u32[]{:S(2)}, u32[]{:S(2)}) collective-permute-start(f32[8,4736]{1,0:T(8,128)S(1)} %constant_dynamic-slice_fusion.3), channel_id=1, source_target_pairs={{0,8},{2,10},{4,12},{6,14},{8,0},{10,2},{12,4},{14,6},{1,9},{3,11}... | collective-permute-start | bytes 454664 | tf_op jit(solution)/shard_map/ppermute | solution.py:94
  142.7 8.9 %collective-permute-done.7 = f32[8,4736]{1,0:T(8,128)S(1)} collective-permute-done((f32[8,4736]{1,0:T(8,128)S(1)}, f32[8,4736]{1,0:T(8,128)S(1)}, u32[]{:S(2)}, u32[]{:S(2)}) %collective-permute-start.7) | collective-permute-done | bytes 151584 | tf_op jit(solution)/shard_map/ppermute | solution.py:94
  151.6 1.9 %collective-permute-start.8 = (f32[4,4736]{1,0:T(4,128)S(1)}, f32[4,4736]{1,0:T(4,128)S(1)}, u32[]{:S(2)}, u32[]{:S(2)}) collective-permute-start(f32[4,4736]{1,0:T(4,128)S(1)} %constant_dynamic-slice_fusion.2), channel_id=1, source_target_pairs={{0,16},{16,0},{32,48},{48,32},{64,80},{80,64},{96,112},{112,96},{1... | collective-permute-start | bytes 227336 | tf_op jit(solution)/shard_map/ppermute | solution.py:94
  153.6 1.0 convolution_select_fusion.1
  155.1 2.8 %collective-permute-done.8 = f32[4,4736]{1,0:T(4,128)S(1)} collective-permute-done((f32[4,4736]{1,0:T(4,128)S(1)}, f32[4,4736]{1,0:T(4,128)S(1)}, u32[]{:S(2)}, u32[]{:S(2)}) %collective-permute-start.8) | collective-permute-done | bytes 75808 | tf_op jit(solution)/shard_map/ppermute | solution.py:94
  158.0 1.9 %collective-permute-start.9 = (f32[2,4736]{1,0:T(2,128)S(1)}, f32[2,4736]{1,0:T(2,128)S(1)}, u32[]{:S(2)}, u32[]{:S(2)}) collective-permute-start(f32[2,4736]{1,0:T(2,128)S(1)} %constant_dynamic-slice_fusion.1), channel_id=1, source_target_pairs={{0,32},{16,48},{32,0},{48,16},{64,96},{80,112},{96,64},{112,80},{1... | collective-permute-start | bytes 113672 | tf_op jit(solution)/shard_map/ppermute | solution.py:94
  160.5 4.2 %collective-permute-done.9 = f32[2,4736]{1,0:T(2,128)S(1)} collective-permute-done((f32[2,4736]{1,0:T(2,128)S(1)}, f32[2,4736]{1,0:T(2,128)S(1)}, u32[]{:S(2)}, u32[]{:S(2)}) %collective-permute-start.9) | collective-permute-done | bytes 37920 | tf_op jit(solution)/shard_map/ppermute | solution.py:94
  164.8 1.9 %collective-permute-start.10 = (f32[1,4736]{1,0:T(1,128)S(1)}, f32[1,4736]{1,0:T(1,128)S(1)}, u32[]{:S(2)}, u32[]{:S(2)}) collective-permute-start(f32[1,4736]{1,0:T(1,128)S(1)} %constant_dynamic-slice_fusion), channel_id=1, source_target_pairs={{0,64},{16,80},{32,96},{48,112},{64,0},{80,16},{96,32},{112,48},{1... | collective-permute-start | bytes 56840 | tf_op jit(solution)/shard_map/ppermute | solution.py:94
  167.3 7.1 %collective-permute-done.10 = f32[1,4736]{1,0:T(1,128)S(1)} collective-permute-done((f32[1,4736]{1,0:T(1,128)S(1)}, f32[1,4736]{1,0:T(1,128)S(1)}, u32[]{:S(2)}, u32[]{:S(2)}) %collective-permute-start.10) | collective-permute-done | bytes 18976 | tf_op jit(solution)/shard_map/ppermute | solution.py:94
  174.4 2.7 %collective-permute-start.11 = (f32[1,4736]{1,0:T(1,128)S(1)}, f32[1,4736]{1,0:T(1,128)S(1)}, u32[]{:S(2)}, u32[]{:S(2)}) collective-permute-start(f32[1,4736]{1,0:T(1,128)S(1)} %dynamic-slice_add_fusion.6), channel_id=1, source_target_pairs={{0,128},{128,0},{256,384},{384,256},{1,129},{129,1},{257,385},{385... | collective-permute-start | bytes 56840 | tf_op jit(solution)/shard_map/ppermute | solution.py:94
  177.1 1.1 convolution_select_fusion
  178.7 1.3 collective-permute-done.11
  180.1 3.3 %collective-permute-start.12 = (f32[1,4736]{1,0:T(1,128)S(1)}, f32[1,4736]{1,0:T(1,128)S(1)}, u32[]{:S(2)}, u32[]{:S(2)}) collective-permute-start(f32[1,4736]{1,0:T(1,128)S(1)} %add.213), channel_id=1, source_target_pairs={{0,256},{128,384},{256,0},{384,128},{1,257},{129,385},{257,1},{385... | collective-permute-start | bytes 56840 | tf_op jit(solution)/shard_map/ppermute | solution.py:94
  183.4 1.4 fusion.26
  184.8 1.1 copy.107
  185.9 1.4 collective-permute-done.12
  (116 shorter events, 23.5 us)
Async XLA Ops:
  0.6 50.5 %copy-start = (bf16[3,3,256,128]{3,2,1,0:T(8,128)(2,1)S(1)}, bf16[3,3,256,128]{3,2,1,0:T(8,128)(2,1)}, u32[]{:S(2)}) copy-start(bf16[3,3,256,128]{3,2,1,0:T(8,128)(2,1)} %param.10) | copy-start | bytes 1769476
  0.6 2.3 %copy-start.1 = (bf16[1,1,32,32,256]{4,3,2,1,0:T(8,128)(2,1)S(1)}, bf16[1,1,32,32,256]{4,3,2,1,0:T(8,128)(2,1)}, u32[]{:S(2)}) copy-start(bf16[1,1,32,32,256]{4,3,2,1,0:T(8,128)(2,1)} %param.7) | copy-start | bytes 1572868
  3.1 16.1 %collective-permute-start.1 = (bf16[32,4,640]{2,1,0:T(4,128)(2,1)S(1)}, bf16[32,4,640]{2,1,0:T(4,128)(2,1)S(1)}, u32[]{:S(2)}, u32[]{:S(2)}) collective-permute-start(bf16[32,4,640]{2,1,0:T(4,128)(2,1)S(1)} %get-tuple-element.36), channel_id=1, source_target_pairs={{0,127},{1,0},{2,1},{3,2},{4,3},{5,4},{6,5},{7,6},{8,7},{9,8},{10,... | collective-permute-start | bytes 491528 | tf_op jit(solution)/shard_map/ppermute | solution.py:21
  16.4 10.0 %collective-permute-start = (bf16[32,4,640]{2,1,0:T(4,128)(2,1)S(1)}, bf16[32,4,640]{2,1,0:T(4,128)(2,1)S(1)}, u32[]{:S(2)}, u32[]{:S(2)}) collective-permute-start(bf16[32,4,640]{2,1,0:T(4,128)(2,1)S(1)} %get-tuple-element.35), channel_id=1, source_target_pairs={{0,1},{1,2},{2,3},{3,4},{4,5},{5,6},{6,7},{7,8},{8,9},{9,10},{10,1... | collective-permute-start | bytes 491528 | tf_op jit(solution)/shard_map/ppermute | solution.py:21
  26.6 8.7 %collective-permute-start.3 = (bf16[4,40,640]{2,1,0:T(8,128)(2,1)S(1)}, bf16[4,40,640]{2,1,0:T(8,128)(2,1)S(1)}, u32[]{:S(2)}, u32[]{:S(2)}) collective-permute-start(bf16[4,40,640]{2,1,0:T(8,128)(2,1)S(1)} %get-tuple-element.34), channel_id=1, source_target_pairs={{0,124},{1,125},{2,126},{3,127},{4,0},{5,1},{6,2},{7,3},{8,4},{9,5... | collective-permute-start | bytes 614408 | tf_op jit(solution)/shard_map/ppermute | solution.py:21
  29.3 14.3 %collective-permute-start.2 = (bf16[4,40,640]{2,1,0:T(8,128)(2,1)S(1)}, bf16[4,40,640]{2,1,0:T(8,128)(2,1)S(1)}, u32[]{:S(2)}, u32[]{:S(2)}) collective-permute-start(bf16[4,40,640]{2,1,0:T(8,128)(2,1)S(1)} %get-tuple-element.33), channel_id=1, source_target_pairs={{0,4},{1,5},{2,6},{3,7},{4,8},{5,9},{6,10},{7,11},{8,12},{9,13},{1... | collective-permute-start | bytes 614408 | tf_op jit(solution)/shard_map/ppermute | solution.py:21
  47.3 7.7 %copy-start.8 = (f32[36,36]{1,0:T(8,128)}, f32[36,36]{1,0:T(8,128)S(1)}, u32[]{:S(2)}) copy-start(f32[36,36]{1,0:T(8,128)S(1)} %convert_reduce_fusion.1) | copy-start | bytes 15556
  47.9 1.1 copy-start.14
  48.0 1.1 copy-start.17
  51.0 0.7 copy-start.13
  51.6 3.7 %copy-start.2 = (f32[36,1,36,128]{3,0,2,1:T(8,128)}, f32[36,1,36,128]{3,0,2,1:T(8,128)S(1)}, u32[]{:S(2)}) copy-start(f32[36,1,36,128]{3,0,2,1:T(8,128)S(1)} %slice.165) | copy-start | bytes 1990660
  71.9 1.4 copy-start.10
  72.0 1.4 copy-start.11
  94.7 5.1 %collective-permute-start.4 = (f32[64,4736]{1,0:T(8,128)}, f32[64,4736]{1,0:T(8,128)}, u32[]{:S(2)}, u32[]{:S(2)}) collective-permute-start(f32[64,4736]{1,0:T(8,128)} %constant_dynamic-slice_fusion.6), channel_id=1, source_target_pairs={{0,1},{1,0},{2,3},{3,2},{4,5},{5,4},{6,7},{7,6},{8,9},{9,8},{10,11... | collective-permute-start | bytes 3637256 | tf_op jit(solution)/shard_map/ppermute | solution.py:94
  101.2 1.0 copy-start.4
  102.3 21.9 %copy-start.9 = (f32[36,36]{1,0:T(8,128)S(1)}, f32[36,36]{1,0:T(8,128)}, u32[]{:S(2)}) copy-start(f32[36,36]{1,0:T(8,128)} %copy-done.8) | copy-start | bytes 15556
  102.3 22.0 %copy-start.7 = (f32[36,8,5,128]{3,1,2,0:T(8,128)S(1)}, f32[36,8,5,128]{3,1,2,0:T(8,128)}, u32[]{:S(2)}) copy-start(f32[36,8,5,128]{3,1,2,0:T(8,128)} %get-tuple-element.38) | copy-start | bytes 2211844
  102.4 18.7 %collective-permute-start.5 = (f32[32,4736]{1,0:T(8,128)S(1)}, f32[32,4736]{1,0:T(8,128)S(1)}, u32[]{:S(2)}, u32[]{:S(2)}) collective-permute-start(f32[32,4736]{1,0:T(8,128)S(1)} %constant_dynamic-slice_fusion.5), channel_id=1, source_target_pairs={{0,2},{2,0},{4,6},{6,4},{8,10},{10,8},{12,14},{14,12},{1,3},{3,1},... | collective-permute-start | bytes 1818632 | tf_op jit(solution)/shard_map/ppermute | solution.py:94
  122.2 18.0 %collective-permute-start.6 = (f32[16,4736]{1,0:T(8,128)S(1)}, f32[16,4736]{1,0:T(8,128)S(1)}, u32[]{:S(2)}, u32[]{:S(2)}) collective-permute-start(f32[16,4736]{1,0:T(8,128)S(1)} %constant_dynamic-slice_fusion.4), channel_id=1, source_target_pairs={{0,4},{2,6},{4,0},{6,2},{8,12},{10,14},{12,8},{14,10},{1,5},{3,7},... | collective-permute-start | bytes 909320 | tf_op jit(solution)/shard_map/ppermute | solution.py:94
  140.3 11.3 %collective-permute-start.7 = (f32[8,4736]{1,0:T(8,128)S(1)}, f32[8,4736]{1,0:T(8,128)S(1)}, u32[]{:S(2)}, u32[]{:S(2)}) collective-permute-start(f32[8,4736]{1,0:T(8,128)S(1)} %constant_dynamic-slice_fusion.3), channel_id=1, source_target_pairs={{0,8},{2,10},{4,12},{6,14},{8,0},{10,2},{12,4},{14,6},{1,9},{3,11}... | collective-permute-start | bytes 454664 | tf_op jit(solution)/shard_map/ppermute | solution.py:94
  142.4 11.1 %copy-start.15 = (bf16[3,3,128,256]{3,2,1,0:T(8,128)(2,1)S(1)}, bf16[3,3,128,256]{3,2,1,0:T(8,128)(2,1)}, u32[]{:S(2)}) copy-start(bf16[3,3,128,256]{3,2,1,0:T(8,128)(2,1)} %param.12) | copy-start | bytes 1769476
  142.5 11.1 %copy-start.16 = (pred[8,5]{0,1:T(8,128)(4,1)S(1)}, pred[8,5]{0,1:T(8,128)(4,1)}, u32[]{:S(2)}) copy-start(pred[8,5]{0,1:T(8,128)(4,1)} %constant.182) | copy-start | bytes 124
  151.6 6.3 %collective-permute-start.8 = (f32[4,4736]{1,0:T(4,128)S(1)}, f32[4,4736]{1,0:T(4,128)S(1)}, u32[]{:S(2)}, u32[]{:S(2)}) collective-permute-start(f32[4,4736]{1,0:T(4,128)S(1)} %constant_dynamic-slice_fusion.2), channel_id=1, source_target_pairs={{0,16},{16,0},{32,48},{48,32},{64,80},{80,64},{96,112},{112,96},{1... | collective-permute-start | bytes 227336 | tf_op jit(solution)/shard_map/ppermute | solution.py:94
  154.6 5.3 %copy-start.12 = (f32[256]{0:T(256)S(1)}, f32[256]{0:T(256)}, u32[]{:S(2)}) copy-start(f32[256]{0:T(256)} %param.13) | copy-start | bytes 3076
  155.1 5.2 %copy-start.6 = (f32[36,8,5,128]{3,1,2,0:T(8,128)S(1)}, f32[36,8,5,128]{3,1,2,0:T(8,128)}, u32[]{:S(2)}) copy-start(f32[36,8,5,128]{3,1,2,0:T(8,128)} %get-tuple-element.37) | copy-start | bytes 2211844
  158.0 6.8 %collective-permute-start.9 = (f32[2,4736]{1,0:T(2,128)S(1)}, f32[2,4736]{1,0:T(2,128)S(1)}, u32[]{:S(2)}, u32[]{:S(2)}) collective-permute-start(f32[2,4736]{1,0:T(2,128)S(1)} %constant_dynamic-slice_fusion.1), channel_id=1, source_target_pairs={{0,32},{16,48},{32,0},{48,16},{64,96},{80,112},{96,64},{112,80},{1... | collective-permute-start | bytes 113672 | tf_op jit(solution)/shard_map/ppermute | solution.py:94
  160.3 6.4 %copy-start.3 = (f32[36,1,36,128]{3,0,2,1:T(8,128)S(1)}, f32[36,1,36,128]{3,0,2,1:T(8,128)}, u32[]{:S(2)}) copy-start(f32[36,1,36,128]{3,0,2,1:T(8,128)} %copy-done.2) | copy-start | bytes 1990660
  164.8 9.6 %collective-permute-start.10 = (f32[1,4736]{1,0:T(1,128)S(1)}, f32[1,4736]{1,0:T(1,128)S(1)}, u32[]{:S(2)}, u32[]{:S(2)}) collective-permute-start(f32[1,4736]{1,0:T(1,128)S(1)} %constant_dynamic-slice_fusion), channel_id=1, source_target_pairs={{0,64},{16,80},{32,96},{48,112},{64,0},{80,16},{96,32},{112,48},{1... | collective-permute-start | bytes 56840 | tf_op jit(solution)/shard_map/ppermute | solution.py:94
  174.4 5.7 %collective-permute-start.11 = (f32[1,4736]{1,0:T(1,128)S(1)}, f32[1,4736]{1,0:T(1,128)S(1)}, u32[]{:S(2)}, u32[]{:S(2)}) collective-permute-start(f32[1,4736]{1,0:T(1,128)S(1)} %dynamic-slice_add_fusion.6), channel_id=1, source_target_pairs={{0,128},{128,0},{256,384},{384,256},{1,129},{129,1},{257,385},{385... | collective-permute-start | bytes 56840 | tf_op jit(solution)/shard_map/ppermute | solution.py:94
  178.6 4.8 %copy-start.5 = (bf16[1,1,32,32,256]{4,3,2,1,0:T(8,128)(2,1)S(1)}, bf16[1,1,32,32,256]{4,3,2,1,0:T(8,128)(2,1)}, u32[]{:S(2)}) copy-start(bf16[1,1,32,32,256]{4,3,2,1,0:T(8,128)(2,1)} %param.9) | copy-start | bytes 1572868
  180.1 7.2 %collective-permute-start.12 = (f32[1,4736]{1,0:T(1,128)S(1)}, f32[1,4736]{1,0:T(1,128)S(1)}, u32[]{:S(2)}, u32[]{:S(2)}) collective-permute-start(f32[1,4736]{1,0:T(1,128)S(1)} %add.213), channel_id=1, source_target_pairs={{0,256},{128,384},{256,0},{384,128},{1,257},{129,385},{257,1},{385... | collective-permute-start | bytes 56840 | tf_op jit(solution)/shard_map/ppermute | solution.py:94

commit v2 on v1

--- a/solution.py
+++ b/solution.py
@@ -94,28 +94,35 @@
     return lax.ppermute(value, axis, [(i, i ^ bit) for i in range(size)])
 
 
-def halve(block, axis, bit):
-    half = block.shape[0] // 2
+def to_wire(send, exact):
+    rounded = lax.reduce_precision(send[:, :exact], exponent_bits=8, mantissa_bits=7)
+    low = (send[:, :exact] - rounded).astype(jnp.bfloat16)
+    return jnp.concatenate(
+        [rounded.astype(jnp.bfloat16), low, send[:, 2 * exact :].astype(jnp.bfloat16)], axis=1
+    )
+
+
+def from_wire(got, exact):
+    got = got.astype(jnp.float32)
+    joined = got[:, :exact] + got[:, exact : 2 * exact]
+    return jnp.concatenate([joined, jnp.zeros_like(joined), got[:, 2 * exact :]], axis=1)
+
+
+def halve(block, axis, bit, exact):
     upper = (lax.axis_index(axis) // bit) % 2
-    keep = lax.dynamic_slice_in_dim(block, upper * half, half, axis=0)
-    send = lax.dynamic_slice_in_dim(block, (1 - upper) * half, half, axis=0)
-    return keep + swap(send, axis, bit)
-
-
-def reduce_shards(rows, sizes):
-    names = ("z", "y", "core")
-    counts = [len(_bits(size)) for size in sizes]
+    even, odd = block[0::2], block[1::2]
+    keep = jnp.where(upper == 0, even, odd)
+    send = jnp.where(upper == 0, odd, even)
+    return keep + from_wire(swap(to_wire(send, exact), axis, bit), exact)
+
+
+def reduce_shards(rows, sizes, exact):
     steps = [("core", b) for b in _bits(sizes[2])]
     steps += [("y", b) for b in _bits(sizes[1])]
     steps += [("z", b) for b in _bits(sizes[0])]
-    starts = dict(zip(names, np.cumsum([0] + counts[:-1]).tolist()))
-    total = dict(zip(names, counts))
-    order = [starts[axis] + total[axis] - 1 - int(math.log2(bit)) for axis, bit in steps]
-    width = rows.shape[1]
-    block = rows.reshape((2,) * len(order) + (width,))
-    block = jnp.transpose(block, order + [len(order)]).reshape(rows.shape)
+    block = rows
     for axis, bit in steps:
-        block = halve(block, axis, bit)
+        block = halve(block, axis, bit, exact)
     snap_size = lax.axis_size("snap")
     bit = 1
     while bit < snap_size:
@@ -172,32 +179,34 @@
     grad_ba = jnp.sum(g_pre_inner.astype(jnp.float32), axis=(0, 1))
     per_a = channels // space_count
     per_b = hidden_channels // space_count
+    exact = per_a + per_b
     rows = jnp.concatenate(
         [
+            grad_ba.reshape(space_count, per_b),
+            grad_bb.reshape(space_count, per_a),
+            jnp.zeros((space_count, exact), jnp.float32),
             jnp.moveaxis(grad_wa.reshape(3, 3, space_count, per_a, hidden_channels), 2, 0).reshape(
                 space_count, -1
             ),
             jnp.moveaxis(grad_wb.reshape(3, 3, space_count, per_b, channels), 2, 0).reshape(
                 space_count, -1
             ),
-            grad_ba.reshape(space_count, per_b),
-            grad_bb.reshape(space_count, per_a),
         ],
         axis=1,
     )
     width = rows.shape[1]
     padded_width = -(-width // 128) * 128
     rows = jnp.pad(rows, ((0, 0), (0, padded_width - width)))
-    mine = reduce_shards(rows, sizes)[0] * scale
-    cut_a = 9 * per_a * hidden_channels
+    mine = reduce_shards(rows, sizes, exact)[0] * scale
+    cut_a = 2 * exact + 9 * per_a * hidden_channels
     cut_b = cut_a + 9 * per_b * channels
     return (
         field_out[None, None],
         g_input[None, None],
-        mine[:cut_a].reshape(3, 3, per_a, hidden_channels),
+        mine[2 * exact : cut_a].reshape(3, 3, per_a, hidden_channels),
         mine[cut_a:cut_b].reshape(3, 3, per_b, channels),
-        mine[cut_b : cut_b + per_b],
-        mine[cut_b + per_b : cut_b + per_b + per_a],
+        mine[:per_b],
+        mine[per_b:exact],
     )
 
 

time: 191 us -> 193 us (1.010)
  waiting for transfers between devices: 75.8 us -> 58.3 us
  local copies, waits for them, and re-layouts: 33 us -> 49.8 us
    slice x2 -> x28, local copies, waits for them, and re-layouts: 1.09 us -> 22.1 us  [the longest x12 16.4 us: halve(): even, odd = (block[0::2], block[1::2])]
    ppermute x9, waiting for transfers between devices: 58.4 us -> 40.9 us  [swap(): return lax.ppermute(value, axis, [(i, i ^ bit) for i in range(size)])]
    concatenate x1 -> x15, local copies, waits for them, and re-layouts: 6.75 us -> 11.4 us  [the longest x7 4.23 us: from_wire(): jnp.concatenate([joined, jnp.zeros_like(joined), got[:, 2 * exact:]], axi...]
    unnamed x40 -> x49, local copies, waits for them, and re-layouts: 5.85 us -> 2.51 us
    transpose x1 -> x0, local copies, waits for them, and re-layouts: 3.3 us -> none  [reduce_shards(): block = jnp.transpose(block, order + [len(order)]).reshape(rows.shape)]
    reshape x2 -> x3, local copies, waits for them, and re-layouts: 6.22 us -> 3.53 us  [the longest x1 1.41 us: local(): jnp.moveaxis(grad_wa.reshape(3, 3, space_count, per_a, hidden_channels),...]
    add x7 -> x14, other arithmetic: 2.67 us -> 5.01 us  [the longest x7 3.87 us: halve(): return keep + from_wire(swap(to_wire(send, exact), axis, bit), exact)]
    another operation x2, other arithmetic: 2.34 us -> 0.08 us  [tap_sums(): return jnp.stack(tap_rows)]
  transfers between devices with their start and end apart: 13 -> 13, of which waited for: 13 -> 13; matrix products, arithmetic and copies ran while one was open for 4% -> 5% of each run, Pallas kernels for 0% -> 0%
where the time goes in v2:
time: 193 us; the launch traced here: 192 us
  waiting for transfers between devices  58.3 us (30%)
  local copies, waits for them, and re-layouts  49.8 us (26%)
  starting transfers between devices  44.3 us (23%)
  matrix products  19.7 us (10%)
  other arithmetic  17.4 us (9%)
  between operations  2.04 us (1%)
    ppermute x9, waiting for transfers between devices, swap(): return lax.ppermute(value, axis, [(i, i ^ bit) for i in range(size)])  40.9 us
    ppermute x9, starting transfers between devices, swap(): return lax.ppermute(value, axis, [(i, i ^ bit) for i in range(size)])  22.4 us
    ppermute x4, starting transfers between devices, from_behind(): lax.ppermute(array, axis, [(i, (i + by) % length) for i in range(length)])  21.9 us
    ppermute x4, waiting for transfers between devices, from_behind(): lax.ppermute(array, axis, [(i, (i + by) % length) for i in range(length)])  17.4 us
    slice x12, local copies, waits for them, and re-layouts, halve(): even, odd = (block[0::2], block[1::2])  16.4 us
    dot_general x18, matrix products, tap_sums(): lax.dot_general(window, flat_out, (((0,), (0,)), ((), ())), preferred_ele...  11.6 us
    conv_general_dilated x4, matrix products, dilated(): lax.conv_general_dilated(padded[None], kernel, (1, 1), 'VALID', rhs_dilat...  8.13 us
    concatenate x7, local copies, waits for them, and re-layouts, from_wire(): jnp.concatenate([joined, jnp.zeros_like(joined), got[:, 2 * exact:]], axi...  4.23 us
  transfers between devices with their start and end apart: 13, of which 13 were waited for; matrix products, arithmetic and copies ran while one was open for 5% of the time, Pallas kernels for 0%

profile of v2, /device:TPU:6, one launch (start us, length us, event | category | flops | bytes accessed | tf_op | source)
XLA Modules:
  0.0 191.5 jit_solution(2919304183371454296)
XLA Ops:
  1.5 1.3 convert_reduce_fusion
  3.1 13.3 %collective-permute-start.1 = (bf16[32,4,640]{2,1,0:T(4,128)(2,1)S(1)}, bf16[32,4,640]{2,1,0:T(4,128)(2,1)S(1)}, u32[]{:S(2)}, u32[]{:S(2)}) collective-permute-start(bf16[32,4,640]{2,1,0:T(4,128)(2,1)S(1)} %get-tuple-element.42), channel_id=1, source_target_pairs={{0,127},{1,0},{2,1},{3,2},{4,3},{5,4},{6,5},{7,6},{8,7},{9,8},{10,... | collective-permute-start | bytes 491528 | tf_op jit(solution)/shard_map/ppermute | solution.py:21
  16.4 1.9 %collective-permute-start = (bf16[32,4,640]{2,1,0:T(4,128)(2,1)S(1)}, bf16[32,4,640]{2,1,0:T(4,128)(2,1)S(1)}, u32[]{:S(2)}, u32[]{:S(2)}) collective-permute-start(bf16[32,4,640]{2,1,0:T(4,128)(2,1)S(1)} %get-tuple-element.41), channel_id=1, source_target_pairs={{0,1},{1,2},{2,3},{3,4},{4,5},{5,6},{6,7},{7,8},{8,9},{9,10},{10,1... | collective-permute-start | bytes 491528 | tf_op jit(solution)/shard_map/ppermute | solution.py:21
  19.3 7.1 %collective-permute-done = bf16[32,4,640]{2,1,0:T(4,128)(2,1)S(1)} collective-permute-done((bf16[32,4,640]{2,1,0:T(4,128)(2,1)S(1)}, bf16[32,4,640]{2,1,0:T(4,128)(2,1)S(1)}, u32[]{:S(2)}, u32[]{:S(2)}) %collective-permute-start) | collective-permute-done | bytes 163872 | tf_op jit(solution)/shard_map/ppermute | solution.py:21
  26.6 1.9 %collective-permute-start.3 = (bf16[4,40,640]{2,1,0:T(8,128)(2,1)S(1)}, bf16[4,40,640]{2,1,0:T(8,128)(2,1)S(1)}, u32[]{:S(2)}, u32[]{:S(2)}) collective-permute-start(bf16[4,40,640]{2,1,0:T(8,128)(2,1)S(1)} %get-tuple-element.40), channel_id=1, source_target_pairs={{0,124},{1,125},{2,126},{3,127},{4,0},{5,1},{6,2},{7,3},{8,4},{9,5... | collective-permute-start | bytes 614408 | tf_op jit(solution)/shard_map/ppermute | solution.py:21
  29.3 4.8 %collective-permute-start.2 = (bf16[4,40,640]{2,1,0:T(8,128)(2,1)S(1)}, bf16[4,40,640]{2,1,0:T(8,128)(2,1)S(1)}, u32[]{:S(2)}, u32[]{:S(2)}) collective-permute-start(bf16[4,40,640]{2,1,0:T(8,128)(2,1)S(1)} %get-tuple-element.39), channel_id=1, source_target_pairs={{0,4},{1,5},{2,6},{3,7},{4,8},{5,9},{6,10},{7,11},{8,12},{9,13},{1... | collective-permute-start | bytes 614408 | tf_op jit(solution)/shard_map/ppermute | solution.py:21
  34.1 1.1 collective-permute-done.3
  35.3 8.4 %collective-permute-done.2 = bf16[4,40,640]{2,1,0:T(8,128)(2,1)S(1)} collective-permute-done((bf16[4,40,640]{2,1,0:T(8,128)(2,1)S(1)}, bf16[4,40,640]{2,1,0:T(8,128)(2,1)S(1)}, u32[]{:S(2)}, u32[]{:S(2)}) %collective-permute-start.2) | collective-permute-done | bytes 204832 | tf_op jit(solution)/shard_map/ppermute | solution.py:21
  43.7 3.3 %pad_maximum_fusion = (bf16[40,40,256]{2,1,0:T(8,128)(2,1)S(1)}, bf16[40,40,256]{2,1,0:T(8,128)(2,1)S(1)}) fusion(bf16[4,40,640]{2,1,0:T(8,128)(2,1)S(1)} %broadcast_select_fusion.2, bf16[4,40,640]{2,1,0:T(8,128)(2,1)S(1)} %broadcast_select_fusion.3, bf16[32,4,640]{2,1,0:T(4,128)(2,1)S(1)} %broadcast_select_fusion.4, ...), kind=kLoop, calls=%fused_computation.50 | loop fusion | flops 11468800 | bytes 3686400 | tf_op jit(solution)/shard_map/concatenate | solution.py:89
  49.0 1.9 %fusion.18 = f32[36,8,5,128]{3,1,2,0:T(8,128)S(1)} fusion(bf16[3,3,128,256]{3,2,1,0:T(8,128)(2,1)S(1)} %copy-done.20, bf16[40,1,7,4,256]{4,2,3,0,1:T(8,128)(2,1)S(1)} %slice.376, bf16[40,1,8,5,256]{4,2,3,0,1:T(8,128)(2,1)S(1)} %copy.147, pred[8,5]{0,1:T(8,128)(4,1)S(1)} %copy-done.22), kind=kOutput, calls=%fused_computation.24 | convolution fusion | flops 853954560 | bytes 2719784 | tf_op jit(solution)/shard_map/conv_general_dilated | solution.py:35
  51.6 3.1 %fusion.34 = (f32[36,8,5,128]{3,1,2,0:T(8,128)}, f32[36,8,5,128]{3,1,2,0:T(8,128)}, f32[36,8,5,128]{3,1,2,0:T(8,128)S(1)}) fusion(f32[128]{0:T(128)S(1)} %copy-done.19, bf16[3,3,256,128]{3,2,1,0:T(8,128)(2,1)S(1)} %copy-done, bf16[40,1,7,4,256]{4,2,3,0,1:T(8,128)(2,1)S(1)} %slice.372, bf16[40,1,8,5,256]{4,2,3,0,1:T(8,128)(2,1)S(1)} %copy.140, ...), kind=kOutput, calls=%fused_computation.60 | convolution fusion | flops 855982080 | bytes 4194856 | tf_op jit(solution)/shard_map/conv_general_dilated | solution.py:35
  70.0 1.4 copy.163
  72.0 1.4 copy.164
  74.1 3.1 %concatenate.81 = f32[128,4614]{1,0:T(8,128)S(1)} concatenate(f32[128,1]{1,0:T(8,128)} %copy.162, f32[128,2]{1,0:T(8,128)} %reshape.116, f32[128,3]{1,0:T(8,128)} %broadcast_in_dim.33, f32[128,2304]{1,0:T(8,128)} %copy.163, f32[128,2304]{1,0:T(8,128)} %copy.164), dimensions={1} | concatenate | bytes 4724736 | tf_op jit(solution)/shard_map/concatenate | solution.py:183
  77.1 1.6 pad.4
  78.7 4.7 %slice.308 = f32[64,4736]{1,0:T(8,128)S(1)} slice(f32[128,4736]{1,0:T(8,128)} %pad.4), slice={[1:128:2], [0:4736:1]} | slice | bytes 2424832 | tf_op jit(solution)/shard_map/slice | solution.py:113
  83.4 4.7 %slice.307 = f32[64,4736]{1,0:T(8,128)S(1)} slice(f32[128,4736]{1,0:T(8,128)} %pad.4), slice={[0:128:2], [0:4736:1]} | slice | bytes 2424832 | tf_op jit(solution)/shard_map/slice | solution.py:113
  88.9 1.1 slice.525
  89.9 2.4 %concatenate.82 = bf16[64,4736]{1,0:T(8,128)(2,1)} concatenate(bf16[64,3]{1,0:T(8,128)(2,1)} %get-tuple-element.44, bf16[64,3]{1,0:T(8,128)(2,1)} %get-tuple-element.43, bf16[64,4730]{1,0:T(8,128)(2,1)} %slice.525), dimensions={1} | concatenate | bytes 1212416 | tf_op jit(solution)/shard_map/concatenate | solution.py:100
  92.3 1.9 collective-permute-start.4
  94.2 2.3 %collective-permute-done.4 = bf16[64,4736]{1,0:T(8,128)(2,1)} collective-permute-done((bf16[64,4736]{1,0:T(8,128)(2,1)}, bf16[64,4736]{1,0:T(8,128)(2,1)}, u32[]{:S(2)}, u32[]{:S(2)}) %collective-permute-start.4) | collective-permute-done | bytes 606240 | tf_op jit(solution)/shard_map/ppermute | solution.py:94
  96.6 1.1 convert_element_type.155
  98.4 2.3 %slice.400 = f32[64,4730]{1,0:T(8,128)} slice(bf16[64,4736]{1,0:T(8,128)(2,1)} %collective-permute-done.4), slice={[0:64], [6:4736]} | slice | bytes 2421760 | tf_op jit(solution)/shard_map/slice | solution.py:108
  101.4 2.4 %concatenate.83 = f32[64,4736]{1,0:T(8,128)} concatenate(f32[64,3]{1,0:T(8,128)} %slice_add_fusion, f32[64,3]{1,0:T(8,128)} %broadcast_in_dim.34, f32[64,4730]{1,0:T(8,128)} %slice.400), dimensions={1} | concatenate | bytes 2424832 | tf_op jit(solution)/shard_map/concatenate | solution.py:108
  103.8 2.5 %select_add_fusion = f32[64,4736]{1,0:T(8,128)} fusion(f32[64,4736]{1,0:T(8,128)} %concatenate.83, f32[64,4736]{1,0:T(8,128)S(1)} %slice.307, f32[64,4736]{1,0:T(8,128)S(1)} %slice.308, pred[]{:T(512)S(6)} %eq.44), kind=kLoop, calls=%fused_computation.23 | loop fusion | flops 606208 | bytes 4849665 | tf_op jit(solution)/shard_map/add | solution.py:116
  106.3 2.5 %slice.315 = f32[32,4736]{1,0:T(8,128)S(1)} slice(f32[64,4736]{1,0:T(8,128)} %select_add_fusion), slice={[1:64:2], [0:4736:1]} | slice | bytes 1212416 | tf_op jit(solution)/shard_map/slice | solution.py:113
  110.3 4.6 %collective-permute-start.5 = (bf16[32,4736]{1,0:T(8,128)(2,1)S(1)}, bf16[32,4736]{1,0:T(8,128)(2,1)S(1)}, u32[]{:S(2)}, u32[]{:S(2)}) collective-permute-start(bf16[32,4736]{1,0:T(8,128)(2,1)S(1)} %concatenate.84), channel_id=1, source_target_pairs={{0,2},{2,0},{4,6},{6,4},{8,10},{10,8},{12,14},{14,12},{1,3},{3,1},... | collective-permute-start | bytes 909320 | tf_op jit(solution)/shard_map/ppermute | solution.py:94
  114.9 7.4 %collective-permute-done.5 = bf16[32,4736]{1,0:T(8,128)(2,1)S(1)} collective-permute-done((bf16[32,4736]{1,0:T(8,128)(2,1)S(1)}, bf16[32,4736]{1,0:T(8,128)(2,1)S(1)}, u32[]{:S(2)}, u32[]{:S(2)}) %collective-permute-start.5) | collective-permute-done | bytes 303136 | tf_op jit(solution)/shard_map/ppermute | solution.py:94
  122.6 1.1 concatenate.85
  123.7 1.2 select_add_fusion.1
  126.7 1.9 collective-permute-start.6
  129.0 9.4 %collective-permute-done.6 = bf16[16,4736]{1,0:T(8,128)(2,1)S(1)} collective-permute-done((bf16[16,4736]{1,0:T(8,128)(2,1)}, bf16[16,4736]{1,0:T(8,128)(2,1)S(1)}, u32[]{:S(2)}, u32[]{:S(2)}) %collective-permute-start.6) | collective-permute-done | bytes 151584 | tf_op jit(solution)/shard_map/ppermute | solution.py:94
  140.3 1.9 %collective-permute-start.7 = (bf16[8,4736]{1,0:T(8,128)(2,1)S(1)}, bf16[8,4736]{1,0:T(8,128)(2,1)S(1)}, u32[]{:S(2)}, u32[]{:S(2)}) collective-permute-start(bf16[8,4736]{1,0:T(8,128)(2,1)S(1)} %concatenate.88), channel_id=1, source_target_pairs={{0,8},{2,10},{4,12},{6,14},{8,0},{10,2},{12,4},{14,6},{1,9},{3,11}... | collective-permute-start | bytes 227336 | tf_op jit(solution)/shard_map/ppermute | solution.py:94
  142.7 7.8 %collective-permute-done.7 = bf16[8,4736]{1,0:T(8,128)(2,1)S(1)} collective-permute-done((bf16[8,4736]{1,0:T(8,128)(2,1)S(1)}, bf16[8,4736]{1,0:T(8,128)(2,1)S(1)}, u32[]{:S(2)}, u32[]{:S(2)}) %collective-permute-start.7) | collective-permute-done | bytes 75808 | tf_op jit(solution)/shard_map/ppermute | solution.py:94
  152.2 1.9 %collective-permute-start.8 = (bf16[4,4736]{1,0:T(4,128)(2,1)S(1)}, bf16[4,4736]{1,0:T(4,128)(2,1)S(1)}, u32[]{:S(2)}, u32[]{:S(2)}) collective-permute-start(bf16[4,4736]{1,0:T(4,128)(2,1)S(1)} %concatenate.90), channel_id=1, source_target_pairs={{0,16},{16,0},{32,48},{48,32},{64,80},{80,64},{96,112},{112,96},{1... | collective-permute-start | bytes 113672 | tf_op jit(solution)/shard_map/ppermute | solution.py:94
  154.1 2.1 %convolution_select_fusion.1 = f32[32,8,5,256]{3,1,2,0:T(8,128)S(1)} fusion(bf16[3,3,128,256]{3,2,1,0:T(8,128)(2,1)} %param.12, bf16[36,1,7,4,128]{4,2,3,0,1:T(8,128)(2,1)S(1)} %slice.374, bf16[36,1,8,5,128]{4,2,3,0,1:T(8,128)(2,1)S(1)} %copy.143, pred[8,5]{0,1:T(8,128)(4,1)S(1)} %copy-done.21), kind=kOutput, calls=%fused_computation.16 | convolution fusion | flops 757293056 | bytes 2527272 | tf_op jit(solution)/shard_map/conv_general_dilated | solution.py:35
  156.7 1.4 collective-permute-done.8
  159.4 1.9 %collective-permute-start.9 = (bf16[2,4736]{1,0:T(2,128)(2,1)S(1)}, bf16[2,4736]{1,0:T(2,128)(2,1)S(1)}, u32[]{:S(2)}, u32[]{:S(2)}) collective-permute-start(bf16[2,4736]{1,0:T(2,128)(2,1)S(1)} %concatenate.92), channel_id=1, source_target_pairs={{0,32},{16,48},{32,0},{48,16},{64,96},{80,112},{96,64},{112,80},{1... | collective-permute-start | bytes 56840 | tf_op jit(solution)/shard_map/ppermute | solution.py:94
  161.8 1.3 copy.150
  163.1 3.1 %collective-permute-done.9 = bf16[2,4736]{1,0:T(2,128)(2,1)S(1)} collective-permute-done((bf16[2,4736]{1,0:T(2,128)(2,1)S(1)}, bf16[2,4736]{1,0:T(2,128)(2,1)S(1)}, u32[]{:S(2)}, u32[]{:S(2)}) %collective-permute-start.9) | collective-permute-done | bytes 18976 | tf_op jit(solution)/shard_map/ppermute | solution.py:94
  166.9 1.9 %collective-permute-start.10 = (bf16[1,4736]{1,0:T(2,128)(2,1)S(1)}, bf16[1,4736]{1,0:T(2,128)(2,1)S(1)}, u32[]{:S(2)}, u32[]{:S(2)}) collective-permute-start(bf16[1,4736]{1,0:T(2,128)(2,1)S(1)} %concatenate.94), channel_id=1, source_target_pairs={{0,64},{16,80},{32,96},{48,112},{64,0},{80,16},{96,32},{112,48},{1... | collective-permute-start | bytes 28424 | tf_op jit(solution)/shard_map/ppermute | solution.py:94
  169.4 7.1 %collective-permute-done.10 = bf16[1,4736]{1,0:T(2,128)(2,1)S(1)} collective-permute-done((bf16[1,4736]{1,0:T(2,128)(2,1)S(1)}, bf16[1,4736]{1,0:T(2,128)(2,1)S(1)}, u32[]{:S(2)}, u32[]{:S(2)}) %collective-permute-start.10) | collective-permute-done | bytes 9504 | tf_op jit(solution)/shard_map/ppermute | solution.py:94
  176.9 3.0 %collective-permute-start.11 = (f32[1,4736]{1,0:T(1,128)S(1)}, f32[1,4736]{1,0:T(1,128)S(1)}, u32[]{:S(2)}, u32[]{:S(2)}) collective-permute-start(f32[1,4736]{1,0:T(1,128)S(1)} %fusion.126), channel_id=1, source_target_pairs={{0,128},{128,0},{256,384},{384,256},{1,129},{129,1},{257,385},{385... | collective-permute-start | bytes 56840 | tf_op jit(solution)/shard_map/ppermute | solution.py:94
  179.9 1.1 convolution_select_fusion
  182.5 3.3 %collective-permute-start.12 = (f32[1,4736]{1,0:T(1,128)S(1)}, f32[1,4736]{1,0:T(1,128)S(1)}, u32[]{:S(2)}, u32[]{:S(2)}) collective-permute-start(f32[1,4736]{1,0:T(1,128)S(1)} %add.184), channel_id=1, source_target_pairs={{0,256},{128,384},{256,0},{384,128},{1,257},{129,385},{257,1},{385... | collective-permute-start | bytes 56840 | tf_op jit(solution)/shard_map/ppermute | solution.py:94
  185.9 1.4 fusion.26
  187.3 1.1 copy.165
  188.3 1.4 collective-permute-done.12
  (193 shorter events, 38.9 us)
Async XLA Ops:
  0.6 50.5 %copy-start = (bf16[3,3,256,128]{3,2,1,0:T(8,128)(2,1)S(1)}, bf16[3,3,256,128]{3,2,1,0:T(8,128)(2,1)}, u32[]{:S(2)}) copy-start(bf16[3,3,256,128]{3,2,1,0:T(8,128)(2,1)} %param.10) | copy-start | bytes 1769476
  0.6 2.3 %copy-start.1 = (bf16[1,1,32,32,256]{4,3,2,1,0:T(8,128)(2,1)S(1)}, bf16[1,1,32,32,256]{4,3,2,1,0:T(8,128)(2,1)}, u32[]{:S(2)}) copy-start(bf16[1,1,32,32,256]{4,3,2,1,0:T(8,128)(2,1)} %param.7) | copy-start | bytes 1572868
  3.1 16.1 %collective-permute-start.1 = (bf16[32,4,640]{2,1,0:T(4,128)(2,1)S(1)}, bf16[32,4,640]{2,1,0:T(4,128)(2,1)S(1)}, u32[]{:S(2)}, u32[]{:S(2)}) collective-permute-start(bf16[32,4,640]{2,1,0:T(4,128)(2,1)S(1)} %get-tuple-element.42), channel_id=1, source_target_pairs={{0,127},{1,0},{2,1},{3,2},{4,3},{5,4},{6,5},{7,6},{8,7},{9,8},{10,... | collective-permute-start | bytes 491528 | tf_op jit(solution)/shard_map/ppermute | solution.py:21
  16.4 10.0 %collective-permute-start = (bf16[32,4,640]{2,1,0:T(4,128)(2,1)S(1)}, bf16[32,4,640]{2,1,0:T(4,128)(2,1)S(1)}, u32[]{:S(2)}, u32[]{:S(2)}) collective-permute-start(bf16[32,4,640]{2,1,0:T(4,128)(2,1)S(1)} %get-tuple-element.41), channel_id=1, source_target_pairs={{0,1},{1,2},{2,3},{3,4},{4,5},{5,6},{6,7},{7,8},{8,9},{9,10},{10,1... | collective-permute-start | bytes 491528 | tf_op jit(solution)/shard_map/ppermute | solution.py:21
  26.6 8.7 %collective-permute-start.3 = (bf16[4,40,640]{2,1,0:T(8,128)(2,1)S(1)}, bf16[4,40,640]{2,1,0:T(8,128)(2,1)S(1)}, u32[]{:S(2)}, u32[]{:S(2)}) collective-permute-start(bf16[4,40,640]{2,1,0:T(8,128)(2,1)S(1)} %get-tuple-element.40), channel_id=1, source_target_pairs={{0,124},{1,125},{2,126},{3,127},{4,0},{5,1},{6,2},{7,3},{8,4},{9,5... | collective-permute-start | bytes 614408 | tf_op jit(solution)/shard_map/ppermute | solution.py:21
  29.3 14.3 %collective-permute-start.2 = (bf16[4,40,640]{2,1,0:T(8,128)(2,1)S(1)}, bf16[4,40,640]{2,1,0:T(8,128)(2,1)S(1)}, u32[]{:S(2)}, u32[]{:S(2)}) collective-permute-start(bf16[4,40,640]{2,1,0:T(8,128)(2,1)S(1)} %get-tuple-element.39), channel_id=1, source_target_pairs={{0,4},{1,5},{2,6},{3,7},{4,8},{5,9},{6,10},{7,11},{8,12},{9,13},{1... | collective-permute-start | bytes 614408 | tf_op jit(solution)/shard_map/ppermute | solution.py:21
  47.2 7.7 %copy-start.13 = (f32[36,36]{1,0:T(8,128)}, f32[36,36]{1,0:T(8,128)S(1)}, u32[]{:S(2)}) copy-start(f32[36,36]{1,0:T(8,128)S(1)} %convert_reduce_fusion.1) | copy-start | bytes 15556
  47.9 1.1 copy-start.20
  47.9 1.1 copy-start.22
  50.9 0.7 copy-start.19
  51.6 3.7 %copy-start.2 = (f32[36,1,36,128]{3,0,2,1:T(8,128)}, f32[36,1,36,128]{3,0,2,1:T(8,128)S(1)}, u32[]{:S(2)}) copy-start(f32[36,1,36,128]{3,0,2,1:T(8,128)S(1)} %slice.377) | copy-start | bytes 1990660
  69.9 1.5 copy-start.11
  69.9 1.5 copy-start.12
  69.9 1.5 copy-start.17
  69.9 1.5 copy-start.7
  69.9 1.5 copy-start.8
  69.9 1.5 copy-start.9
  69.9 1.5 copy-start.10
  69.9 1.5 copy-start.15
  69.9 1.5 copy-start.16
  92.3 4.3 %collective-permute-start.4 = (bf16[64,4736]{1,0:T(8,128)(2,1)}, bf16[64,4736]{1,0:T(8,128)(2,1)}, u32[]{:S(2)}, u32[]{:S(2)}) collective-permute-start(bf16[64,4736]{1,0:T(8,128)(2,1)} %concatenate.82), channel_id=1, source_target_pairs={{0,1},{1,0},{2,3},{3,2},{4,5},{5,4},{6,7},{7,6},{8,9},{9,8},{10,11... | collective-permute-start | bytes 1818632 | tf_op jit(solution)/shard_map/ppermute | solution.py:94
  106.3 2.5 %copy-start.4 = (f32[64,4736]{1,0:T(8,128)S(1)}, f32[64,4736]{1,0:T(8,128)}, u32[]{:S(2)}) copy-start(f32[64,4736]{1,0:T(8,128)} %select_add_fusion) | copy-start | bytes 3637252
  110.3 12.0 %collective-permute-start.5 = (bf16[32,4736]{1,0:T(8,128)(2,1)S(1)}, bf16[32,4736]{1,0:T(8,128)(2,1)S(1)}, u32[]{:S(2)}, u32[]{:S(2)}) collective-permute-start(bf16[32,4736]{1,0:T(8,128)(2,1)S(1)} %concatenate.84), channel_id=1, source_target_pairs={{0,2},{2,0},{4,6},{6,4},{8,10},{10,8},{12,14},{14,12},{1,3},{3,1},... | collective-permute-start | bytes 909320 | tf_op jit(solution)/shard_map/ppermute | solution.py:94
  124.8 4.0 %copy-start.14 = (f32[36,36]{1,0:T(8,128)S(1)}, f32[36,36]{1,0:T(8,128)}, u32[]{:S(2)}) copy-start(f32[36,36]{1,0:T(8,128)} %copy-done.13) | copy-start | bytes 15556
  125.7 3.1 %copy-start.6 = (f32[36,8,5,128]{3,1,2,0:T(8,128)S(1)}, f32[36,8,5,128]{3,1,2,0:T(8,128)}, u32[]{:S(2)}) copy-start(f32[36,8,5,128]{3,1,2,0:T(8,128)} %get-tuple-element.46) | copy-start | bytes 2211844
  126.7 11.7 %collective-permute-start.6 = (bf16[16,4736]{1,0:T(8,128)(2,1)}, bf16[16,4736]{1,0:T(8,128)(2,1)S(1)}, u32[]{:S(2)}, u32[]{:S(2)}) collective-permute-start(bf16[16,4736]{1,0:T(8,128)(2,1)} %concatenate.86), channel_id=1, source_target_pairs={{0,4},{2,6},{4,0},{6,2},{8,12},{10,14},{12,8},{14,10},{1,5},{3,7},... | collective-permute-start | bytes 454664 | tf_op jit(solution)/shard_map/ppermute | solution.py:94
  140.3 10.2 %collective-permute-start.7 = (bf16[8,4736]{1,0:T(8,128)(2,1)S(1)}, bf16[8,4736]{1,0:T(8,128)(2,1)S(1)}, u32[]{:S(2)}, u32[]{:S(2)}) collective-permute-start(bf16[8,4736]{1,0:T(8,128)(2,1)S(1)} %concatenate.88), channel_id=1, source_target_pairs={{0,8},{2,10},{4,12},{6,14},{8,0},{10,2},{12,4},{14,6},{1,9},{3,11}... | collective-permute-start | bytes 227336 | tf_op jit(solution)/shard_map/ppermute | solution.py:94
  142.6 11.5 %copy-start.21 = (pred[8,5]{0,1:T(8,128)(4,1)S(1)}, pred[8,5]{0,1:T(8,128)(4,1)}, u32[]{:S(2)}) copy-start(pred[8,5]{0,1:T(8,128)(4,1)} %constant.183) | copy-start | bytes 124
  152.2 5.9 %collective-permute-start.8 = (bf16[4,4736]{1,0:T(4,128)(2,1)S(1)}, bf16[4,4736]{1,0:T(4,128)(2,1)S(1)}, u32[]{:S(2)}, u32[]{:S(2)}) collective-permute-start(bf16[4,4736]{1,0:T(4,128)(2,1)S(1)} %concatenate.90), channel_id=1, source_target_pairs={{0,16},{16,0},{32,48},{48,32},{64,80},{80,64},{96,112},{112,96},{1... | collective-permute-start | bytes 113672 | tf_op jit(solution)/shard_map/ppermute | solution.py:94
  156.2 5.1 %copy-start.18 = (f32[256]{0:T(256)S(1)}, f32[256]{0:T(256)}, u32[]{:S(2)}) copy-start(f32[256]{0:T(256)} %param.13) | copy-start | bytes 3076
  159.4 6.8 %collective-permute-start.9 = (bf16[2,4736]{1,0:T(2,128)(2,1)S(1)}, bf16[2,4736]{1,0:T(2,128)(2,1)S(1)}, u32[]{:S(2)}, u32[]{:S(2)}) collective-permute-start(bf16[2,4736]{1,0:T(2,128)(2,1)S(1)} %concatenate.92), channel_id=1, source_target_pairs={{0,32},{16,48},{32,0},{48,16},{64,96},{80,112},{96,64},{112,80},{1... | collective-permute-start | bytes 56840 | tf_op jit(solution)/shard_map/ppermute | solution.py:94
  163.0 5.8 %copy-start.3 = (f32[36,1,36,128]{3,0,2,1:T(8,128)S(1)}, f32[36,1,36,128]{3,0,2,1:T(8,128)}, u32[]{:S(2)}) copy-start(f32[36,1,36,128]{3,0,2,1:T(8,128)} %copy-done.2) | copy-start | bytes 1990660
  166.9 9.6 %collective-permute-start.10 = (bf16[1,4736]{1,0:T(2,128)(2,1)S(1)}, bf16[1,4736]{1,0:T(2,128)(2,1)S(1)}, u32[]{:S(2)}, u32[]{:S(2)}) collective-permute-start(bf16[1,4736]{1,0:T(2,128)(2,1)S(1)} %concatenate.94), channel_id=1, source_target_pairs={{0,64},{16,80},{32,96},{48,112},{64,0},{80,16},{96,32},{112,48},{1... | collective-permute-start | bytes 28424 | tf_op jit(solution)/shard_map/ppermute | solution.py:94
  176.9 5.7 %collective-permute-start.11 = (f32[1,4736]{1,0:T(1,128)S(1)}, f32[1,4736]{1,0:T(1,128)S(1)}, u32[]{:S(2)}, u32[]{:S(2)}) collective-permute-start(f32[1,4736]{1,0:T(1,128)S(1)} %fusion.126), channel_id=1, source_target_pairs={{0,128},{128,0},{256,384},{384,256},{1,129},{129,1},{257,385},{385... | collective-permute-start | bytes 56840 | tf_op jit(solution)/shard_map/ppermute | solution.py:94
  181.4 4.5 %copy-start.5 = (bf16[1,1,32,32,256]{4,3,2,1,0:T(8,128)(2,1)S(1)}, bf16[1,1,32,32,256]{4,3,2,1,0:T(8,128)(2,1)}, u32[]{:S(2)}) copy-start(bf16[1,1,32,32,256]{4,3,2,1,0:T(8,128)(2,1)} %param.9) | copy-start | bytes 1572868
  182.5 7.2 %collective-permute-start.12 = (f32[1,4736]{1,0:T(1,128)S(1)}, f32[1,4736]{1,0:T(1,128)S(1)}, u32[]{:S(2)}, u32[]{:S(2)}) collective-permute-start(f32[1,4736]{1,0:T(1,128)S(1)} %add.184), channel_id=1, source_target_pairs={{0,256},{128,384},{256,0},{384,128},{1,257},{129,385},{257,1},{385... | collective-permute-start | bytes 56840 | tf_op jit(solution)/shard_map/ppermute | solution.py:94

commit v3 on v1

--- a/solution.py
+++ b/solution.py
@@ -102,19 +102,25 @@
     return keep + swap(send, axis, bit)
 
 
-def reduce_shards(rows, sizes):
-    names = ("z", "y", "core")
-    counts = [len(_bits(size)) for size in sizes]
+def butterfly_steps(sizes):
     steps = [("core", b) for b in _bits(sizes[2])]
     steps += [("y", b) for b in _bits(sizes[1])]
     steps += [("z", b) for b in _bits(sizes[0])]
+    return steps
+
+
+def shard_bit_order(sizes):
+    names = ("z", "y", "core")
+    counts = [len(_bits(size)) for size in sizes]
     starts = dict(zip(names, np.cumsum([0] + counts[:-1]).tolist()))
     total = dict(zip(names, counts))
-    order = [starts[axis] + total[axis] - 1 - int(math.log2(bit)) for axis, bit in steps]
-    width = rows.shape[1]
-    block = rows.reshape((2,) * len(order) + (width,))
-    block = jnp.transpose(block, order + [len(order)]).reshape(rows.shape)
-    for axis, bit in steps:
+    return [
+        starts[axis] + total[axis] - 1 - int(math.log2(bit)) for axis, bit in butterfly_steps(sizes)
+    ]
+
+
+def reduce_shards(block, sizes):
+    for axis, bit in butterfly_steps(sizes):
         block = halve(block, axis, bit)
     snap_size = lax.axis_size("snap")
     bit = 1
@@ -122,6 +128,20 @@
         block = block + swap(block, "snap", bit)
         bit *= 2
     return block
+
+
+def shard_rows(grad, sizes, per):
+    order = shard_bit_order(sizes)
+    bits = len(order)
+    split = grad.reshape((9,) + (2,) * bits + (per * grad.shape[-1],))
+    moved = jnp.transpose(split, [1 + o for o in order] + [0, bits + 1])
+    return moved.reshape(2**bits, -1)
+
+
+def bias_rows(grad, sizes, per):
+    order = shard_bit_order(sizes)
+    split = grad.reshape((2,) * len(order) + (per,))
+    return jnp.transpose(split, order + [len(order)]).reshape(2 ** len(order), per)
 
 
 def _bits(size):
@@ -174,14 +194,10 @@
     per_b = hidden_channels // space_count
     rows = jnp.concatenate(
         [
-            jnp.moveaxis(grad_wa.reshape(3, 3, space_count, per_a, hidden_channels), 2, 0).reshape(
-                space_count, -1
-            ),
-            jnp.moveaxis(grad_wb.reshape(3, 3, space_count, per_b, channels), 2, 0).reshape(
-                space_count, -1
-            ),
-            grad_ba.reshape(space_count, per_b),
-            grad_bb.reshape(space_count, per_a),
+            shard_rows(grad_wa, sizes, per_a),
+            shard_rows(grad_wb, sizes, per_b),
+            bias_rows(grad_ba, sizes, per_b),
+            bias_rows(grad_bb, sizes, per_a),
         ],
         axis=1,
     )

time: 191 us -> 176 us (0.921)
  local copies, waits for them, and re-layouts: 33 us -> 21.7 us
  other arithmetic: 15.6 us -> 12.3 us
    transpose x3 -> x2, local copies, waits for them, and re-layouts: 5.32 us -> 1.01 us  [bias_rows(): jnp.transpose(split, order + [len(order)]).reshape(2 ** len(order), per)]
    concatenate x1, local copies, waits for them, and re-layouts: 6.75 us -> 2.52 us  [local(): jnp.concatenate([shard_rows(grad_wa, sizes, per_a), shard_rows(grad_wb, s...]
    reshape x4 -> x7, local copies, waits for them, and re-layouts: 6.99 us -> 4.22 us  [the longest x4 3.16 us: shard_rows(): split = grad.reshape((9,) + (2,) * bits + (per * grad.shape[-1],))]
    another operation x2 -> x6, other arithmetic: 2.34 us -> 0.35 us  [tap_sums(): return jnp.stack(tap_rows)]
    unnamed x40 -> x55, local copies, waits for them, and re-layouts: 5.85 us -> 7.5 us
  transfers between devices with their start and end apart: 13 -> 13, of which waited for: 13 -> 13; matrix products, arithmetic and copies ran while one was open for 4% -> 5% of each run, Pallas kernels for 0% -> 0%
where the time goes in v3:
time: 176 us; the launch traced here: 174 us
  waiting for transfers between devices  75.8 us (43%)
  starting transfers between devices  44.2 us (25%)
  local copies, waits for them, and re-layouts  21.7 us (12%)
  matrix products  18.7 us (11%)
  other arithmetic  12.3 us (7%)
  between operations  1.8 us (1%)
    ppermute x9, waiting for transfers between devices, swap(): return lax.ppermute(value, axis, [(i, i ^ bit) for i in range(size)])  58.4 us
    ppermute x9, starting transfers between devices, swap(): return lax.ppermute(value, axis, [(i, i ^ bit) for i in range(size)])  22.3 us
    ppermute x4, starting transfers between devices, from_behind(): lax.ppermute(array, axis, [(i, (i + by) % length) for i in range(length)])  21.9 us
    ppermute x4, waiting for transfers between devices, from_behind(): lax.ppermute(array, axis, [(i, (i + by) % length) for i in range(length)])  17.4 us
    dot_general x18, matrix products, tap_sums(): lax.dot_general(window, flat_out, (((0,), (0,)), ((), ())), preferred_ele...  11.7 us
    unnamed x55, local copies, waits for them, and re-layouts  7.5 us
    conv_general_dilated x4, matrix products, dilated(): lax.conv_general_dilated(padded[None], kernel, (1, 1), 'VALID', rhs_dilat...  7.03 us
  transfers between devices with their start and end apart: 13, of which 13 were waited for; matrix products, arithmetic and copies ran while one was open for 5% of the time, Pallas kernels for 0%

profile of v3, /device:TPU:6, one launch (start us, length us, event | category | flops | bytes accessed | tf_op | source)
XLA Modules:
  0.0 174.5 jit_solution(7921081296020059106)
XLA Ops:
  1.5 1.3 convert_reduce_fusion
  3.1 13.3 %collective-permute-start.1 = (bf16[32,4,640]{2,1,0:T(4,128)(2,1)S(1)}, bf16[32,4,640]{2,1,0:T(4,128)(2,1)S(1)}, u32[]{:S(2)}, u32[]{:S(2)}) collective-permute-start(bf16[32,4,640]{2,1,0:T(4,128)(2,1)S(1)} %get-tuple-element.30), channel_id=1, source_target_pairs={{0,127},{1,0},{2,1},{3,2},{4,3},{5,4},{6,5},{7,6},{8,7},{9,8},{10,... | collective-permute-start | bytes 491528 | tf_op jit(solution)/shard_map/ppermute | solution.py:21
  16.4 1.9 %collective-permute-start = (bf16[32,4,640]{2,1,0:T(4,128)(2,1)S(1)}, bf16[32,4,640]{2,1,0:T(4,128)(2,1)S(1)}, u32[]{:S(2)}, u32[]{:S(2)}) collective-permute-start(bf16[32,4,640]{2,1,0:T(4,128)(2,1)S(1)} %get-tuple-element.29), channel_id=1, source_target_pairs={{0,1},{1,2},{2,3},{3,4},{4,5},{5,6},{6,7},{7,8},{8,9},{9,10},{10,1... | collective-permute-start | bytes 491528 | tf_op jit(solution)/shard_map/ppermute | solution.py:21
  19.3 7.1 %collective-permute-done = bf16[32,4,640]{2,1,0:T(4,128)(2,1)S(1)} collective-permute-done((bf16[32,4,640]{2,1,0:T(4,128)(2,1)S(1)}, bf16[32,4,640]{2,1,0:T(4,128)(2,1)S(1)}, u32[]{:S(2)}, u32[]{:S(2)}) %collective-permute-start) | collective-permute-done | bytes 163872 | tf_op jit(solution)/shard_map/ppermute | solution.py:21
  26.6 1.9 %collective-permute-start.3 = (bf16[4,40,640]{2,1,0:T(8,128)(2,1)S(1)}, bf16[4,40,640]{2,1,0:T(8,128)(2,1)S(1)}, u32[]{:S(2)}, u32[]{:S(2)}) collective-permute-start(bf16[4,40,640]{2,1,0:T(8,128)(2,1)S(1)} %get-tuple-element.28), channel_id=1, source_target_pairs={{0,124},{1,125},{2,126},{3,127},{4,0},{5,1},{6,2},{7,3},{8,4},{9,5... | collective-permute-start | bytes 614408 | tf_op jit(solution)/shard_map/ppermute | solution.py:21
  29.4 4.8 %collective-permute-start.2 = (bf16[4,40,640]{2,1,0:T(8,128)(2,1)S(1)}, bf16[4,40,640]{2,1,0:T(8,128)(2,1)S(1)}, u32[]{:S(2)}, u32[]{:S(2)}) collective-permute-start(bf16[4,40,640]{2,1,0:T(8,128)(2,1)S(1)} %get-tuple-element.27), channel_id=1, source_target_pairs={{0,4},{1,5},{2,6},{3,7},{4,8},{5,9},{6,10},{7,11},{8,12},{9,13},{1... | collective-permute-start | bytes 614408 | tf_op jit(solution)/shard_map/ppermute | solution.py:21
  34.2 1.0 collective-permute-done.3
  35.3 8.5 %collective-permute-done.2 = bf16[4,40,640]{2,1,0:T(8,128)(2,1)S(1)} collective-permute-done((bf16[4,40,640]{2,1,0:T(8,128)(2,1)S(1)}, bf16[4,40,640]{2,1,0:T(8,128)(2,1)S(1)}, u32[]{:S(2)}, u32[]{:S(2)}) %collective-permute-start.2) | collective-permute-done | bytes 204832 | tf_op jit(solution)/shard_map/ppermute | solution.py:21
  43.7 3.3 %pad_maximum_fusion.2 = (bf16[40,40,256]{2,1,0:T(8,128)(2,1)S(1)}, bf16[40,40,256]{2,1,0:T(8,128)(2,1)S(1)}) fusion(bf16[4,40,640]{2,1,0:T(8,128)(2,1)S(1)} %broadcast_select_fusion, bf16[4,40,640]{2,1,0:T(8,128)(2,1)S(1)} %broadcast_select_fusion.1, bf16[32,4,640]{2,1,0:T(4,128)(2,1)S(1)} %broadcast_select_fusion.2, ...), kind=kLoop, calls=%fused_computation.59 | loop fusion | flops 11468800 | bytes 3686400 | tf_op jit(solution)/shard_map/concatenate | solution.py:89
  49.1 1.9 %fusion.19 = f32[36,8,5,128]{3,1,2,0:T(8,128)S(1)} fusion(bf16[3,3,128,256]{3,2,1,0:T(8,128)(2,1)S(1)} %copy-done.21, bf16[40,1,7,4,256]{4,2,3,0,1:T(8,128)(2,1)S(1)} %slice.164, bf16[40,1,8,5,256]{4,2,3,0,1:T(8,128)(2,1)S(1)} %copy.62, pred[8,5]{0,1:T(8,128)(4,1)S(1)} %copy-done.24), kind=kOutput, calls=%fused_computation.25 | convolution fusion | flops 853954560 | bytes 2719784 | tf_op jit(solution)/shard_map/conv_general_dilated | solution.py:35
  51.7 3.1 %fusion.35 = (f32[36,8,5,128]{3,1,2,0:T(8,128)}, f32[36,8,5,128]{3,1,2,0:T(8,128)}, f32[36,8,5,128]{3,1,2,0:T(8,128)S(1)}) fusion(f32[128]{0:T(128)S(1)} %copy-done.20, bf16[3,3,256,128]{3,2,1,0:T(8,128)(2,1)S(1)} %copy-done, bf16[40,1,7,4,256]{4,2,3,0,1:T(8,128)(2,1)S(1)} %slice.160, bf16[40,1,8,5,256]{4,2,3,0,1:T(8,128)(2,1)S(1)} %copy.55, ...), kind=kOutput, calls=%fused_computation.69 | convolution fusion | flops 855982080 | bytes 4194856 | tf_op jit(solution)/shard_map/conv_general_dilated | solution.py:35
  59.2 0.9 convolution_bitcast_fusion
  60.2 0.9 convolution_bitcast_fusion.1
  61.1 0.9 convolution_bitcast_fusion.2
  62.0 0.9 convolution_bitcast_fusion.6
  63.0 0.9 convolution_bitcast_fusion.7
  64.8 0.9 convolution_bitcast_fusion.3
  65.8 0.9 convolution_bitcast_fusion.4
  68.6 1.0 copy.75
  69.6 2.0 %copy.89 = f32[16,8,9,256]{3,1,2,0:T(8,128)} copy(f32[16,8,9,256]{3,2,1,0:T(8,128)S(1)} %bitcast.205) | data formatting | bytes 2359296
  73.4 2.0 %copy.90 = f32[16,8,9,256]{3,1,2,0:T(8,128)} copy(f32[16,8,9,256]{3,2,1,0:T(8,128)S(1)} %bitcast.206) | data formatting | bytes 2359296
  76.5 2.5 %concatenate.35 = f32[128,4611]{1,0:T(8,128)S(1)} concatenate(f32[128,2304]{1,0:T(8,128)} %bitcast.207, f32[128,2304]{1,0:T(8,128)} %bitcast.208, f32[128,1]{1,0:T(8,128)} %reshape.197, f32[128,2]{1,0:T(8,128)} %bitcast.220), dimensions={1} | concatenate | bytes 4721664 | tf_op jit(solution)/shard_map/concatenate | solution.py:195
  79.1 1.1 pad_dynamic-slice_fusion
  80.2 1.9 %collective-permute-start.4 = (f32[64,4736]{1,0:T(8,128)}, f32[64,4736]{1,0:T(8,128)}, u32[]{:S(2)}, u32[]{:S(2)}) collective-permute-start(f32[64,4736]{1,0:T(8,128)} %pad_dynamic-slice_fusion), channel_id=1, source_target_pairs={{0,1},{1,0},{2,3},{3,2},{4,5},{5,4},{6,7},{7,6},{8,9},{9,8},{10,11... | collective-permute-start | bytes 3637256 | tf_op jit(solution)/shard_map/ppermute | solution.py:94
  82.1 3.2 %collective-permute-done.4 = f32[64,4736]{1,0:T(8,128)} collective-permute-done((f32[64,4736]{1,0:T(8,128)}, f32[64,4736]{1,0:T(8,128)}, u32[]{:S(2)}, u32[]{:S(2)}) %collective-permute-start.4) | collective-permute-done | bytes 1212448 | tf_op jit(solution)/shard_map/ppermute | solution.py:94
  85.3 1.4 fusion.18
  86.7 1.0 copy-done.4
  87.8 4.7 %collective-permute-start.5 = (f32[32,4736]{1,0:T(8,128)S(1)}, f32[32,4736]{1,0:T(8,128)S(1)}, u32[]{:S(2)}, u32[]{:S(2)}) collective-permute-start(f32[32,4736]{1,0:T(8,128)S(1)} %constant_dynamic-slice_fusion.5), channel_id=1, source_target_pairs={{0,2},{2,0},{4,6},{6,4},{8,10},{10,8},{12,14},{14,12},{1,3},{3,1},... | collective-permute-start | bytes 1818632 | tf_op jit(solution)/shard_map/ppermute | solution.py:94
  92.6 13.9 %collective-permute-done.5 = f32[32,4736]{1,0:T(8,128)S(1)} collective-permute-done((f32[32,4736]{1,0:T(8,128)S(1)}, f32[32,4736]{1,0:T(8,128)S(1)}, u32[]{:S(2)}, u32[]{:S(2)}) %collective-permute-start.5) | collective-permute-done | bytes 606240 | tf_op jit(solution)/shard_map/ppermute | solution.py:94
  106.5 1.2 dynamic-slice_add_fusion
  107.7 1.9 %collective-permute-start.6 = (f32[16,4736]{1,0:T(8,128)S(1)}, f32[16,4736]{1,0:T(8,128)S(1)}, u32[]{:S(2)}, u32[]{:S(2)}) collective-permute-start(f32[16,4736]{1,0:T(8,128)S(1)} %constant_dynamic-slice_fusion.4), channel_id=1, source_target_pairs={{0,4},{2,6},{4,0},{6,2},{8,12},{10,14},{12,8},{14,10},{1,5},{3,7},... | collective-permute-start | bytes 909320 | tf_op jit(solution)/shard_map/ppermute | solution.py:94
  110.0 15.7 %collective-permute-done.6 = f32[16,4736]{1,0:T(8,128)S(1)} collective-permute-done((f32[16,4736]{1,0:T(8,128)S(1)}, f32[16,4736]{1,0:T(8,128)S(1)}, u32[]{:S(2)}, u32[]{:S(2)}) %collective-permute-start.6) | collective-permute-done | bytes 303136 | tf_op jit(solution)/shard_map/ppermute | solution.py:94
  125.8 1.9 %collective-permute-start.7 = (f32[8,4736]{1,0:T(8,128)S(1)}, f32[8,4736]{1,0:T(8,128)S(1)}, u32[]{:S(2)}, u32[]{:S(2)}) collective-permute-start(f32[8,4736]{1,0:T(8,128)S(1)} %constant_dynamic-slice_fusion.3), channel_id=1, source_target_pairs={{0,8},{2,10},{4,12},{6,14},{8,0},{10,2},{12,4},{14,6},{1,9},{3,11}... | collective-permute-start | bytes 454664 | tf_op jit(solution)/shard_map/ppermute | solution.py:94
  128.2 8.9 %collective-permute-done.7 = f32[8,4736]{1,0:T(8,128)S(1)} collective-permute-done((f32[8,4736]{1,0:T(8,128)S(1)}, f32[8,4736]{1,0:T(8,128)S(1)}, u32[]{:S(2)}, u32[]{:S(2)}) %collective-permute-start.7) | collective-permute-done | bytes 151584 | tf_op jit(solution)/shard_map/ppermute | solution.py:94
  137.2 1.9 %collective-permute-start.8 = (f32[4,4736]{1,0:T(4,128)S(1)}, f32[4,4736]{1,0:T(4,128)S(1)}, u32[]{:S(2)}, u32[]{:S(2)}) collective-permute-start(f32[4,4736]{1,0:T(4,128)S(1)} %constant_dynamic-slice_fusion.2), channel_id=1, source_target_pairs={{0,16},{16,0},{32,48},{48,32},{64,80},{80,64},{96,112},{112,96},{1... | collective-permute-start | bytes 227336 | tf_op jit(solution)/shard_map/ppermute | solution.py:94
  139.1 1.0 convolution_select_fusion.1
  140.6 2.8 %collective-permute-done.8 = f32[4,4736]{1,0:T(4,128)S(1)} collective-permute-done((f32[4,4736]{1,0:T(4,128)S(1)}, f32[4,4736]{1,0:T(4,128)S(1)}, u32[]{:S(2)}, u32[]{:S(2)}) %collective-permute-start.8) | collective-permute-done | bytes 75808 | tf_op jit(solution)/shard_map/ppermute | solution.py:94
  143.5 1.9 %collective-permute-start.9 = (f32[2,4736]{1,0:T(2,128)S(1)}, f32[2,4736]{1,0:T(2,128)S(1)}, u32[]{:S(2)}, u32[]{:S(2)}) collective-permute-start(f32[2,4736]{1,0:T(2,128)S(1)} %constant_dynamic-slice_fusion.1), channel_id=1, source_target_pairs={{0,32},{16,48},{32,0},{48,16},{64,96},{80,112},{96,64},{112,80},{1... | collective-permute-start | bytes 113672 | tf_op jit(solution)/shard_map/ppermute | solution.py:94
  146.1 4.2 %collective-permute-done.9 = f32[2,4736]{1,0:T(2,128)S(1)} collective-permute-done((f32[2,4736]{1,0:T(2,128)S(1)}, f32[2,4736]{1,0:T(2,128)S(1)}, u32[]{:S(2)}, u32[]{:S(2)}) %collective-permute-start.9) | collective-permute-done | bytes 37920 | tf_op jit(solution)/shard_map/ppermute | solution.py:94
  150.3 1.9 %collective-permute-start.10 = (f32[1,4736]{1,0:T(1,128)S(1)}, f32[1,4736]{1,0:T(1,128)S(1)}, u32[]{:S(2)}, u32[]{:S(2)}) collective-permute-start(f32[1,4736]{1,0:T(1,128)S(1)} %constant_dynamic-slice_fusion), channel_id=1, source_target_pairs={{0,64},{16,80},{32,96},{48,112},{64,0},{80,16},{96,32},{112,48},{1... | collective-permute-start | bytes 56840 | tf_op jit(solution)/shard_map/ppermute | solution.py:94
  152.8 7.1 %collective-permute-done.10 = f32[1,4736]{1,0:T(1,128)S(1)} collective-permute-done((f32[1,4736]{1,0:T(1,128)S(1)}, f32[1,4736]{1,0:T(1,128)S(1)}, u32[]{:S(2)}, u32[]{:S(2)}) %collective-permute-start.10) | collective-permute-done | bytes 18976 | tf_op jit(solution)/shard_map/ppermute | solution.py:94
  159.9 2.7 %collective-permute-start.11 = (f32[1,4736]{1,0:T(1,128)S(1)}, f32[1,4736]{1,0:T(1,128)S(1)}, u32[]{:S(2)}, u32[]{:S(2)}) collective-permute-start(f32[1,4736]{1,0:T(1,128)S(1)} %dynamic-slice_add_fusion.5), channel_id=1, source_target_pairs={{0,128},{128,0},{256,384},{384,256},{1,129},{129,1},{257,385},{385... | collective-permute-start | bytes 56840 | tf_op jit(solution)/shard_map/ppermute | solution.py:94
  162.6 1.1 convolution_select_fusion
  164.3 1.3 collective-permute-done.11
  165.6 3.3 %collective-permute-start.12 = (f32[1,4736]{1,0:T(1,128)S(1)}, f32[1,4736]{1,0:T(1,128)S(1)}, u32[]{:S(2)}, u32[]{:S(2)}) collective-permute-start(f32[1,4736]{1,0:T(1,128)S(1)} %add.213), channel_id=1, source_target_pairs={{0,256},{128,384},{256,0},{384,128},{1,257},{129,385},{257,1},{385... | collective-permute-start | bytes 56840 | tf_op jit(solution)/shard_map/ppermute | solution.py:94
  168.9 1.4 fusion.27
  170.3 1.1 copy.80
  171.4 1.3 collective-permute-done.12
  (133 shorter events, 20.8 us)
Async XLA Ops:
  0.6 50.6 %copy-start = (bf16[3,3,256,128]{3,2,1,0:T(8,128)(2,1)S(1)}, bf16[3,3,256,128]{3,2,1,0:T(8,128)(2,1)}, u32[]{:S(2)}) copy-start(bf16[3,3,256,128]{3,2,1,0:T(8,128)(2,1)} %param.10) | copy-start | bytes 1769476
  0.6 2.3 %copy-start.1 = (bf16[1,1,32,32,256]{4,3,2,1,0:T(8,128)(2,1)S(1)}, bf16[1,1,32,32,256]{4,3,2,1,0:T(8,128)(2,1)}, u32[]{:S(2)}) copy-start(bf16[1,1,32,32,256]{4,3,2,1,0:T(8,128)(2,1)} %param.7) | copy-start | bytes 1572868
  3.1 16.1 %collective-permute-start.1 = (bf16[32,4,640]{2,1,0:T(4,128)(2,1)S(1)}, bf16[32,4,640]{2,1,0:T(4,128)(2,1)S(1)}, u32[]{:S(2)}, u32[]{:S(2)}) collective-permute-start(bf16[32,4,640]{2,1,0:T(4,128)(2,1)S(1)} %get-tuple-element.30), channel_id=1, source_target_pairs={{0,127},{1,0},{2,1},{3,2},{4,3},{5,4},{6,5},{7,6},{8,7},{9,8},{10,... | collective-permute-start | bytes 491528 | tf_op jit(solution)/shard_map/ppermute | solution.py:21
  16.4 10.0 %collective-permute-start = (bf16[32,4,640]{2,1,0:T(4,128)(2,1)S(1)}, bf16[32,4,640]{2,1,0:T(4,128)(2,1)S(1)}, u32[]{:S(2)}, u32[]{:S(2)}) collective-permute-start(bf16[32,4,640]{2,1,0:T(4,128)(2,1)S(1)} %get-tuple-element.29), channel_id=1, source_target_pairs={{0,1},{1,2},{2,3},{3,4},{4,5},{5,6},{6,7},{7,8},{8,9},{9,10},{10,1... | collective-permute-start | bytes 491528 | tf_op jit(solution)/shard_map/ppermute | solution.py:21
  26.6 8.7 %collective-permute-start.3 = (bf16[4,40,640]{2,1,0:T(8,128)(2,1)S(1)}, bf16[4,40,640]{2,1,0:T(8,128)(2,1)S(1)}, u32[]{:S(2)}, u32[]{:S(2)}) collective-permute-start(bf16[4,40,640]{2,1,0:T(8,128)(2,1)S(1)} %get-tuple-element.28), channel_id=1, source_target_pairs={{0,124},{1,125},{2,126},{3,127},{4,0},{5,1},{6,2},{7,3},{8,4},{9,5... | collective-permute-start | bytes 614408 | tf_op jit(solution)/shard_map/ppermute | solution.py:21
  29.4 14.3 %collective-permute-start.2 = (bf16[4,40,640]{2,1,0:T(8,128)(2,1)S(1)}, bf16[4,40,640]{2,1,0:T(8,128)(2,1)S(1)}, u32[]{:S(2)}, u32[]{:S(2)}) collective-permute-start(bf16[4,40,640]{2,1,0:T(8,128)(2,1)S(1)} %get-tuple-element.27), channel_id=1, source_target_pairs={{0,4},{1,5},{2,6},{3,7},{4,8},{5,9},{6,10},{7,11},{8,12},{9,13},{1... | collective-permute-start | bytes 614408 | tf_op jit(solution)/shard_map/ppermute | solution.py:21
  47.3 7.7 %copy-start.14 = (f32[36,36]{1,0:T(8,128)}, f32[36,36]{1,0:T(8,128)S(1)}, u32[]{:S(2)}) copy-start(f32[36,36]{1,0:T(8,128)S(1)} %convert_reduce_fusion.1) | copy-start | bytes 15556
  48.0 1.1 copy-start.21
  48.0 1.1 copy-start.24
  51.0 0.7 copy-start.20
  51.7 3.7 %copy-start.2 = (f32[36,1,36,128]{3,0,2,1:T(8,128)}, f32[36,1,36,128]{3,0,2,1:T(8,128)S(1)}, u32[]{:S(2)}) copy-start(f32[36,1,36,128]{3,0,2,1:T(8,128)S(1)} %slice.165) | copy-start | bytes 1990660
  69.5 2.1 %copy-start.12 = (f32[1,128,256]{2,1,0:T(8,128)S(1)}, f32[1,128,256]{2,1,0:T(8,128)}, u32[]{:S(2)}) copy-start(f32[1,128,256]{2,1,0:T(8,128)} %convolution_bitcast_fusion.1) | copy-start | bytes 393220
  69.6 2.1 %copy-start.13 = (f32[1,128,256]{2,1,0:T(8,128)S(1)}, f32[1,128,256]{2,1,0:T(8,128)}, u32[]{:S(2)}) copy-start(f32[1,128,256]{2,1,0:T(8,128)} %convolution_bitcast_fusion.2) | copy-start | bytes 393220
  69.6 2.1 %copy-start.18 = (f32[1,128,256]{2,1,0:T(8,128)S(1)}, f32[1,128,256]{2,1,0:T(8,128)}, u32[]{:S(2)}) copy-start(f32[1,128,256]{2,1,0:T(8,128)} %convolution_bitcast_fusion) | copy-start | bytes 393220
  69.6 2.1 %copy-start.8 = (f32[1,128,256]{2,1,0:T(8,128)S(1)}, f32[1,128,256]{2,1,0:T(8,128)}, u32[]{:S(2)}) copy-start(f32[1,128,256]{2,1,0:T(8,128)} %convolution_bitcast_fusion.7) | copy-start | bytes 393220
  69.6 2.1 %copy-start.9 = (f32[1,128,256]{2,1,0:T(8,128)S(1)}, f32[1,128,256]{2,1,0:T(8,128)}, u32[]{:S(2)}) copy-start(f32[1,128,256]{2,1,0:T(8,128)} %convolution_bitcast_fusion.8) | copy-start | bytes 393220
  69.6 2.1 %copy-start.10 = (f32[1,128,256]{2,1,0:T(8,128)S(1)}, f32[1,128,256]{2,1,0:T(8,128)}, u32[]{:S(2)}) copy-start(f32[1,128,256]{2,1,0:T(8,128)} %convolution_bitcast_fusion.4) | copy-start | bytes 393220
  69.6 2.1 %copy-start.11 = (f32[1,128,256]{2,1,0:T(8,128)S(1)}, f32[1,128,256]{2,1,0:T(8,128)}, u32[]{:S(2)}) copy-start(f32[1,128,256]{2,1,0:T(8,128)} %convolution_bitcast_fusion.5) | copy-start | bytes 393220
  69.6 2.1 %copy-start.16 = (f32[1,128,256]{2,1,0:T(8,128)S(1)}, f32[1,128,256]{2,1,0:T(8,128)}, u32[]{:S(2)}) copy-start(f32[1,128,256]{2,1,0:T(8,128)} %convolution_bitcast_fusion.6) | copy-start | bytes 393220
  69.6 2.1 %copy-start.17 = (f32[1,128,256]{2,1,0:T(8,128)S(1)}, f32[1,128,256]{2,1,0:T(8,128)}, u32[]{:S(2)}) copy-start(f32[1,128,256]{2,1,0:T(8,128)} %convolution_bitcast_fusion.3) | copy-start | bytes 393220
  80.2 5.1 %collective-permute-start.4 = (f32[64,4736]{1,0:T(8,128)}, f32[64,4736]{1,0:T(8,128)}, u32[]{:S(2)}, u32[]{:S(2)}) collective-permute-start(f32[64,4736]{1,0:T(8,128)} %pad_dynamic-slice_fusion), channel_id=1, source_target_pairs={{0,1},{1,0},{2,3},{3,2},{4,5},{5,4},{6,7},{7,6},{8,9},{9,8},{10,11... | collective-permute-start | bytes 3637256 | tf_op jit(solution)/shard_map/ppermute | solution.py:94
  86.7 1.1 copy-start.4
  87.8 22.0 %copy-start.15 = (f32[36,36]{1,0:T(8,128)S(1)}, f32[36,36]{1,0:T(8,128)}, u32[]{:S(2)}) copy-start(f32[36,36]{1,0:T(8,128)} %copy-done.14) | copy-start | bytes 15556
  87.8 22.1 %copy-start.7 = (f32[36,8,5,128]{3,1,2,0:T(8,128)S(1)}, f32[36,8,5,128]{3,1,2,0:T(8,128)}, u32[]{:S(2)}) copy-start(f32[36,8,5,128]{3,1,2,0:T(8,128)} %get-tuple-element.32) | copy-start | bytes 2211844
  87.8 18.7 %collective-permute-start.5 = (f32[32,4736]{1,0:T(8,128)S(1)}, f32[32,4736]{1,0:T(8,128)S(1)}, u32[]{:S(2)}, u32[]{:S(2)}) collective-permute-start(f32[32,4736]{1,0:T(8,128)S(1)} %constant_dynamic-slice_fusion.5), channel_id=1, source_target_pairs={{0,2},{2,0},{4,6},{6,4},{8,10},{10,8},{12,14},{14,12},{1,3},{3,1},... | collective-permute-start | bytes 1818632 | tf_op jit(solution)/shard_map/ppermute | solution.py:94
  107.7 18.0 %collective-permute-start.6 = (f32[16,4736]{1,0:T(8,128)S(1)}, f32[16,4736]{1,0:T(8,128)S(1)}, u32[]{:S(2)}, u32[]{:S(2)}) collective-permute-start(f32[16,4736]{1,0:T(8,128)S(1)} %constant_dynamic-slice_fusion.4), channel_id=1, source_target_pairs={{0,4},{2,6},{4,0},{6,2},{8,12},{10,14},{12,8},{14,10},{1,5},{3,7},... | collective-permute-start | bytes 909320 | tf_op jit(solution)/shard_map/ppermute | solution.py:94
  125.8 11.3 %collective-permute-start.7 = (f32[8,4736]{1,0:T(8,128)S(1)}, f32[8,4736]{1,0:T(8,128)S(1)}, u32[]{:S(2)}, u32[]{:S(2)}) collective-permute-start(f32[8,4736]{1,0:T(8,128)S(1)} %constant_dynamic-slice_fusion.3), channel_id=1, source_target_pairs={{0,8},{2,10},{4,12},{6,14},{8,0},{10,2},{12,4},{14,6},{1,9},{3,11}... | collective-permute-start | bytes 454664 | tf_op jit(solution)/shard_map/ppermute | solution.py:94
  128.0 11.1 %copy-start.22 = (bf16[3,3,128,256]{3,2,1,0:T(8,128)(2,1)S(1)}, bf16[3,3,128,256]{3,2,1,0:T(8,128)(2,1)}, u32[]{:S(2)}) copy-start(bf16[3,3,128,256]{3,2,1,0:T(8,128)(2,1)} %param.12) | copy-start | bytes 1769476
  128.0 11.1 %copy-start.23 = (pred[8,5]{0,1:T(8,128)(4,1)S(1)}, pred[8,5]{0,1:T(8,128)(4,1)}, u32[]{:S(2)}) copy-start(pred[8,5]{0,1:T(8,128)(4,1)} %constant.182) | copy-start | bytes 124
  137.2 6.3 %collective-permute-start.8 = (f32[4,4736]{1,0:T(4,128)S(1)}, f32[4,4736]{1,0:T(4,128)S(1)}, u32[]{:S(2)}, u32[]{:S(2)}) collective-permute-start(f32[4,4736]{1,0:T(4,128)S(1)} %constant_dynamic-slice_fusion.2), channel_id=1, source_target_pairs={{0,16},{16,0},{32,48},{48,32},{64,80},{80,64},{96,112},{112,96},{1... | collective-permute-start | bytes 227336 | tf_op jit(solution)/shard_map/ppermute | solution.py:94
  140.1 5.3 %copy-start.19 = (f32[256]{0:T(256)S(1)}, f32[256]{0:T(256)}, u32[]{:S(2)}) copy-start(f32[256]{0:T(256)} %param.13) | copy-start | bytes 3076
  140.6 5.3 %copy-start.6 = (f32[36,8,5,128]{3,1,2,0:T(8,128)S(1)}, f32[36,8,5,128]{3,1,2,0:T(8,128)}, u32[]{:S(2)}) copy-start(f32[36,8,5,128]{3,1,2,0:T(8,128)} %get-tuple-element.31) | copy-start | bytes 2211844
  143.5 6.8 %collective-permute-start.9 = (f32[2,4736]{1,0:T(2,128)S(1)}, f32[2,4736]{1,0:T(2,128)S(1)}, u32[]{:S(2)}, u32[]{:S(2)}) collective-permute-start(f32[2,4736]{1,0:T(2,128)S(1)} %constant_dynamic-slice_fusion.1), channel_id=1, source_target_pairs={{0,32},{16,48},{32,0},{48,16},{64,96},{80,112},{96,64},{112,80},{1... | collective-permute-start | bytes 113672 | tf_op jit(solution)/shard_map/ppermute | solution.py:94
  145.8 6.4 %copy-start.3 = (f32[36,1,36,128]{3,0,2,1:T(8,128)S(1)}, f32[36,1,36,128]{3,0,2,1:T(8,128)}, u32[]{:S(2)}) copy-start(f32[36,1,36,128]{3,0,2,1:T(8,128)} %copy-done.2) | copy-start | bytes 1990660
  150.3 9.6 %collective-permute-start.10 = (f32[1,4736]{1,0:T(1,128)S(1)}, f32[1,4736]{1,0:T(1,128)S(1)}, u32[]{:S(2)}, u32[]{:S(2)}) collective-permute-start(f32[1,4736]{1,0:T(1,128)S(1)} %constant_dynamic-slice_fusion), channel_id=1, source_target_pairs={{0,64},{16,80},{32,96},{48,112},{64,0},{80,16},{96,32},{112,48},{1... | collective-permute-start | bytes 56840 | tf_op jit(solution)/shard_map/ppermute | solution.py:94
  159.9 5.7 %collective-permute-start.11 = (f32[1,4736]{1,0:T(1,128)S(1)}, f32[1,4736]{1,0:T(1,128)S(1)}, u32[]{:S(2)}, u32[]{:S(2)}) collective-permute-start(f32[1,4736]{1,0:T(1,128)S(1)} %dynamic-slice_add_fusion.5), channel_id=1, source_target_pairs={{0,128},{128,0},{256,384},{384,256},{1,129},{129,1},{257,385},{385... | collective-permute-start | bytes 56840 | tf_op jit(solution)/shard_map/ppermute | solution.py:94
  164.1 4.8 %copy-start.5 = (bf16[1,1,32,32,256]{4,3,2,1,0:T(8,128)(2,1)S(1)}, bf16[1,1,32,32,256]{4,3,2,1,0:T(8,128)(2,1)}, u32[]{:S(2)}) copy-start(bf16[1,1,32,32,256]{4,3,2,1,0:T(8,128)(2,1)} %param.9) | copy-start | bytes 1572868
  165.6 7.2 %collective-permute-start.12 = (f32[1,4736]{1,0:T(1,128)S(1)}, f32[1,4736]{1,0:T(1,128)S(1)}, u32[]{:S(2)}, u32[]{:S(2)}) collective-permute-start(f32[1,4736]{1,0:T(1,128)S(1)} %add.213), channel_id=1, source_target_pairs={{0,256},{128,384},{256,0},{384,128},{1,257},{129,385},{257,1},{385... | collective-permute-start | bytes 56840 | tf_op jit(solution)/shard_map/ppermute | solution.py:94

commit v4 on v3

--- a/solution.py
+++ b/solution.py
@@ -102,26 +102,32 @@
     return keep + swap(send, axis, bit)
 
 
-def butterfly_steps(sizes):
-    steps = [("core", b) for b in _bits(sizes[2])]
-    steps += [("y", b) for b in _bits(sizes[1])]
-    steps += [("z", b) for b in _bits(sizes[0])]
-    return steps
-
-
-def shard_bit_order(sizes):
+def butterfly_steps(sizes, z_first):
+    core = [("core", b) for b in _bits(sizes[2])]
+    y = [("y", b) for b in _bits(sizes[1])]
+    z = [("z", b) for b in _bits(sizes[0])]
+    return core + (z + y if z_first else y + z)
+
+
+def shard_bit_order(sizes, z_first):
     names = ("z", "y", "core")
     counts = [len(_bits(size)) for size in sizes]
     starts = dict(zip(names, np.cumsum([0] + counts[:-1]).tolist()))
     total = dict(zip(names, counts))
     return [
-        starts[axis] + total[axis] - 1 - int(math.log2(bit)) for axis, bit in butterfly_steps(sizes)
+        starts[axis] + total[axis] - 1 - int(math.log2(bit))
+        for axis, bit in butterfly_steps(sizes, z_first)
     ]
 
 
-def reduce_shards(block, sizes):
-    for axis, bit in butterfly_steps(sizes):
-        block = halve(block, axis, bit)
+def reduce_shards(blocks, sizes):
+    first, second = blocks
+    for (axis_a, bit_a), (axis_b, bit_b) in zip(
+        butterfly_steps(sizes, False), butterfly_steps(sizes, True)
+    ):
+        first = halve(first, axis_a, bit_a)
+        second = halve(second, axis_b, bit_b)
+    block = jnp.concatenate([first, second], axis=1)
     snap_size = lax.axis_size("snap")
     bit = 1
     while bit < snap_size:
@@ -130,18 +136,21 @@
     return block
 
 
-def shard_rows(grad, sizes, per):
-    order = shard_bit_order(sizes)
+def shard_rows(grad, order, per):
     bits = len(order)
     split = grad.reshape((9,) + (2,) * bits + (per * grad.shape[-1],))
     moved = jnp.transpose(split, [1 + o for o in order] + [0, bits + 1])
     return moved.reshape(2**bits, -1)
 
 
-def bias_rows(grad, sizes, per):
-    order = shard_bit_order(sizes)
+def bias_rows(grad, order, per):
     split = grad.reshape((2,) * len(order) + (per,))
     return jnp.transpose(split, order + [len(order)]).reshape(2 ** len(order), per)
+
+
+def lane_pad(rows):
+    width = rows.shape[1]
+    return jnp.pad(rows, ((0, 0), (0, -(-width // 128) * 128 - width)))
 
 
 def _bits(size):
@@ -192,28 +201,29 @@
     grad_ba = jnp.sum(g_pre_inner.astype(jnp.float32), axis=(0, 1))
     per_a = channels // space_count
     per_b = hidden_channels // space_count
-    rows = jnp.concatenate(
-        [
-            shard_rows(grad_wa, sizes, per_a),
-            shard_rows(grad_wb, sizes, per_b),
-            bias_rows(grad_ba, sizes, per_b),
-            bias_rows(grad_bb, sizes, per_a),
-        ],
-        axis=1,
-    )
-    width = rows.shape[1]
-    padded_width = -(-width // 128) * 128
-    rows = jnp.pad(rows, ((0, 0), (0, padded_width - width)))
-    mine = reduce_shards(rows, sizes)[0] * scale
-    cut_a = 9 * per_a * hidden_channels
-    cut_b = cut_a + 9 * per_b * channels
+    order_a = shard_bit_order(sizes, False)
+    order_b = shard_bit_order(sizes, True)
+    rows_a = lane_pad(
+        jnp.concatenate(
+            [shard_rows(grad_wa, order_a, per_a), bias_rows(grad_ba, order_a, per_b)], axis=1
+        )
+    )
+    rows_b = lane_pad(
+        jnp.concatenate(
+            [shard_rows(grad_wb, order_b, per_b), bias_rows(grad_bb, order_b, per_a)], axis=1
+        )
+    )
+    mine = reduce_shards((rows_a, rows_b), sizes)[0] * scale
+    size_a = 9 * per_a * hidden_channels
+    size_b = 9 * per_b * channels
+    base_b = rows_a.shape[1]
     return (
         field_out[None, None],
         g_input[None, None],
-        mine[:cut_a].reshape(3, 3, per_a, hidden_channels),
-        mine[cut_a:cut_b].reshape(3, 3, per_b, channels),
-        mine[cut_b : cut_b + per_b],
-        mine[cut_b + per_b : cut_b + per_b + per_a],
+        mine[:size_a].reshape(3, 3, per_a, hidden_channels),
+        mine[base_b : base_b + size_b].reshape(3, 3, per_b, channels),
+        mine[size_a : size_a + per_b],
+        mine[base_b + size_b : base_b + size_b + per_a],
     )
 
 

time: 176 us -> 171 us (0.972)
  waiting for transfers between devices: 75.8 us -> 33.5 us
  starting transfers between devices: 44.2 us -> 79.8 us
  other arithmetic: 12.3 us -> 15.4 us
    ppermute x9 -> x16, waiting for transfers between devices: 58.4 us -> 24.2 us  [swap(): return lax.ppermute(value, axis, [(i, i ^ bit) for i in range(size)])]
    ppermute x9 -> x16, starting transfers between devices: 22.3 us -> 54.5 us  [swap(): return lax.ppermute(value, axis, [(i, i ^ bit) for i in range(size)])]
    ppermute x4, waiting for transfers between devices: 17.4 us -> 9.34 us  [from_behind(): lax.ppermute(array, axis, [(i, (i + by) % length) for i in range(length)])]
    another operation x6, other arithmetic: 0.35 us -> 5.47 us  [tap_sums(): return jnp.stack(tap_rows)]
    reshape x4, local copies, waits for them, and re-layouts: 3.16 us -> 7.64 us  [shard_rows(): split = grad.reshape((9,) + (2,) * bits + (per * grad.shape[-1],))]
    ppermute x4, starting transfers between devices: 21.9 us -> 25.3 us  [from_behind(): lax.ppermute(array, axis, [(i, (i + by) % length) for i in range(length)])]
    unnamed x55 -> x33, local copies, waits for them, and re-layouts: 7.5 us -> 4.46 us
    concatenate x1 -> x0, local copies, waits for them, and re-layouts: 2.52 us -> none  [local(): jnp.concatenate([shard_rows(grad_wa, sizes, per_a), shard_rows(grad_wb, s...]
  transfers between devices with their start and end apart: 13 -> 20, of which waited for: 13 -> 13; matrix products, arithmetic and copies ran while one was open for 5% -> 5% of each run, Pallas kernels for 0% -> 0%
where the time goes in v4:
time: 171 us; the launch traced here: 170 us
  starting transfers between devices  79.8 us (47%)
  waiting for transfers between devices  33.5 us (20%)
  local copies, waits for them, and re-layouts  21.5 us (13%)
  matrix products  17.6 us (10%)
  other arithmetic  15.4 us (9%)
  between operations  1.91 us (1%)
    ppermute x16, starting transfers between devices, swap(): return lax.ppermute(value, axis, [(i, i ^ bit) for i in range(size)])  54.5 us
    ppermute x4, starting transfers between devices, from_behind(): lax.ppermute(array, axis, [(i, (i + by) % length) for i in range(length)])  25.3 us
    ppermute x16, waiting for transfers between devices, swap(): return lax.ppermute(value, axis, [(i, i ^ bit) for i in range(size)])  24.2 us
    dot_general x18, matrix products, tap_sums(): lax.dot_general(window, flat_out, (((0,), (0,)), ((), ())), preferred_ele...  11.6 us
    ppermute x4, waiting for transfers between devices, from_behind(): lax.ppermute(array, axis, [(i, (i + by) % length) for i in range(length)])  9.34 us
    reshape x4, local copies, waits for them, and re-layouts, shard_rows(): split = grad.reshape((9,) + (2,) * bits + (per * grad.shape[-1],))  7.64 us
    conv_general_dilated x4, matrix products, dilated(): lax.conv_general_dilated(padded[None], kernel, (1, 1), 'VALID', rhs_dilat...  5.96 us
    another operation x6, other arithmetic, tap_sums(): return jnp.stack(tap_rows)  5.47 us
  transfers between devices with their start and end apart: 20, of which 13 were waited for; matrix products, arithmetic and copies ran while one was open for 5% of the time, Pallas kernels for 0%

profile of v4, /device:TPU:6, one launch (start us, length us, event | category | flops | bytes accessed | tf_op | source)
XLA Modules:
  0.0 169.7 jit_solution(11108765021145145304)
XLA Ops:
  1.5 1.3 convert_reduce_fusion
  3.1 1.9 %collective-permute-start = (bf16[32,4,640]{2,1,0:T(4,128)(2,1)S(1)}, bf16[32,4,640]{2,1,0:T(4,128)(2,1)S(1)}, u32[]{:S(2)}, u32[]{:S(2)}) collective-permute-start(bf16[32,4,640]{2,1,0:T(4,128)(2,1)S(1)} %get-tuple-element.30), channel_id=1, source_target_pairs={{0,1},{1,2},{2,3},{3,4},{4,5},{5,6},{6,7},{7,8},{8,9},{9,10},{10,1... | collective-permute-start | bytes 491528 | tf_op jit(solution)/shard_map/ppermute | solution.py:21
  5.0 13.3 %collective-permute-start.1 = (bf16[32,4,640]{2,1,0:T(4,128)(2,1)S(1)}, bf16[32,4,640]{2,1,0:T(4,128)(2,1)S(1)}, u32[]{:S(2)}, u32[]{:S(2)}) collective-permute-start(bf16[32,4,640]{2,1,0:T(4,128)(2,1)S(1)} %get-tuple-element.31), channel_id=1, source_target_pairs={{0,127},{1,0},{2,1},{3,2},{4,3},{5,4},{6,5},{7,6},{8,7},{9,8},{10,... | collective-permute-start | bytes 491528 | tf_op jit(solution)/shard_map/ppermute | solution.py:21
  18.4 1.0 collective-permute-done
  19.5 1.7 collective-permute-done.1
  21.4 1.9 %collective-permute-start.2 = (bf16[4,40,640]{2,1,0:T(8,128)(2,1)S(1)}, bf16[4,40,640]{2,1,0:T(8,128)(2,1)S(1)}, u32[]{:S(2)}, u32[]{:S(2)}) collective-permute-start(bf16[4,40,640]{2,1,0:T(8,128)(2,1)S(1)} %get-tuple-element.28), channel_id=1, source_target_pairs={{0,4},{1,5},{2,6},{3,7},{4,8},{5,9},{6,10},{7,11},{8,12},{9,13},{1... | collective-permute-start | bytes 614408 | tf_op jit(solution)/shard_map/ppermute | solution.py:21
  24.4 8.1 %collective-permute-start.3 = (bf16[4,40,640]{2,1,0:T(8,128)(2,1)S(1)}, bf16[4,40,640]{2,1,0:T(8,128)(2,1)S(1)}, u32[]{:S(2)}, u32[]{:S(2)}) collective-permute-start(bf16[4,40,640]{2,1,0:T(8,128)(2,1)S(1)} %get-tuple-element.29), channel_id=1, source_target_pairs={{0,124},{1,125},{2,126},{3,127},{4,0},{5,1},{6,2},{7,3},{8,4},{9,5... | collective-permute-start | bytes 614408 | tf_op jit(solution)/shard_map/ppermute | solution.py:21
  32.6 2.1 %collective-permute-done.2 = bf16[4,40,640]{2,1,0:T(8,128)(2,1)S(1)} collective-permute-done((bf16[4,40,640]{2,1,0:T(8,128)(2,1)S(1)}, bf16[4,40,640]{2,1,0:T(8,128)(2,1)S(1)}, u32[]{:S(2)}, u32[]{:S(2)}) %collective-permute-start.2) | collective-permute-done | bytes 204832 | tf_op jit(solution)/shard_map/ppermute | solution.py:21
  34.7 4.5 %collective-permute-done.3 = bf16[4,40,640]{2,1,0:T(8,128)(2,1)S(1)} collective-permute-done((bf16[4,40,640]{2,1,0:T(8,128)(2,1)S(1)}, bf16[4,40,640]{2,1,0:T(8,128)(2,1)S(1)}, u32[]{:S(2)}, u32[]{:S(2)}) %collective-permute-start.3) | collective-permute-done | bytes 204832 | tf_op jit(solution)/shard_map/ppermute | solution.py:21
  39.7 3.3 %pad_maximum_fusion.2 = (bf16[40,40,256]{2,1,0:T(8,128)(2,1)S(1)}, bf16[40,40,256]{2,1,0:T(8,128)(2,1)S(1)}) fusion(bf16[4,40,640]{2,1,0:T(8,128)(2,1)S(1)} %broadcast_select_fusion, bf16[4,40,640]{2,1,0:T(8,128)(2,1)S(1)} %broadcast_select_fusion.1, bf16[32,4,640]{2,1,0:T(4,128)(2,1)S(1)} %broadcast_select_fusion.2, ...), kind=kLoop, calls=%fused_computation.60 | loop fusion | flops 11468800 | bytes 3686400 | tf_op jit(solution)/shard_map/concatenate | solution.py:89
  44.2 1.9 %fusion.18 = f32[36,8,5,128]{3,1,2,0:T(8,128)S(1)} fusion(bf16[3,3,128,256]{3,2,1,0:T(8,128)(2,1)S(1)} %copy-done.10, bf16[40,1,7,4,256]{4,2,3,0,1:T(8,128)(2,1)S(1)} %slice.164, bf16[40,1,8,5,256]{4,2,3,0,1:T(8,128)(2,1)S(1)} %copy.62, pred[8,5]{0,1:T(8,128)(4,1)S(1)} %copy-done.13), kind=kOutput, calls=%fused_computation.26 | convolution fusion | flops 853954560 | bytes 2719784 | tf_op jit(solution)/shard_map/conv_general_dilated | solution.py:35
  47.3 2.0 %fusion.34 = (f32[36,8,5,128]{3,1,2,0:T(8,128)S(1)}, f32[36,8,5,128]{3,1,2,0:T(8,128)S(1)}, f32[36,8,5,128]{3,1,2,0:T(8,128)S(1)}) fusion(f32[128]{0:T(128)S(1)} %copy-done.9, bf16[3,3,256,128]{3,2,1,0:T(8,128)(2,1)S(1)} %copy-done, bf16[40,1,7,4,256]{4,2,3,0,1:T(8,128)(2,1)S(1)} %slice.160, bf16[40,1,8,5,256]{4,2,3,0,1:T(8,128)(2,1)S(1)} %copy.55, ...), kind=kOutput, calls=%fused_computation.70 | convolution fusion | flops 855982080 | bytes 4194856 | tf_op jit(solution)/shard_map/conv_general_dilated | solution.py:35
  51.3 1.0 convolution_bitcast_fusion.11
  52.4 1.1 convolution_bitcast_fusion.9
  64.6 1.0 convolution_select_fusion.1
  65.6 1.5 copy.59
  69.4 1.1 pad_maximum_fusion
  70.5 2.0 %reshape.99 = f32[9,2,2,2,2,2,2,2,256]{8,7,6,5,4,3,2,1,0:T(2,128)S(1)} reshape(f32[3,3,256,128]{3,2,1,0:T(8,128)} %pad_maximum_fusion) | data formatting | bytes 2359296 | tf_op jit(solution)/shard_map/reshape | solution.py:141
  72.5 1.1 maximum_bitcast_fusion.5
  73.6 1.1 maximum_bitcast_fusion.3
  74.7 1.1 pad_maximum_fusion.1
  75.8 2.9 %reshape.103 = f32[9,2,2,2,2,2,2,2,256]{8,7,6,5,4,3,2,1,0:T(2,128)} reshape(f32[3,3,128,256]{3,2,1,0:T(8,128)} %pad_maximum_fusion.1) | data formatting | bytes 2359296 | tf_op jit(solution)/shard_map/reshape | solution.py:141
  78.7 2.0 %copy.78 = f32[9,2,2,2,2,2,2,2,256]{8,0,4,5,6,1,2,3,7:T(8,128)S(1)} copy(f32[9,2,2,2,2,2,2,2,256]{8,7,6,5,4,3,2,1,0:T(2,128)} %reshape.103) | data formatting | bytes 2359296 | tf_op jit(solution)/shard_map/reshape | solution.py:141
  81.8 1.9 %collective-permute-start.11 = (f32[64,2432]{1,0:T(8,128)S(1)}, f32[64,2432]{1,0:T(8,128)S(1)}, u32[]{:S(2)}, u32[]{:S(2)}) collective-permute-start(f32[64,2432]{1,0:T(8,128)S(1)} %constant_dynamic-slice_fusion.6), channel_id=1, source_target_pairs={{0,1},{1,0},{2,3},{3,2},{4,5},{5,4},{6,7},{7,6},{8,9},{9,8},{10,11... | collective-permute-start | bytes 1867784 | tf_op jit(solution)/shard_map/ppermute | solution.py:94
  85.6 2.5 %collective-permute-start.4 = (f32[64,2432]{1,0:T(8,128)S(1)}, f32[64,2432]{1,0:T(8,128)S(1)}, u32[]{:S(2)}, u32[]{:S(2)}) collective-permute-start(f32[64,2432]{1,0:T(8,128)S(1)} %constant_dynamic-slice_fusion.13), channel_id=1, source_target_pairs={{0,1},{1,0},{2,3},{3,2},{4,5},{5,4},{6,7},{7,6},{8,9},{9,8},{10,11... | collective-permute-start | bytes 1867784 | tf_op jit(solution)/shard_map/ppermute | solution.py:94
  88.7 1.9 %collective-permute-start.12 = (f32[32,2432]{1,0:T(8,128)S(1)}, f32[32,2432]{1,0:T(8,128)S(1)}, u32[]{:S(2)}, u32[]{:S(2)}) collective-permute-start(f32[32,2432]{1,0:T(8,128)S(1)} %constant_dynamic-slice_fusion.5), channel_id=1, source_target_pairs={{0,16},{16,0},{32,48},{48,32},{64,80},{80,64},{96,112},{112,96},{1... | collective-permute-start | bytes 933896 | tf_op jit(solution)/shard_map/ppermute | solution.py:94
  90.8 1.9 %collective-permute-start.5 = (f32[32,2432]{1,0:T(8,128)S(1)}, f32[32,2432]{1,0:T(8,128)S(1)}, u32[]{:S(2)}, u32[]{:S(2)}) collective-permute-start(f32[32,2432]{1,0:T(8,128)S(1)} %constant_dynamic-slice_fusion.12), channel_id=1, source_target_pairs={{0,2},{2,0},{4,6},{6,4},{8,10},{10,8},{12,14},{14,12},{1,3},{3,1},... | collective-permute-start | bytes 933896 | tf_op jit(solution)/shard_map/ppermute | solution.py:94
  92.7 7.2 %collective-permute-done.12 = f32[32,2432]{1,0:T(8,128)S(1)} collective-permute-done((f32[32,2432]{1,0:T(8,128)S(1)}, f32[32,2432]{1,0:T(8,128)S(1)}, u32[]{:S(2)}, u32[]{:S(2)}) %collective-permute-start.12) | collective-permute-done | bytes 311328 | tf_op jit(solution)/shard_map/ppermute | solution.py:94
  100.0 1.9 %collective-permute-start.13 = (f32[16,2432]{1,0:T(8,128)S(1)}, f32[16,2432]{1,0:T(8,128)S(1)}, u32[]{:S(2)}, u32[]{:S(2)}) collective-permute-start(f32[16,2432]{1,0:T(8,128)S(1)} %constant_dynamic-slice_fusion.4), channel_id=1, source_target_pairs={{0,32},{16,48},{32,0},{48,16},{64,96},{80,112},{96,64},{112,80},{1... | collective-permute-start | bytes 466952 | tf_op jit(solution)/shard_map/ppermute | solution.py:94
  102.1 4.7 %collective-permute-start.6 = (f32[16,2432]{1,0:T(8,128)S(1)}, f32[16,2432]{1,0:T(8,128)S(1)}, u32[]{:S(2)}, u32[]{:S(2)}) collective-permute-start(f32[16,2432]{1,0:T(8,128)S(1)} %constant_dynamic-slice_fusion.11), channel_id=1, source_target_pairs={{0,4},{2,6},{4,0},{6,2},{8,12},{10,14},{12,8},{14,10},{1,5},{3,7},... | collective-permute-start | bytes 466952 | tf_op jit(solution)/shard_map/ppermute | solution.py:94
  106.8 4.4 %collective-permute-done.13 = f32[16,2432]{1,0:T(8,128)S(1)} collective-permute-done((f32[16,2432]{1,0:T(8,128)S(1)}, f32[16,2432]{1,0:T(8,128)S(1)}, u32[]{:S(2)}, u32[]{:S(2)}) %collective-permute-start.13) | collective-permute-done | bytes 155680 | tf_op jit(solution)/shard_map/ppermute | solution.py:94
  111.2 5.1 %collective-permute-start.14 = (f32[8,2432]{1,0:T(8,128)S(1)}, f32[8,2432]{1,0:T(8,128)S(1)}, u32[]{:S(2)}, u32[]{:S(2)}) collective-permute-start(f32[8,2432]{1,0:T(8,128)S(1)} %constant_dynamic-slice_fusion.3), channel_id=1, source_target_pairs={{0,64},{16,80},{32,96},{48,112},{64,0},{80,16},{96,32},{112,48},{1... | collective-permute-start | bytes 233480 | tf_op jit(solution)/shard_map/ppermute | solution.py:94
  116.4 4.7 %collective-permute-start.7 = (f32[8,2432]{1,0:T(8,128)S(1)}, f32[8,2432]{1,0:T(8,128)S(1)}, u32[]{:S(2)}, u32[]{:S(2)}) collective-permute-start(f32[8,2432]{1,0:T(8,128)S(1)} %constant_dynamic-slice_fusion.10), channel_id=1, source_target_pairs={{0,8},{2,10},{4,12},{6,14},{8,0},{10,2},{12,4},{14,6},{1,9},{3,11}... | collective-permute-start | bytes 233480 | tf_op jit(solution)/shard_map/ppermute | solution.py:94
  122.2 2.1 %collective-permute-start.15 = (f32[4,2432]{1,0:T(4,128)S(1)}, f32[4,2432]{1,0:T(4,128)S(1)}, u32[]{:S(2)}, u32[]{:S(2)}) collective-permute-start(f32[4,2432]{1,0:T(4,128)S(1)} %constant_dynamic-slice_fusion.2), channel_id=1, source_target_pairs={{0,2},{2,0},{4,6},{6,4},{8,10},{10,8},{12,14},{14,12},{1,3},{3,1},... | collective-permute-start | bytes 116744 | tf_op jit(solution)/shard_map/ppermute | solution.py:94
  124.2 2.4 %collective-permute-done.7 = f32[8,2432]{1,0:T(8,128)S(1)} collective-permute-done((f32[8,2432]{1,0:T(8,128)S(1)}, f32[8,2432]{1,0:T(8,128)S(1)}, u32[]{:S(2)}, u32[]{:S(2)}) %collective-permute-start.7) | collective-permute-done | bytes 77856 | tf_op jit(solution)/shard_map/ppermute | solution.py:94
  126.7 2.5 %collective-permute-start.8 = (f32[4,2432]{1,0:T(4,128)S(1)}, f32[4,2432]{1,0:T(4,128)S(1)}, u32[]{:S(2)}, u32[]{:S(2)}) collective-permute-start(f32[4,2432]{1,0:T(4,128)S(1)} %constant_dynamic-slice_fusion.9), channel_id=1, source_target_pairs={{0,16},{16,0},{32,48},{48,32},{64,80},{80,64},{96,112},{112,96},{1... | collective-permute-start | bytes 116744 | tf_op jit(solution)/shard_map/ppermute | solution.py:94
  129.2 5.4 %collective-permute-start.16 = (f32[2,2432]{1,0:T(2,128)S(1)}, f32[2,2432]{1,0:T(2,128)S(1)}, u32[]{:S(2)}, u32[]{:S(2)}) collective-permute-start(f32[2,2432]{1,0:T(2,128)S(1)} %constant_dynamic-slice_fusion.1), channel_id=1, source_target_pairs={{0,4},{2,6},{4,0},{6,2},{8,12},{10,14},{12,8},{14,10},{1,5},{3,7},... | collective-permute-start | bytes 58376 | tf_op jit(solution)/shard_map/ppermute | solution.py:94
  134.7 5.3 %collective-permute-start.9 = (f32[2,2432]{1,0:T(2,128)S(1)}, f32[2,2432]{1,0:T(2,128)S(1)}, u32[]{:S(2)}, u32[]{:S(2)}) collective-permute-start(f32[2,2432]{1,0:T(2,128)S(1)} %constant_dynamic-slice_fusion.8), channel_id=1, source_target_pairs={{0,32},{16,48},{32,0},{48,16},{64,96},{80,112},{96,64},{112,80},{1... | collective-permute-start | bytes 58376 | tf_op jit(solution)/shard_map/ppermute | solution.py:94
  140.1 5.4 %collective-permute-start.17 = (f32[1,2432]{1,0:T(1,128)S(1)}, f32[1,2432]{1,0:T(1,128)S(1)}, u32[]{:S(2)}, u32[]{:S(2)}) collective-permute-start(f32[1,2432]{1,0:T(1,128)S(1)} %constant_dynamic-slice_fusion), channel_id=1, source_target_pairs={{0,8},{2,10},{4,12},{6,14},{8,0},{10,2},{12,4},{14,6},{1,9},{3,11}... | collective-permute-start | bytes 29192 | tf_op jit(solution)/shard_map/ppermute | solution.py:94
  145.5 3.2 %collective-permute-start.10 = (f32[1,2432]{1,0:T(1,128)S(1)}, f32[1,2432]{1,0:T(1,128)S(1)}, u32[]{:S(2)}, u32[]{:S(2)}) collective-permute-start(f32[1,2432]{1,0:T(1,128)S(1)} %constant_dynamic-slice_fusion.7), channel_id=1, source_target_pairs={{0,64},{16,80},{32,96},{48,112},{64,0},{80,16},{96,32},{112,48},{1... | collective-permute-start | bytes 29192 | tf_op jit(solution)/shard_map/ppermute | solution.py:94
  149.5 5.4 %collective-permute-done.10 = f32[1,2432]{1,0:T(1,128)S(1)} collective-permute-done((f32[1,2432]{1,0:T(1,128)S(1)}, f32[1,2432]{1,0:T(1,128)S(1)}, u32[]{:S(2)}, u32[]{:S(2)}) %collective-permute-start.10) | collective-permute-done | bytes 9760 | tf_op jit(solution)/shard_map/ppermute | solution.py:94
  155.0 2.7 %collective-permute-start.18 = (f32[1,4864]{1,0:T(1,128)S(1)}, f32[1,4864]{1,0:T(1,128)S(1)}, u32[]{:S(2)}, u32[]{:S(2)}) collective-permute-start(f32[1,4864]{1,0:T(1,128)S(1)} %pad_maximum_fusion.49), channel_id=1, source_target_pairs={{0,128},{128,0},{256,384},{384,256},{1,129},{129,1},{257,385},{385... | collective-permute-start | bytes 58376 | tf_op jit(solution)/shard_map/ppermute | solution.py:94
  157.8 1.1 convolution_select_fusion
  159.4 1.4 collective-permute-done.18
  160.9 3.2 %collective-permute-start.19 = (f32[1,4864]{1,0:T(1,128)S(1)}, f32[1,4864]{1,0:T(1,128)S(1)}, u32[]{:S(2)}, u32[]{:S(2)}) collective-permute-start(f32[1,4864]{1,0:T(1,128)S(1)} %fusion.139), channel_id=1, source_target_pairs={{0,256},{128,384},{256,0},{384,128},{1,257},{129,385},{257,1},{385... | collective-permute-start | bytes 58376 | tf_op jit(solution)/shard_map/ppermute | solution.py:94
  164.0 1.4 fusion.26
  165.4 1.1 copy.80
  166.5 1.5 collective-permute-done.19
  (141 shorter events, 28.5 us)
Async XLA Ops:
  0.6 46.4 %copy-start = (bf16[3,3,256,128]{3,2,1,0:T(8,128)(2,1)S(1)}, bf16[3,3,256,128]{3,2,1,0:T(8,128)(2,1)}, u32[]{:S(2)}) copy-start(bf16[3,3,256,128]{3,2,1,0:T(8,128)(2,1)} %param.10) | copy-start | bytes 1769476
  0.6 2.3 %copy-start.1 = (bf16[1,1,32,32,256]{4,3,2,1,0:T(8,128)(2,1)S(1)}, bf16[1,1,32,32,256]{4,3,2,1,0:T(8,128)(2,1)}, u32[]{:S(2)}) copy-start(bf16[1,1,32,32,256]{4,3,2,1,0:T(8,128)(2,1)} %param.7) | copy-start | bytes 1572868
  3.1 16.3 %collective-permute-start = (bf16[32,4,640]{2,1,0:T(4,128)(2,1)S(1)}, bf16[32,4,640]{2,1,0:T(4,128)(2,1)S(1)}, u32[]{:S(2)}, u32[]{:S(2)}) collective-permute-start(bf16[32,4,640]{2,1,0:T(4,128)(2,1)S(1)} %get-tuple-element.30), channel_id=1, source_target_pairs={{0,1},{1,2},{2,3},{3,4},{4,5},{5,6},{6,7},{7,8},{8,9},{9,10},{10,1... | collective-permute-start | bytes 491528 | tf_op jit(solution)/shard_map/ppermute | solution.py:21
  5.0 16.1 %collective-permute-start.1 = (bf16[32,4,640]{2,1,0:T(4,128)(2,1)S(1)}, bf16[32,4,640]{2,1,0:T(4,128)(2,1)S(1)}, u32[]{:S(2)}, u32[]{:S(2)}) collective-permute-start(bf16[32,4,640]{2,1,0:T(4,128)(2,1)S(1)} %get-tuple-element.31), channel_id=1, source_target_pairs={{0,127},{1,0},{2,1},{3,2},{4,3},{5,4},{6,5},{7,6},{8,7},{9,8},{10,... | collective-permute-start | bytes 491528 | tf_op jit(solution)/shard_map/ppermute | solution.py:21
  21.4 13.3 %collective-permute-start.2 = (bf16[4,40,640]{2,1,0:T(8,128)(2,1)S(1)}, bf16[4,40,640]{2,1,0:T(8,128)(2,1)S(1)}, u32[]{:S(2)}, u32[]{:S(2)}) collective-permute-start(bf16[4,40,640]{2,1,0:T(8,128)(2,1)S(1)} %get-tuple-element.28), channel_id=1, source_target_pairs={{0,4},{1,5},{2,6},{3,7},{4,8},{5,9},{6,10},{7,11},{8,12},{9,13},{1... | collective-permute-start | bytes 614408 | tf_op jit(solution)/shard_map/ppermute | solution.py:21
  24.4 14.8 %collective-permute-start.3 = (bf16[4,40,640]{2,1,0:T(8,128)(2,1)S(1)}, bf16[4,40,640]{2,1,0:T(8,128)(2,1)S(1)}, u32[]{:S(2)}, u32[]{:S(2)}) collective-permute-start(bf16[4,40,640]{2,1,0:T(8,128)(2,1)S(1)} %get-tuple-element.29), channel_id=1, source_target_pairs={{0,124},{1,125},{2,126},{3,127},{4,0},{5,1},{6,2},{7,3},{8,4},{9,5... | collective-permute-start | bytes 614408 | tf_op jit(solution)/shard_map/ppermute | solution.py:21
  43.1 1.1 copy-start.10
  43.1 1.1 copy-start.13
  46.7 0.7 copy-start.9
  63.9 0.7 copy-start.11
  65.6 2.7 %copy-start.7 = (f32[1,256,128]{2,1,0:T(8,128)S(1)}, f32[1,256,128]{2,1,0:T(8,128)}, u32[]{:S(2)}) copy-start(f32[1,256,128]{2,1,0:T(8,128)} %convolution_bitcast_fusion.10) | copy-start | bytes 393220
  80.7 0.9 copy-start.5
  81.8 6.8 %collective-permute-start.11 = (f32[64,2432]{1,0:T(8,128)S(1)}, f32[64,2432]{1,0:T(8,128)S(1)}, u32[]{:S(2)}, u32[]{:S(2)}) collective-permute-start(f32[64,2432]{1,0:T(8,128)S(1)} %constant_dynamic-slice_fusion.6), channel_id=1, source_target_pairs={{0,1},{1,0},{2,3},{3,2},{4,5},{5,4},{6,7},{7,6},{8,9},{9,8},{10,11... | collective-permute-start | bytes 1867784 | tf_op jit(solution)/shard_map/ppermute | solution.py:94
  84.5 1.0 copy-start.6
  85.5 2.7 %copy-start.2 = (f32[32,8,5,256]{3,0,2,1:T(8,128)S(1)}, f32[32,8,5,256]{3,0,2,1:T(8,128)}, u32[]{:S(2)}) copy-start(f32[32,8,5,256]{3,0,2,1:T(8,128)} %copy.59) | copy-start | bytes 3932164
  85.5 2.7 %copy-start.8 = (f32[256]{0:T(256)S(1)}, f32[256]{0:T(256)}, u32[]{:S(2)}) copy-start(f32[256]{0:T(256)} %param.13) | copy-start | bytes 3076
  85.6 5.0 %collective-permute-start.4 = (f32[64,2432]{1,0:T(8,128)S(1)}, f32[64,2432]{1,0:T(8,128)S(1)}, u32[]{:S(2)}, u32[]{:S(2)}) collective-permute-start(f32[64,2432]{1,0:T(8,128)S(1)} %constant_dynamic-slice_fusion.13), channel_id=1, source_target_pairs={{0,1},{1,0},{2,3},{3,2},{4,5},{5,4},{6,7},{7,6},{8,9},{9,8},{10,11... | collective-permute-start | bytes 1867784 | tf_op jit(solution)/shard_map/ppermute | solution.py:94
  88.7 11.2 %collective-permute-start.12 = (f32[32,2432]{1,0:T(8,128)S(1)}, f32[32,2432]{1,0:T(8,128)S(1)}, u32[]{:S(2)}, u32[]{:S(2)}) collective-permute-start(f32[32,2432]{1,0:T(8,128)S(1)} %constant_dynamic-slice_fusion.5), channel_id=1, source_target_pairs={{0,16},{16,0},{32,48},{48,32},{64,80},{80,64},{96,112},{112,96},{1... | collective-permute-start | bytes 933896 | tf_op jit(solution)/shard_map/ppermute | solution.py:94
  90.8 11.2 %collective-permute-start.5 = (f32[32,2432]{1,0:T(8,128)S(1)}, f32[32,2432]{1,0:T(8,128)S(1)}, u32[]{:S(2)}, u32[]{:S(2)}) collective-permute-start(f32[32,2432]{1,0:T(8,128)S(1)} %constant_dynamic-slice_fusion.12), channel_id=1, source_target_pairs={{0,2},{2,0},{4,6},{6,4},{8,10},{10,8},{12,14},{14,12},{1,3},{3,1},... | collective-permute-start | bytes 933896 | tf_op jit(solution)/shard_map/ppermute | solution.py:94
  100.0 11.2 %collective-permute-start.13 = (f32[16,2432]{1,0:T(8,128)S(1)}, f32[16,2432]{1,0:T(8,128)S(1)}, u32[]{:S(2)}, u32[]{:S(2)}) collective-permute-start(f32[16,2432]{1,0:T(8,128)S(1)} %constant_dynamic-slice_fusion.4), channel_id=1, source_target_pairs={{0,32},{16,48},{32,0},{48,16},{64,96},{80,112},{96,64},{112,80},{1... | collective-permute-start | bytes 466952 | tf_op jit(solution)/shard_map/ppermute | solution.py:94
  102.0 55.7 %copy-start.4 = (bf16[36,1,7,4,128]{4,2,3,0,1:T(8,128)(2,1)S(1)}, bf16[36,1,7,4,128]{4,2,3,0,1:T(8,128)(2,1)}, u32[]{:S(2)}) copy-start(bf16[36,1,7,4,128]{4,2,3,0,1:T(8,128)(2,1)} %slice.167) | copy-start | bytes 774148
  102.0 55.7 %copy-start.12 = (pred[8,5]{0,1:T(8,128)(4,1)S(1)}, pred[8,5]{0,1:T(8,128)(4,1)}, u32[]{:S(2)}) copy-start(pred[8,5]{0,1:T(8,128)(4,1)} %constant.213) | copy-start | bytes 124
  102.1 14.3 %collective-permute-start.6 = (f32[16,2432]{1,0:T(8,128)S(1)}, f32[16,2432]{1,0:T(8,128)S(1)}, u32[]{:S(2)}, u32[]{:S(2)}) collective-permute-start(f32[16,2432]{1,0:T(8,128)S(1)} %constant_dynamic-slice_fusion.11), channel_id=1, source_target_pairs={{0,4},{2,6},{4,0},{6,2},{8,12},{10,14},{12,8},{14,10},{1,5},{3,7},... | collective-permute-start | bytes 466952 | tf_op jit(solution)/shard_map/ppermute | solution.py:94
  111.2 10.9 %collective-permute-start.14 = (f32[8,2432]{1,0:T(8,128)S(1)}, f32[8,2432]{1,0:T(8,128)S(1)}, u32[]{:S(2)}, u32[]{:S(2)}) collective-permute-start(f32[8,2432]{1,0:T(8,128)S(1)} %constant_dynamic-slice_fusion.3), channel_id=1, source_target_pairs={{0,64},{16,80},{32,96},{48,112},{64,0},{80,16},{96,32},{112,48},{1... | collective-permute-start | bytes 233480 | tf_op jit(solution)/shard_map/ppermute | solution.py:94
  116.4 10.2 %collective-permute-start.7 = (f32[8,2432]{1,0:T(8,128)S(1)}, f32[8,2432]{1,0:T(8,128)S(1)}, u32[]{:S(2)}, u32[]{:S(2)}) collective-permute-start(f32[8,2432]{1,0:T(8,128)S(1)} %constant_dynamic-slice_fusion.10), channel_id=1, source_target_pairs={{0,8},{2,10},{4,12},{6,14},{8,0},{10,2},{12,4},{14,6},{1,9},{3,11}... | collective-permute-start | bytes 233480 | tf_op jit(solution)/shard_map/ppermute | solution.py:94
  122.2 7.0 %collective-permute-start.15 = (f32[4,2432]{1,0:T(4,128)S(1)}, f32[4,2432]{1,0:T(4,128)S(1)}, u32[]{:S(2)}, u32[]{:S(2)}) collective-permute-start(f32[4,2432]{1,0:T(4,128)S(1)} %constant_dynamic-slice_fusion.2), channel_id=1, source_target_pairs={{0,2},{2,0},{4,6},{6,4},{8,10},{10,8},{12,14},{14,12},{1,3},{3,1},... | collective-permute-start | bytes 116744 | tf_op jit(solution)/shard_map/ppermute | solution.py:94
  126.7 7.9 %collective-permute-start.8 = (f32[4,2432]{1,0:T(4,128)S(1)}, f32[4,2432]{1,0:T(4,128)S(1)}, u32[]{:S(2)}, u32[]{:S(2)}) collective-permute-start(f32[4,2432]{1,0:T(4,128)S(1)} %constant_dynamic-slice_fusion.9), channel_id=1, source_target_pairs={{0,16},{16,0},{32,48},{48,32},{64,80},{80,64},{96,112},{112,96},{1... | collective-permute-start | bytes 116744 | tf_op jit(solution)/shard_map/ppermute | solution.py:94
  129.2 10.8 %collective-permute-start.16 = (f32[2,2432]{1,0:T(2,128)S(1)}, f32[2,2432]{1,0:T(2,128)S(1)}, u32[]{:S(2)}, u32[]{:S(2)}) collective-permute-start(f32[2,2432]{1,0:T(2,128)S(1)} %constant_dynamic-slice_fusion.1), channel_id=1, source_target_pairs={{0,4},{2,6},{4,0},{6,2},{8,12},{10,14},{12,8},{14,10},{1,5},{3,7},... | collective-permute-start | bytes 58376 | tf_op jit(solution)/shard_map/ppermute | solution.py:94
  134.7 10.7 %collective-permute-start.9 = (f32[2,2432]{1,0:T(2,128)S(1)}, f32[2,2432]{1,0:T(2,128)S(1)}, u32[]{:S(2)}, u32[]{:S(2)}) collective-permute-start(f32[2,2432]{1,0:T(2,128)S(1)} %constant_dynamic-slice_fusion.8), channel_id=1, source_target_pairs={{0,32},{16,48},{32,0},{48,16},{64,96},{80,112},{96,64},{112,80},{1... | collective-permute-start | bytes 58376 | tf_op jit(solution)/shard_map/ppermute | solution.py:94
  140.1 9.5 %collective-permute-start.17 = (f32[1,2432]{1,0:T(1,128)S(1)}, f32[1,2432]{1,0:T(1,128)S(1)}, u32[]{:S(2)}, u32[]{:S(2)}) collective-permute-start(f32[1,2432]{1,0:T(1,128)S(1)} %constant_dynamic-slice_fusion), channel_id=1, source_target_pairs={{0,8},{2,10},{4,12},{6,14},{8,0},{10,2},{12,4},{14,6},{1,9},{3,11}... | collective-permute-start | bytes 29192 | tf_op jit(solution)/shard_map/ppermute | solution.py:94
  145.5 9.5 %collective-permute-start.10 = (f32[1,2432]{1,0:T(1,128)S(1)}, f32[1,2432]{1,0:T(1,128)S(1)}, u32[]{:S(2)}, u32[]{:S(2)}) collective-permute-start(f32[1,2432]{1,0:T(1,128)S(1)} %constant_dynamic-slice_fusion.7), channel_id=1, source_target_pairs={{0,64},{16,80},{32,96},{48,112},{64,0},{80,16},{96,32},{112,48},{1... | collective-permute-start | bytes 29192 | tf_op jit(solution)/shard_map/ppermute | solution.py:94
  155.0 5.8 %collective-permute-start.18 = (f32[1,4864]{1,0:T(1,128)S(1)}, f32[1,4864]{1,0:T(1,128)S(1)}, u32[]{:S(2)}, u32[]{:S(2)}) collective-permute-start(f32[1,4864]{1,0:T(1,128)S(1)} %pad_maximum_fusion.49), channel_id=1, source_target_pairs={{0,128},{128,0},{256,384},{384,256},{1,129},{129,1},{257,385},{385... | collective-permute-start | bytes 58376 | tf_op jit(solution)/shard_map/ppermute | solution.py:94
  159.3 4.8 %copy-start.3 = (bf16[1,1,32,32,256]{4,3,2,1,0:T(8,128)(2,1)S(1)}, bf16[1,1,32,32,256]{4,3,2,1,0:T(8,128)(2,1)}, u32[]{:S(2)}) copy-start(bf16[1,1,32,32,256]{4,3,2,1,0:T(8,128)(2,1)} %param.9) | copy-start | bytes 1572868
  160.9 7.2 %collective-permute-start.19 = (f32[1,4864]{1,0:T(1,128)S(1)}, f32[1,4864]{1,0:T(1,128)S(1)}, u32[]{:S(2)}, u32[]{:S(2)}) collective-permute-start(f32[1,4864]{1,0:T(1,128)S(1)} %fusion.139), channel_id=1, source_target_pairs={{0,256},{128,384},{256,0},{384,128},{1,257},{129,385},{257,1},{385... | collective-permute-start | bytes 58376 | tf_op jit(solution)/shard_map/ppermute | solution.py:94

commit v5 on v4

--- a/solution.py
+++ b/solution.py
@@ -72,21 +72,26 @@
     position = (lax.axis_index(SPACE) + 1) % count
     column = position % DEV_COLS
     line = position // DEV_COLS
-    last_line = count // DEV_COLS - 1
-    strips = []
-    for offset in (1, -1):
-        edge_cells = region[:, -width:] if offset == 1 else region[:, :width]
-        arrived = from_behind(edge_cells, SPACE, offset)
-        inside = column != 0 if offset == 1 else column != DEV_COLS - 1
-        strips.append(jnp.where(inside, arrived, jnp.zeros_like(arrived)))
-    widened = jnp.concatenate([strips[0], region, strips[1]], axis=1)
-    row_bands = []
-    for offset in (DEV_COLS, -DEV_COLS):
-        edge_cells = widened[-width:] if offset > 0 else widened[:width]
-        arrived = from_behind(edge_cells, SPACE, offset)
-        inside = line != 0 if offset > 0 else line != last_line
-        row_bands.append(jnp.where(inside, arrived, jnp.zeros_like(arrived)))
-    return jnp.concatenate([row_bands[0], widened, row_bands[1]], axis=0)
+    lines = count // DEV_COLS
+    rows_of = {-1: slice(-width, None), 0: slice(None), 1: slice(0, width)}
+    bands = []
+    for d_line in (-1, 0, 1):
+        band = []
+        for d_col in (-1, 0, 1):
+            if d_line == 0 and d_col == 0:
+                band.append(region)
+                continue
+            cells = region[rows_of[d_line], rows_of[d_col]]
+            arrived = from_behind(cells, SPACE, -(DEV_COLS * d_line + d_col))
+            inside = (
+                (line + d_line >= 0)
+                & (line + d_line < lines)
+                & (column + d_col >= 0)
+                & (column + d_col < DEV_COLS)
+            )
+            band.append(jnp.where(inside, arrived, jnp.zeros_like(arrived)))
+        bands.append(jnp.concatenate(band, axis=1))
+    return jnp.concatenate(bands, axis=0)
 
 
 def swap(value, axis, bit):

time: 171 us -> 179 us (1.047)
  starting transfers between devices: 79.8 us -> 93 us
  waiting for transfers between devices: 33.5 us -> 29.8 us
  other arithmetic: 15.4 us -> 13.1 us
    ppermute x4 -> x8, starting transfers between devices: 25.3 us -> 41.5 us  [from_behind(): lax.ppermute(array, axis, [(i, (i + by) % length) for i in range(length)])]
    ppermute x4 -> x8, waiting for transfers between devices: 9.34 us -> 3.04 us  [from_behind(): lax.ppermute(array, axis, [(i, (i + by) % length) for i in range(length)])]
    ppermute x16, starting transfers between devices: 54.5 us -> 51.5 us  [swap(): return lax.ppermute(value, axis, [(i, i ^ bit) for i in range(size)])]
    concatenate x1, other arithmetic: 3.27 us -> 0.48 us  [grid_halo(): return jnp.concatenate(bands, axis=0)]
    ppermute x16, waiting for transfers between devices: 24.2 us -> 26.7 us  [swap(): return lax.ppermute(value, axis, [(i, i ^ bit) for i in range(size)])]
  transfers between devices with their start and end apart: 20 -> 24, of which waited for: 13 -> 11; matrix products, arithmetic and copies ran while one was open for 5% -> 4% of each run, Pallas kernels for 0% -> 0%
where the time goes in v5:
time: 179 us; the launch traced here: 178 us
  starting transfers between devices  93 us (52%)
  waiting for transfers between devices  29.8 us (17%)
  local copies, waits for them, and re-layouts  20.7 us (12%)
  matrix products  19.1 us (11%)
  other arithmetic  13.1 us (7%)
  between operations  2.22 us (1%)
    ppermute x16, starting transfers between devices, swap(): return lax.ppermute(value, axis, [(i, i ^ bit) for i in range(size)])  51.5 us
    ppermute x8, starting transfers between devices, from_behind(): lax.ppermute(array, axis, [(i, (i + by) % length) for i in range(length)])  41.5 us
    ppermute x16, waiting for transfers between devices, swap(): return lax.ppermute(value, axis, [(i, i ^ bit) for i in range(size)])  26.7 us
    dot_general x18, matrix products, tap_sums(): lax.dot_general(window, flat_out, (((0,), (0,)), ((), ())), preferred_ele...  13.1 us
    reshape x4, local copies, waits for them, and re-layouts, shard_rows(): split = grad.reshape((9,) + (2,) * bits + (per * grad.shape[-1],))  7.66 us
    conv_general_dilated x4, matrix products, dilated(): lax.conv_general_dilated(padded[None], kernel, (1, 1), 'VALID', rhs_dilat...  5.97 us
    another operation x6, other arithmetic, tap_sums(): return jnp.stack(tap_rows)  5.45 us
    unnamed x33, local copies, waits for them, and re-layouts  4.42 us
  transfers between devices with their start and end apart: 24, of which 11 were waited for; matrix products, arithmetic and copies ran while one was open for 4% of the time, Pallas kernels for 0%

profile of v5, /device:TPU:6, one launch (start us, length us, event | category | flops | bytes accessed | tf_op | source)
XLA Modules:
  0.0 177.8 jit_solution(10462639977459850042)
XLA Ops:
  1.5 1.3 convert_reduce_fusion
  3.0 3.9 %collective-permute-start = (bf16[4,4,640]{2,1,0:T(4,128)(2,1)S(1)}, bf16[4,4,640]{2,1,0:T(4,128)(2,1)S(1)}, u32[]{:S(2)}, u32[]{:S(2)}) collective-permute-start(bf16[4,4,640]{2,1,0:T(4,128)(2,1)S(1)} %get-tuple-element.26), channel_id=1, source_target_pairs={{0,5},{1,6},{2,7},{3,8},{4,9},{5,10},{6,11},{7,12},{8,13},{9,14},{... | collective-permute-start | bytes 61448 | tf_op jit(solution)/shard_map/ppermute | solution.py:21
  6.9 12.8 %collective-permute-start.7 = (bf16[4,4,640]{2,1,0:T(4,128)(2,1)S(1)}, bf16[4,4,640]{2,1,0:T(4,128)(2,1)S(1)}, u32[]{:S(2)}, u32[]{:S(2)}) collective-permute-start(bf16[4,4,640]{2,1,0:T(4,128)(2,1)S(1)} %get-tuple-element.27), channel_id=1, source_target_pairs={{0,123},{1,124},{2,125},{3,126},{4,127},{5,0},{6,1},{7,2},{8,3},{9... | collective-permute-start | bytes 61448 | tf_op jit(solution)/shard_map/ppermute | solution.py:21
  19.8 3.8 %collective-permute-start.5 = (bf16[4,4,640]{2,1,0:T(4,128)(2,1)S(1)}, bf16[4,4,640]{2,1,0:T(4,128)(2,1)S(1)}, u32[]{:S(2)}, u32[]{:S(2)}) collective-permute-start(bf16[4,4,640]{2,1,0:T(4,128)(2,1)S(1)} %get-tuple-element.28), channel_id=1, source_target_pairs={{0,125},{1,126},{2,127},{3,0},{4,1},{5,2},{6,3},{7,4},{8,5},{9,6},... | collective-permute-start | bytes 61448 | tf_op jit(solution)/shard_map/ppermute | solution.py:21
  23.6 1.9 %collective-permute-start.2 = (bf16[4,4,640]{2,1,0:T(4,128)(2,1)S(1)}, bf16[4,4,640]{2,1,0:T(4,128)(2,1)S(1)}, u32[]{:S(2)}, u32[]{:S(2)}) collective-permute-start(bf16[4,4,640]{2,1,0:T(4,128)(2,1)S(1)} %get-tuple-element.29), channel_id=1, source_target_pairs={{0,3},{1,4},{2,5},{3,6},{4,7},{5,8},{6,9},{7,10},{8,11},{9,12},{10... | collective-permute-start | bytes 61448 | tf_op jit(solution)/shard_map/ppermute | solution.py:21
  25.6 2.7 %collective-permute-start.3 = (bf16[32,4,640]{2,1,0:T(4,128)(2,1)S(1)}, bf16[32,4,640]{2,1,0:T(4,128)(2,1)S(1)}, u32[]{:S(2)}, u32[]{:S(2)}) collective-permute-start(bf16[32,4,640]{2,1,0:T(4,128)(2,1)S(1)} %get-tuple-element.32), channel_id=1, source_target_pairs={{0,1},{1,2},{2,3},{3,4},{4,5},{5,6},{6,7},{7,8},{8,9},{9,10},{10,1... | collective-permute-start | bytes 491528 | tf_op jit(solution)/shard_map/ppermute | solution.py:21
  29.1 6.3 %collective-permute-start.4 = (bf16[32,4,640]{2,1,0:T(4,128)(2,1)S(1)}, bf16[32,4,640]{2,1,0:T(4,128)(2,1)S(1)}, u32[]{:S(2)}, u32[]{:S(2)}) collective-permute-start(bf16[32,4,640]{2,1,0:T(4,128)(2,1)S(1)} %get-tuple-element.33), channel_id=1, source_target_pairs={{0,127},{1,0},{2,1},{3,2},{4,3},{5,4},{6,5},{7,6},{8,7},{9,8},{10,... | collective-permute-start | bytes 491528 | tf_op jit(solution)/shard_map/ppermute | solution.py:21
  35.5 1.9 %collective-permute-start.1 = (bf16[4,32,640]{2,1,0:T(8,128)(2,1)S(1)}, bf16[4,32,640]{2,1,0:T(8,128)(2,1)S(1)}, u32[]{:S(2)}, u32[]{:S(2)}) collective-permute-start(bf16[4,32,640]{2,1,0:T(8,128)(2,1)S(1)} %get-tuple-element.30), channel_id=1, source_target_pairs={{0,4},{1,5},{2,6},{3,7},{4,8},{5,9},{6,10},{7,11},{8,12},{9,13},{1... | collective-permute-start | bytes 491528 | tf_op jit(solution)/shard_map/ppermute | solution.py:21
  37.4 8.1 %collective-permute-start.6 = (bf16[4,32,640]{2,1,0:T(8,128)(2,1)S(1)}, bf16[4,32,640]{2,1,0:T(8,128)(2,1)S(1)}, u32[]{:S(2)}, u32[]{:S(2)}) collective-permute-start(bf16[4,32,640]{2,1,0:T(8,128)(2,1)S(1)} %get-tuple-element.31), channel_id=1, source_target_pairs={{0,124},{1,125},{2,126},{3,127},{4,0},{5,1},{6,2},{7,3},{8,4},{9,5... | collective-permute-start | bytes 491528 | tf_op jit(solution)/shard_map/ppermute | solution.py:21
  45.8 2.2 %collective-permute-done.1 = bf16[4,32,640]{2,1,0:T(8,128)(2,1)S(1)} collective-permute-done((bf16[4,32,640]{2,1,0:T(8,128)(2,1)S(1)}, bf16[4,32,640]{2,1,0:T(8,128)(2,1)S(1)}, u32[]{:S(2)}, u32[]{:S(2)}) %collective-permute-start.1) | collective-permute-done | bytes 163872 | tf_op jit(solution)/shard_map/ppermute | solution.py:21
  51.5 1.9 %fusion.18 = f32[36,8,5,128]{3,1,2,0:T(8,128)S(1)} fusion(bf16[3,3,128,256]{3,2,1,0:T(8,128)(2,1)S(1)} %copy-done.11, bf16[40,1,7,4,256]{4,2,3,0,1:T(8,128)(2,1)S(1)} %slice.180, bf16[40,1,8,5,256]{4,2,3,0,1:T(8,128)(2,1)S(1)} %copy.62, pred[8,5]{0,1:T(8,128)(4,1)S(1)} %copy-done.13), kind=kOutput, calls=%fused_computation.26 | convolution fusion | flops 853954560 | bytes 2719784 | tf_op jit(solution)/shard_map/conv_general_dilated | solution.py:35
  54.7 2.0 %fusion.36 = (f32[36,8,5,128]{3,1,2,0:T(8,128)S(1)}, f32[36,8,5,128]{3,1,2,0:T(8,128)S(1)}, f32[36,8,5,128]{3,1,2,0:T(8,128)S(1)}) fusion(f32[128]{0:T(128)S(1)} %copy-done.10, bf16[3,3,256,128]{3,2,1,0:T(8,128)(2,1)S(1)} %copy-done, bf16[40,1,7,4,256]{4,2,3,0,1:T(8,128)(2,1)S(1)} %slice.176, bf16[40,1,8,5,256]{4,2,3,0,1:T(8,128)(2,1)S(1)} %copy.55, ...), kind=kOutput, calls=%fused_computation.74 | convolution fusion | flops 855982080 | bytes 4194856 | tf_op jit(solution)/shard_map/conv_general_dilated | solution.py:35
  59.7 1.0 convolution_bitcast_fusion.9
  74.2 1.5 copy.59
  78.0 1.1 pad_maximum_fusion
  79.1 2.0 %reshape.99 = f32[9,2,2,2,2,2,2,2,256]{8,7,6,5,4,3,2,1,0:T(2,128)S(1)} reshape(f32[3,3,256,128]{3,2,1,0:T(8,128)} %pad_maximum_fusion) | data formatting | bytes 2359296 | tf_op jit(solution)/shard_map/reshape | solution.py:146
  81.2 1.1 maximum_bitcast_fusion.5
  82.2 1.1 maximum_bitcast_fusion.3
  83.3 1.1 pad_maximum_fusion.1
  84.4 2.9 %reshape.103 = f32[9,2,2,2,2,2,2,2,256]{8,7,6,5,4,3,2,1,0:T(2,128)} reshape(f32[3,3,128,256]{3,2,1,0:T(8,128)} %pad_maximum_fusion.1) | data formatting | bytes 2359296 | tf_op jit(solution)/shard_map/reshape | solution.py:146
  87.3 2.0 %copy.78 = f32[9,2,2,2,2,2,2,2,256]{8,0,4,5,6,1,2,3,7:T(8,128)S(1)} copy(f32[9,2,2,2,2,2,2,2,256]{8,7,6,5,4,3,2,1,0:T(2,128)} %reshape.103) | data formatting | bytes 2359296 | tf_op jit(solution)/shard_map/reshape | solution.py:146
  90.4 1.9 %collective-permute-start.15 = (f32[64,2432]{1,0:T(8,128)S(1)}, f32[64,2432]{1,0:T(8,128)S(1)}, u32[]{:S(2)}, u32[]{:S(2)}) collective-permute-start(f32[64,2432]{1,0:T(8,128)S(1)} %constant_dynamic-slice_fusion.6), channel_id=1, source_target_pairs={{0,1},{1,0},{2,3},{3,2},{4,5},{5,4},{6,7},{7,6},{8,9},{9,8},{10,11... | collective-permute-start | bytes 1867784 | tf_op jit(solution)/shard_map/ppermute | solution.py:99
  94.3 2.5 %collective-permute-start.8 = (f32[64,2432]{1,0:T(8,128)S(1)}, f32[64,2432]{1,0:T(8,128)S(1)}, u32[]{:S(2)}, u32[]{:S(2)}) collective-permute-start(f32[64,2432]{1,0:T(8,128)S(1)} %constant_dynamic-slice_fusion.13), channel_id=1, source_target_pairs={{0,1},{1,0},{2,3},{3,2},{4,5},{5,4},{6,7},{7,6},{8,9},{9,8},{10,11... | collective-permute-start | bytes 1867784 | tf_op jit(solution)/shard_map/ppermute | solution.py:99
  97.4 1.9 %collective-permute-start.16 = (f32[32,2432]{1,0:T(8,128)S(1)}, f32[32,2432]{1,0:T(8,128)S(1)}, u32[]{:S(2)}, u32[]{:S(2)}) collective-permute-start(f32[32,2432]{1,0:T(8,128)S(1)} %constant_dynamic-slice_fusion.5), channel_id=1, source_target_pairs={{0,16},{16,0},{32,48},{48,32},{64,80},{80,64},{96,112},{112,96},{1... | collective-permute-start | bytes 933896 | tf_op jit(solution)/shard_map/ppermute | solution.py:99
  99.4 1.9 %collective-permute-start.9 = (f32[32,2432]{1,0:T(8,128)S(1)}, f32[32,2432]{1,0:T(8,128)S(1)}, u32[]{:S(2)}, u32[]{:S(2)}) collective-permute-start(f32[32,2432]{1,0:T(8,128)S(1)} %constant_dynamic-slice_fusion.12), channel_id=1, source_target_pairs={{0,2},{2,0},{4,6},{6,4},{8,10},{10,8},{12,14},{14,12},{1,3},{3,1},... | collective-permute-start | bytes 933896 | tf_op jit(solution)/shard_map/ppermute | solution.py:99
  101.3 7.2 %collective-permute-done.16 = f32[32,2432]{1,0:T(8,128)S(1)} collective-permute-done((f32[32,2432]{1,0:T(8,128)S(1)}, f32[32,2432]{1,0:T(8,128)S(1)}, u32[]{:S(2)}, u32[]{:S(2)}) %collective-permute-start.16) | collective-permute-done | bytes 311328 | tf_op jit(solution)/shard_map/ppermute | solution.py:99
  108.6 1.9 %collective-permute-start.17 = (f32[16,2432]{1,0:T(8,128)S(1)}, f32[16,2432]{1,0:T(8,128)S(1)}, u32[]{:S(2)}, u32[]{:S(2)}) collective-permute-start(f32[16,2432]{1,0:T(8,128)S(1)} %constant_dynamic-slice_fusion.4), channel_id=1, source_target_pairs={{0,32},{16,48},{32,0},{48,16},{64,96},{80,112},{96,64},{112,80},{1... | collective-permute-start | bytes 466952 | tf_op jit(solution)/shard_map/ppermute | solution.py:99
  110.7 3.0 %collective-permute-start.10 = (f32[16,2432]{1,0:T(8,128)S(1)}, f32[16,2432]{1,0:T(8,128)S(1)}, u32[]{:S(2)}, u32[]{:S(2)}) collective-permute-start(f32[16,2432]{1,0:T(8,128)S(1)} %constant_dynamic-slice_fusion.11), channel_id=1, source_target_pairs={{0,4},{2,6},{4,0},{6,2},{8,12},{10,14},{12,8},{14,10},{1,5},{3,7},... | collective-permute-start | bytes 466952 | tf_op jit(solution)/shard_map/ppermute | solution.py:99
  113.6 6.2 %collective-permute-done.17 = f32[16,2432]{1,0:T(8,128)S(1)} collective-permute-done((f32[16,2432]{1,0:T(8,128)S(1)}, f32[16,2432]{1,0:T(8,128)S(1)}, u32[]{:S(2)}, u32[]{:S(2)}) %collective-permute-start.17) | collective-permute-done | bytes 155680 | tf_op jit(solution)/shard_map/ppermute | solution.py:99
  119.9 6.0 %collective-permute-start.18 = (f32[8,2432]{1,0:T(8,128)S(1)}, f32[8,2432]{1,0:T(8,128)S(1)}, u32[]{:S(2)}, u32[]{:S(2)}) collective-permute-start(f32[8,2432]{1,0:T(8,128)S(1)} %constant_dynamic-slice_fusion.3), channel_id=1, source_target_pairs={{0,64},{16,80},{32,96},{48,112},{64,0},{80,16},{96,32},{112,48},{1... | collective-permute-start | bytes 233480 | tf_op jit(solution)/shard_map/ppermute | solution.py:99
  126.0 3.6 %collective-permute-start.11 = (f32[8,2432]{1,0:T(8,128)S(1)}, f32[8,2432]{1,0:T(8,128)S(1)}, u32[]{:S(2)}, u32[]{:S(2)}) collective-permute-start(f32[8,2432]{1,0:T(8,128)S(1)} %constant_dynamic-slice_fusion.10), channel_id=1, source_target_pairs={{0,8},{2,10},{4,12},{6,14},{8,0},{10,2},{12,4},{14,6},{1,9},{3,11}... | collective-permute-start | bytes 233480 | tf_op jit(solution)/shard_map/ppermute | solution.py:99
  129.6 1.9 %collective-permute-done.18 = f32[8,2432]{1,0:T(8,128)S(1)} collective-permute-done((f32[8,2432]{1,0:T(8,128)S(1)}, f32[8,2432]{1,0:T(8,128)S(1)}, u32[]{:S(2)}, u32[]{:S(2)}) %collective-permute-start.18) | collective-permute-done | bytes 77856 | tf_op jit(solution)/shard_map/ppermute | solution.py:99
  131.6 1.9 %collective-permute-start.19 = (f32[4,2432]{1,0:T(4,128)S(1)}, f32[4,2432]{1,0:T(4,128)S(1)}, u32[]{:S(2)}, u32[]{:S(2)}) collective-permute-start(f32[4,2432]{1,0:T(4,128)S(1)} %constant_dynamic-slice_fusion.2), channel_id=1, source_target_pairs={{0,2},{2,0},{4,6},{6,4},{8,10},{10,8},{12,14},{14,12},{1,3},{3,1},... | collective-permute-start | bytes 116744 | tf_op jit(solution)/shard_map/ppermute | solution.py:99
  133.5 3.7 %collective-permute-done.11 = f32[8,2432]{1,0:T(8,128)S(1)} collective-permute-done((f32[8,2432]{1,0:T(8,128)S(1)}, f32[8,2432]{1,0:T(8,128)S(1)}, u32[]{:S(2)}, u32[]{:S(2)}) %collective-permute-start.11) | collective-permute-done | bytes 77856 | tf_op jit(solution)/shard_map/ppermute | solution.py:99
  137.3 1.9 %collective-permute-start.12 = (f32[4,2432]{1,0:T(4,128)S(1)}, f32[4,2432]{1,0:T(4,128)S(1)}, u32[]{:S(2)}, u32[]{:S(2)}) collective-permute-start(f32[4,2432]{1,0:T(4,128)S(1)} %constant_dynamic-slice_fusion.9), channel_id=1, source_target_pairs={{0,16},{16,0},{32,48},{48,32},{64,80},{80,64},{96,112},{112,96},{1... | collective-permute-start | bytes 116744 | tf_op jit(solution)/shard_map/ppermute | solution.py:99
  139.3 2.3 %collective-permute-start.20 = (f32[2,2432]{1,0:T(2,128)S(1)}, f32[2,2432]{1,0:T(2,128)S(1)}, u32[]{:S(2)}, u32[]{:S(2)}) collective-permute-start(f32[2,2432]{1,0:T(2,128)S(1)} %constant_dynamic-slice_fusion.1), channel_id=1, source_target_pairs={{0,4},{2,6},{4,0},{6,2},{8,12},{10,14},{12,8},{14,10},{1,5},{3,7},... | collective-permute-start | bytes 58376 | tf_op jit(solution)/shard_map/ppermute | solution.py:99
  141.6 1.6 collective-permute-done.12
  143.2 3.6 %collective-permute-start.13 = (f32[2,2432]{1,0:T(2,128)S(1)}, f32[2,2432]{1,0:T(2,128)S(1)}, u32[]{:S(2)}, u32[]{:S(2)}) collective-permute-start(f32[2,2432]{1,0:T(2,128)S(1)} %constant_dynamic-slice_fusion.8), channel_id=1, source_target_pairs={{0,32},{16,48},{32,0},{48,16},{64,96},{80,112},{96,64},{112,80},{1... | collective-permute-start | bytes 58376 | tf_op jit(solution)/shard_map/ppermute | solution.py:99
  146.9 6.7 %collective-permute-start.21 = (f32[1,2432]{1,0:T(1,128)S(1)}, f32[1,2432]{1,0:T(1,128)S(1)}, u32[]{:S(2)}, u32[]{:S(2)}) collective-permute-start(f32[1,2432]{1,0:T(1,128)S(1)} %constant_dynamic-slice_fusion), channel_id=1, source_target_pairs={{0,8},{2,10},{4,12},{6,14},{8,0},{10,2},{12,4},{14,6},{1,9},{3,11}... | collective-permute-start | bytes 29192 | tf_op jit(solution)/shard_map/ppermute | solution.py:99
  153.7 6.0 %collective-permute-start.14 = (f32[1,2432]{1,0:T(1,128)S(1)}, f32[1,2432]{1,0:T(1,128)S(1)}, u32[]{:S(2)}, u32[]{:S(2)}) collective-permute-start(f32[1,2432]{1,0:T(1,128)S(1)} %constant_dynamic-slice_fusion.7), channel_id=1, source_target_pairs={{0,64},{16,80},{32,96},{48,112},{64,0},{80,16},{96,32},{112,48},{1... | collective-permute-start | bytes 29192 | tf_op jit(solution)/shard_map/ppermute | solution.py:99
  159.7 3.4 %collective-permute-done.14 = f32[1,2432]{1,0:T(1,128)S(1)} collective-permute-done((f32[1,2432]{1,0:T(1,128)S(1)}, f32[1,2432]{1,0:T(1,128)S(1)}, u32[]{:S(2)}, u32[]{:S(2)}) %collective-permute-start.14) | collective-permute-done | bytes 9760 | tf_op jit(solution)/shard_map/ppermute | solution.py:99
  163.2 3.0 %collective-permute-start.22 = (f32[1,4864]{1,0:T(1,128)S(1)}, f32[1,4864]{1,0:T(1,128)S(1)}, u32[]{:S(2)}, u32[]{:S(2)}) collective-permute-start(f32[1,4864]{1,0:T(1,128)S(1)} %pad_maximum_fusion.53), channel_id=1, source_target_pairs={{0,128},{128,0},{256,384},{384,256},{1,129},{129,1},{257,385},{385... | collective-permute-start | bytes 58376 | tf_op jit(solution)/shard_map/ppermute | solution.py:99
  166.2 1.1 convolution_select_fusion
  167.8 1.2 collective-permute-done.22
  169.0 3.2 %collective-permute-start.23 = (f32[1,4864]{1,0:T(1,128)S(1)}, f32[1,4864]{1,0:T(1,128)S(1)}, u32[]{:S(2)}, u32[]{:S(2)}) collective-permute-start(f32[1,4864]{1,0:T(1,128)S(1)} %fusion.163), channel_id=1, source_target_pairs={{0,256},{128,384},{256,0},{384,128},{1,257},{129,385},{257,1},{385... | collective-permute-start | bytes 58376 | tf_op jit(solution)/shard_map/ppermute | solution.py:99
  172.2 1.4 fusion.26
  173.6 1.1 copy.80
  174.7 1.4 collective-permute-done.23
  (155 shorter events, 31.2 us)
Async XLA Ops:
  0.6 53.7 %copy-start = (bf16[3,3,256,128]{3,2,1,0:T(8,128)(2,1)S(1)}, bf16[3,3,256,128]{3,2,1,0:T(8,128)(2,1)}, u32[]{:S(2)}) copy-start(bf16[3,3,256,128]{3,2,1,0:T(8,128)(2,1)} %param.10) | copy-start | bytes 1769476
  0.6 2.3 %copy-start.1 = (bf16[1,1,32,32,256]{4,3,2,1,0:T(8,128)(2,1)S(1)}, bf16[1,1,32,32,256]{4,3,2,1,0:T(8,128)(2,1)}, u32[]{:S(2)}) copy-start(bf16[1,1,32,32,256]{4,3,2,1,0:T(8,128)(2,1)} %param.7) | copy-start | bytes 1572868
  3.0 26.1 %collective-permute-start = (bf16[4,4,640]{2,1,0:T(4,128)(2,1)S(1)}, bf16[4,4,640]{2,1,0:T(4,128)(2,1)S(1)}, u32[]{:S(2)}, u32[]{:S(2)}) collective-permute-start(bf16[4,4,640]{2,1,0:T(4,128)(2,1)S(1)} %get-tuple-element.26), channel_id=1, source_target_pairs={{0,5},{1,6},{2,7},{3,8},{4,9},{5,10},{6,11},{7,12},{8,13},{9,14},{... | collective-permute-start | bytes 61448 | tf_op jit(solution)/shard_map/ppermute | solution.py:21
  6.9 28.5 %collective-permute-start.7 = (bf16[4,4,640]{2,1,0:T(4,128)(2,1)S(1)}, bf16[4,4,640]{2,1,0:T(4,128)(2,1)S(1)}, u32[]{:S(2)}, u32[]{:S(2)}) collective-permute-start(bf16[4,4,640]{2,1,0:T(4,128)(2,1)S(1)} %get-tuple-element.27), channel_id=1, source_target_pairs={{0,123},{1,124},{2,125},{3,126},{4,127},{5,0},{6,1},{7,2},{8,3},{9... | collective-permute-start | bytes 61448 | tf_op jit(solution)/shard_map/ppermute | solution.py:21
  19.8 17.6 %collective-permute-start.5 = (bf16[4,4,640]{2,1,0:T(4,128)(2,1)S(1)}, bf16[4,4,640]{2,1,0:T(4,128)(2,1)S(1)}, u32[]{:S(2)}, u32[]{:S(2)}) collective-permute-start(bf16[4,4,640]{2,1,0:T(4,128)(2,1)S(1)} %get-tuple-element.28), channel_id=1, source_target_pairs={{0,125},{1,126},{2,127},{3,0},{4,1},{5,2},{6,3},{7,4},{8,5},{9,6},... | collective-permute-start | bytes 61448 | tf_op jit(solution)/shard_map/ppermute | solution.py:21
  23.6 22.1 %collective-permute-start.2 = (bf16[4,4,640]{2,1,0:T(4,128)(2,1)S(1)}, bf16[4,4,640]{2,1,0:T(4,128)(2,1)S(1)}, u32[]{:S(2)}, u32[]{:S(2)}) collective-permute-start(bf16[4,4,640]{2,1,0:T(4,128)(2,1)S(1)} %get-tuple-element.29), channel_id=1, source_target_pairs={{0,3},{1,4},{2,5},{3,6},{4,7},{5,8},{6,9},{7,10},{8,11},{9,12},{10... | collective-permute-start | bytes 61448 | tf_op jit(solution)/shard_map/ppermute | solution.py:21
  25.6 20.0 %collective-permute-start.3 = (bf16[32,4,640]{2,1,0:T(4,128)(2,1)S(1)}, bf16[32,4,640]{2,1,0:T(4,128)(2,1)S(1)}, u32[]{:S(2)}, u32[]{:S(2)}) collective-permute-start(bf16[32,4,640]{2,1,0:T(4,128)(2,1)S(1)} %get-tuple-element.32), channel_id=1, source_target_pairs={{0,1},{1,2},{2,3},{3,4},{4,5},{5,6},{6,7},{7,8},{8,9},{9,10},{10,1... | collective-permute-start | bytes 491528 | tf_op jit(solution)/shard_map/ppermute | solution.py:21
  29.1 16.6 %collective-permute-start.4 = (bf16[32,4,640]{2,1,0:T(4,128)(2,1)S(1)}, bf16[32,4,640]{2,1,0:T(4,128)(2,1)S(1)}, u32[]{:S(2)}, u32[]{:S(2)}) collective-permute-start(bf16[32,4,640]{2,1,0:T(4,128)(2,1)S(1)} %get-tuple-element.33), channel_id=1, source_target_pairs={{0,127},{1,0},{2,1},{3,2},{4,3},{5,4},{6,5},{7,6},{8,7},{9,8},{10,... | collective-permute-start | bytes 491528 | tf_op jit(solution)/shard_map/ppermute | solution.py:21
  35.5 12.5 %collective-permute-start.1 = (bf16[4,32,640]{2,1,0:T(8,128)(2,1)S(1)}, bf16[4,32,640]{2,1,0:T(8,128)(2,1)S(1)}, u32[]{:S(2)}, u32[]{:S(2)}) collective-permute-start(bf16[4,32,640]{2,1,0:T(8,128)(2,1)S(1)} %get-tuple-element.30), channel_id=1, source_target_pairs={{0,4},{1,5},{2,6},{3,7},{4,8},{5,9},{6,10},{7,11},{8,12},{9,13},{1... | collective-permute-start | bytes 491528 | tf_op jit(solution)/shard_map/ppermute | solution.py:21
  37.4 11.4 %collective-permute-start.6 = (bf16[4,32,640]{2,1,0:T(8,128)(2,1)S(1)}, bf16[4,32,640]{2,1,0:T(8,128)(2,1)S(1)}, u32[]{:S(2)}, u32[]{:S(2)}) collective-permute-start(bf16[4,32,640]{2,1,0:T(8,128)(2,1)S(1)} %get-tuple-element.31), channel_id=1, source_target_pairs={{0,124},{1,125},{2,126},{3,127},{4,0},{5,1},{6,2},{7,3},{8,4},{9,5... | collective-permute-start | bytes 491528 | tf_op jit(solution)/shard_map/ppermute | solution.py:21
  50.5 1.1 copy-start.11
  50.5 1.1 copy-start.13
  54.0 0.7 copy-start.10
  72.5 0.7 copy-start.12
  74.2 2.7 %copy-start.8 = (f32[1,256,128]{2,1,0:T(8,128)S(1)}, f32[1,256,128]{2,1,0:T(8,128)}, u32[]{:S(2)}) copy-start(f32[1,256,128]{2,1,0:T(8,128)} %convolution_bitcast_fusion.10) | copy-start | bytes 393220
  74.2 3.7 %copy-start.6 = (f32[1,256,128]{2,1,0:T(8,128)S(1)}, f32[1,256,128]{2,1,0:T(8,128)}, u32[]{:S(2)}) copy-start(f32[1,256,128]{2,1,0:T(8,128)} %convolution_bitcast_fusion.16) | copy-start | bytes 393220
  74.2 3.7 %copy-start.7 = (f32[1,256,128]{2,1,0:T(8,128)S(1)}, f32[1,256,128]{2,1,0:T(8,128)}, u32[]{:S(2)}) copy-start(f32[1,256,128]{2,1,0:T(8,128)} %convolution_bitcast_fusion.17) | copy-start | bytes 393220
  90.4 6.8 %collective-permute-start.15 = (f32[64,2432]{1,0:T(8,128)S(1)}, f32[64,2432]{1,0:T(8,128)S(1)}, u32[]{:S(2)}, u32[]{:S(2)}) collective-permute-start(f32[64,2432]{1,0:T(8,128)S(1)} %constant_dynamic-slice_fusion.6), channel_id=1, source_target_pairs={{0,1},{1,0},{2,3},{3,2},{4,5},{5,4},{6,7},{7,6},{8,9},{9,8},{10,11... | collective-permute-start | bytes 1867784 | tf_op jit(solution)/shard_map/ppermute | solution.py:99
  93.1 1.0 copy-start.5
  94.1 2.7 %copy-start.2 = (f32[32,8,5,256]{3,0,2,1:T(8,128)S(1)}, f32[32,8,5,256]{3,0,2,1:T(8,128)}, u32[]{:S(2)}) copy-start(f32[32,8,5,256]{3,0,2,1:T(8,128)} %copy.59) | copy-start | bytes 3932164
  94.1 2.7 %copy-start.9 = (f32[256]{0:T(256)S(1)}, f32[256]{0:T(256)}, u32[]{:S(2)}) copy-start(f32[256]{0:T(256)} %param.13) | copy-start | bytes 3076
  94.3 5.0 %collective-permute-start.8 = (f32[64,2432]{1,0:T(8,128)S(1)}, f32[64,2432]{1,0:T(8,128)S(1)}, u32[]{:S(2)}, u32[]{:S(2)}) collective-permute-start(f32[64,2432]{1,0:T(8,128)S(1)} %constant_dynamic-slice_fusion.13), channel_id=1, source_target_pairs={{0,1},{1,0},{2,3},{3,2},{4,5},{5,4},{6,7},{7,6},{8,9},{9,8},{10,11... | collective-permute-start | bytes 1867784 | tf_op jit(solution)/shard_map/ppermute | solution.py:99
  97.4 11.2 %collective-permute-start.16 = (f32[32,2432]{1,0:T(8,128)S(1)}, f32[32,2432]{1,0:T(8,128)S(1)}, u32[]{:S(2)}, u32[]{:S(2)}) collective-permute-start(f32[32,2432]{1,0:T(8,128)S(1)} %constant_dynamic-slice_fusion.5), channel_id=1, source_target_pairs={{0,16},{16,0},{32,48},{48,32},{64,80},{80,64},{96,112},{112,96},{1... | collective-permute-start | bytes 933896 | tf_op jit(solution)/shard_map/ppermute | solution.py:99
  99.4 11.2 %collective-permute-start.9 = (f32[32,2432]{1,0:T(8,128)S(1)}, f32[32,2432]{1,0:T(8,128)S(1)}, u32[]{:S(2)}, u32[]{:S(2)}) collective-permute-start(f32[32,2432]{1,0:T(8,128)S(1)} %constant_dynamic-slice_fusion.12), channel_id=1, source_target_pairs={{0,2},{2,0},{4,6},{6,4},{8,10},{10,8},{12,14},{14,12},{1,3},{3,1},... | collective-permute-start | bytes 933896 | tf_op jit(solution)/shard_map/ppermute | solution.py:99
  108.6 11.2 %collective-permute-start.17 = (f32[16,2432]{1,0:T(8,128)S(1)}, f32[16,2432]{1,0:T(8,128)S(1)}, u32[]{:S(2)}, u32[]{:S(2)}) collective-permute-start(f32[16,2432]{1,0:T(8,128)S(1)} %constant_dynamic-slice_fusion.4), channel_id=1, source_target_pairs={{0,32},{16,48},{32,0},{48,16},{64,96},{80,112},{96,64},{112,80},{1... | collective-permute-start | bytes 466952 | tf_op jit(solution)/shard_map/ppermute | solution.py:99
  110.6 55.5 %copy-start.4 = (bf16[36,1,7,4,128]{4,2,3,0,1:T(8,128)(2,1)S(1)}, bf16[36,1,7,4,128]{4,2,3,0,1:T(8,128)(2,1)}, u32[]{:S(2)}) copy-start(bf16[36,1,7,4,128]{4,2,3,0,1:T(8,128)(2,1)} %slice.183) | copy-start | bytes 774148
  110.7 15.3 %collective-permute-start.10 = (f32[16,2432]{1,0:T(8,128)S(1)}, f32[16,2432]{1,0:T(8,128)S(1)}, u32[]{:S(2)}, u32[]{:S(2)}) collective-permute-start(f32[16,2432]{1,0:T(8,128)S(1)} %constant_dynamic-slice_fusion.11), channel_id=1, source_target_pairs={{0,4},{2,6},{4,0},{6,2},{8,12},{10,14},{12,8},{14,10},{1,5},{3,7},... | collective-permute-start | bytes 466952 | tf_op jit(solution)/shard_map/ppermute | solution.py:99
  119.9 11.7 %collective-permute-start.18 = (f32[8,2432]{1,0:T(8,128)S(1)}, f32[8,2432]{1,0:T(8,128)S(1)}, u32[]{:S(2)}, u32[]{:S(2)}) collective-permute-start(f32[8,2432]{1,0:T(8,128)S(1)} %constant_dynamic-slice_fusion.3), channel_id=1, source_target_pairs={{0,64},{16,80},{32,96},{48,112},{64,0},{80,16},{96,32},{112,48},{1... | collective-permute-start | bytes 233480 | tf_op jit(solution)/shard_map/ppermute | solution.py:99
  126.0 11.3 %collective-permute-start.11 = (f32[8,2432]{1,0:T(8,128)S(1)}, f32[8,2432]{1,0:T(8,128)S(1)}, u32[]{:S(2)}, u32[]{:S(2)}) collective-permute-start(f32[8,2432]{1,0:T(8,128)S(1)} %constant_dynamic-slice_fusion.10), channel_id=1, source_target_pairs={{0,8},{2,10},{4,12},{6,14},{8,0},{10,2},{12,4},{14,6},{1,9},{3,11}... | collective-permute-start | bytes 233480 | tf_op jit(solution)/shard_map/ppermute | solution.py:99
  131.6 7.6 %collective-permute-start.19 = (f32[4,2432]{1,0:T(4,128)S(1)}, f32[4,2432]{1,0:T(4,128)S(1)}, u32[]{:S(2)}, u32[]{:S(2)}) collective-permute-start(f32[4,2432]{1,0:T(4,128)S(1)} %constant_dynamic-slice_fusion.2), channel_id=1, source_target_pairs={{0,2},{2,0},{4,6},{6,4},{8,10},{10,8},{12,14},{14,12},{1,3},{3,1},... | collective-permute-start | bytes 116744 | tf_op jit(solution)/shard_map/ppermute | solution.py:99
  137.3 5.9 %collective-permute-start.12 = (f32[4,2432]{1,0:T(4,128)S(1)}, f32[4,2432]{1,0:T(4,128)S(1)}, u32[]{:S(2)}, u32[]{:S(2)}) collective-permute-start(f32[4,2432]{1,0:T(4,128)S(1)} %constant_dynamic-slice_fusion.9), channel_id=1, source_target_pairs={{0,16},{16,0},{32,48},{48,32},{64,80},{80,64},{96,112},{112,96},{1... | collective-permute-start | bytes 116744 | tf_op jit(solution)/shard_map/ppermute | solution.py:99
  139.3 7.6 %collective-permute-start.20 = (f32[2,2432]{1,0:T(2,128)S(1)}, f32[2,2432]{1,0:T(2,128)S(1)}, u32[]{:S(2)}, u32[]{:S(2)}) collective-permute-start(f32[2,2432]{1,0:T(2,128)S(1)} %constant_dynamic-slice_fusion.1), channel_id=1, source_target_pairs={{0,4},{2,6},{4,0},{6,2},{8,12},{10,14},{12,8},{14,10},{1,5},{3,7},... | collective-permute-start | bytes 58376 | tf_op jit(solution)/shard_map/ppermute | solution.py:99
  143.2 10.4 %collective-permute-start.13 = (f32[2,2432]{1,0:T(2,128)S(1)}, f32[2,2432]{1,0:T(2,128)S(1)}, u32[]{:S(2)}, u32[]{:S(2)}) collective-permute-start(f32[2,2432]{1,0:T(2,128)S(1)} %constant_dynamic-slice_fusion.8), channel_id=1, source_target_pairs={{0,32},{16,48},{32,0},{48,16},{64,96},{80,112},{96,64},{112,80},{1... | collective-permute-start | bytes 58376 | tf_op jit(solution)/shard_map/ppermute | solution.py:99
  146.9 12.8 %collective-permute-start.21 = (f32[1,2432]{1,0:T(1,128)S(1)}, f32[1,2432]{1,0:T(1,128)S(1)}, u32[]{:S(2)}, u32[]{:S(2)}) collective-permute-start(f32[1,2432]{1,0:T(1,128)S(1)} %constant_dynamic-slice_fusion), channel_id=1, source_target_pairs={{0,8},{2,10},{4,12},{6,14},{8,0},{10,2},{12,4},{14,6},{1,9},{3,11}... | collective-permute-start | bytes 29192 | tf_op jit(solution)/shard_map/ppermute | solution.py:99
  153.7 9.5 %collective-permute-start.14 = (f32[1,2432]{1,0:T(1,128)S(1)}, f32[1,2432]{1,0:T(1,128)S(1)}, u32[]{:S(2)}, u32[]{:S(2)}) collective-permute-start(f32[1,2432]{1,0:T(1,128)S(1)} %constant_dynamic-slice_fusion.7), channel_id=1, source_target_pairs={{0,64},{16,80},{32,96},{48,112},{64,0},{80,16},{96,32},{112,48},{1... | collective-permute-start | bytes 29192 | tf_op jit(solution)/shard_map/ppermute | solution.py:99
  163.2 5.7 %collective-permute-start.22 = (f32[1,4864]{1,0:T(1,128)S(1)}, f32[1,4864]{1,0:T(1,128)S(1)}, u32[]{:S(2)}, u32[]{:S(2)}) collective-permute-start(f32[1,4864]{1,0:T(1,128)S(1)} %pad_maximum_fusion.53), channel_id=1, source_target_pairs={{0,128},{128,0},{256,384},{384,256},{1,129},{129,1},{257,385},{385... | collective-permute-start | bytes 58376 | tf_op jit(solution)/shard_map/ppermute | solution.py:99
  167.6 4.5 %copy-start.3 = (bf16[1,1,32,32,256]{4,3,2,1,0:T(8,128)(2,1)S(1)}, bf16[1,1,32,32,256]{4,3,2,1,0:T(8,128)(2,1)}, u32[]{:S(2)}) copy-start(bf16[1,1,32,32,256]{4,3,2,1,0:T(8,128)(2,1)} %param.9) | copy-start | bytes 1572868
  169.0 7.2 %collective-permute-start.23 = (f32[1,4864]{1,0:T(1,128)S(1)}, f32[1,4864]{1,0:T(1,128)S(1)}, u32[]{:S(2)}, u32[]{:S(2)}) collective-permute-start(f32[1,4864]{1,0:T(1,128)S(1)} %fusion.163), channel_id=1, source_target_pairs={{0,256},{128,384},{256,0},{384,128},{1,257},{129,385},{257,1},{385... | collective-permute-start | bytes 58376 | tf_op jit(solution)/shard_map/ppermute | solution.py:99

commit v6 on v4

--- a/solution.py
+++ b/solution.py
@@ -50,21 +50,22 @@
 def tap_sums(padded, grad_out):
     span_y = grad_out.shape[0]
     span_x = grad_out.shape[1]
-    flat_out = grad_out.reshape(span_y * span_x, grad_out.shape[2])
-    tap_rows = []
-    for tap_y in range(3):
-        tap_line = []
-        for tap_x in range(3):
-            window = padded[2 * tap_y : 2 * tap_y + span_y, 2 * tap_x : 2 * tap_x + span_x].reshape(
-                span_y * span_x, padded.shape[2]
-            )
-            tap_line.append(
-                lax.dot_general(
-                    window, flat_out, (((0,), (0,)), ((), ())), preferred_element_type=jnp.float32
-                )
-            )
-        tap_rows.append(jnp.stack(tap_line))
-    return jnp.stack(tap_rows)
+    cells = span_y * span_x
+    flat_out = grad_out.reshape(cells, grad_out.shape[2])
+    windows = [
+        padded[2 * tap_y : 2 * tap_y + span_y, 2 * tap_x : 2 * tap_x + span_x].reshape(
+            cells, padded.shape[2]
+        )
+        for tap_y in range(3)
+        for tap_x in range(3)
+    ]
+    summed = lax.dot_general(
+        jnp.concatenate(windows, axis=1),
+        flat_out,
+        (((0,), (0,)), ((), ())),
+        preferred_element_type=jnp.float32,
+    )
+    return summed.reshape(3, 3, padded.shape[2], grad_out.shape[2])
 
 
 def grid_halo(region, width):

time: 171 us -> 183 us (1.070)
  local copies, waits for them, and re-layouts: 21.5 us -> 40.6 us
  matrix products: 17.6 us -> 10.2 us
  waiting for transfers between devices: 33.5 us -> 29.1 us
  starting transfers between devices: 79.8 us -> 83 us
    unnamed x33 -> x92, local copies, waits for them, and re-layouts: 4.46 us -> 16.9 us
    dot_general x18 -> x2, matrix products: 11.6 us -> 3.13 us  [tap_sums(): lax.dot_general(jnp.concatenate(windows, axis=1), flat_out, (((0,), (0,))...]
    reshape x4 -> x0, local copies, waits for them, and re-layouts: 7.64 us -> none  [shard_rows(): split = grad.reshape((9,) + (2,) * bits + (per * grad.shape[-1],))]
    another operation x6 -> x0, other arithmetic: 5.47 us -> none  [tap_sums(): return jnp.stack(tap_rows)]
    dot_general x0 -> x2, local copies, waits for them, and re-layouts: none -> 5.18 us  [tap_sums(): lax.dot_general(jnp.concatenate(windows, axis=1), flat_out, (((0,), (0,))...]
    slice x2 -> x13, local copies, waits for them, and re-layouts: 0.32 us -> 4.31 us  [the longest x12 3.54 us: tap_sums(): padded[2 * tap_y:2 * tap_y + span_y, 2 * tap_x:2 * tap_x + span_x]]
    ppermute x4, waiting for transfers between devices: 9.34 us -> 5.79 us  [from_behind(): lax.ppermute(array, axis, [(i, (i + by) % length) for i in range(length)])]
    ppermute x16, starting transfers between devices: 54.5 us -> 57.6 us  [swap(): return lax.ppermute(value, axis, [(i, i ^ bit) for i in range(size)])]
  transfers between devices with their start and end apart: 20 -> 20, of which waited for: 13 -> 11; matrix products, arithmetic and copies ran while one was open for 5% -> 16% of each run, Pallas kernels for 0% -> 0%
where the time goes in v6:
time: 183 us; the launch traced here: 181 us
  starting transfers between devices  83 us (45%)
  local copies, waits for them, and re-layouts  40.6 us (22%)
  waiting for transfers between devices  29.1 us (16%)
  other arithmetic  16.2 us (9%)
  matrix products  10.2 us (6%)
  between operations  2.16 us (1%)
    ppermute x16, starting transfers between devices, swap(): return lax.ppermute(value, axis, [(i, i ^ bit) for i in range(size)])  57.6 us
    ppermute x4, starting transfers between devices, from_behind(): lax.ppermute(array, axis, [(i, (i + by) % length) for i in range(length)])  25.4 us
    ppermute x16, waiting for transfers between devices, swap(): return lax.ppermute(value, axis, [(i, i ^ bit) for i in range(size)])  23.3 us
    unnamed x92, local copies, waits for them, and re-layouts  16.9 us
    conv_general_dilated x4, matrix products, dilated(): lax.conv_general_dilated(padded[None], kernel, (1, 1), 'VALID', rhs_dilat...  7.12 us
    ppermute x4, waiting for transfers between devices, from_behind(): lax.ppermute(array, axis, [(i, (i + by) % length) for i in range(length)])  5.79 us
    dot_general x2, local copies, waits for them, and re-layouts, tap_sums(): lax.dot_general(jnp.concatenate(windows, axis=1), flat_out, (((0,), (0,))...  5.18 us
    concatenate x3, other arithmetic, grid_halo(): return jnp.concatenate([row_bands[0], widened, row_bands[1]], axis=0)  4.89 us
  transfers between devices with their start and end apart: 20, of which 11 were waited for; matrix products, arithmetic and copies ran while one was open for 16% of the time, Pallas kernels for 0%

profile of v6, /device:TPU:6, one launch (start us, length us, event | category | flops | bytes accessed | tf_op | source)
XLA Modules:
  0.0 181.3 jit_solution(17387783258412819016)
XLA Ops:
  1.6 1.3 copy.226
  2.9 2.1 %convert_reduce_fusion = (f32[256]{0:T(256)}, bf16[32,32,256]{2,0,1:T(8,128)(2,1)S(1)}) fusion(bf16[1,1,32,32,256]{4,3,2,1,0:T(8,128)(2,1)} %param.9, f32[32,32]{0,1:T(8,128)S(1)} %copy.159), kind=kLoop, calls=%fused_computation.45 | loop fusion | flops 1310464 | bytes 1053696 | tf_op jit(solution)/shard_map/reduce_sum | solution.py:194
  6.2 1.9 %collective-permute-start = (bf16[32,4,640]{2,0,1:T(8,128)(2,1)}, bf16[32,4,640]{2,0,1:T(8,128)(2,1)}, u32[]{:S(2)}, u32[]{:S(2)}) collective-permute-start(bf16[32,4,640]{2,0,1:T(8,128)(2,1)} %get-tuple-element.50), channel_id=1, source_target_pairs={{0,1},{1,2},{2,3},{3,4},{4,5},{5,6},{6,7},{7,8},{8,9},{9,10},{10,1... | collective-permute-start | bytes 491528 | tf_op jit(solution)/shard_map/ppermute | solution.py:21
  8.1 13.3 %collective-permute-start.1 = (bf16[32,4,640]{2,0,1:T(8,128)(2,1)}, bf16[32,4,640]{2,0,1:T(8,128)(2,1)}, u32[]{:S(2)}, u32[]{:S(2)}) collective-permute-start(bf16[32,4,640]{2,0,1:T(8,128)(2,1)} %get-tuple-element.51), channel_id=1, source_target_pairs={{0,127},{1,0},{2,1},{3,2},{4,3},{5,4},{6,5},{7,6},{8,7},{9,8},{10,... | collective-permute-start | bytes 491528 | tf_op jit(solution)/shard_map/ppermute | solution.py:21
  24.6 1.6 broadcast_select_fusion.2
  28.1 1.9 %collective-permute-start.2 = (bf16[4,40,640]{2,1,0:T(8,128)(2,1)}, bf16[4,40,640]{2,1,0:T(8,128)(2,1)}, u32[]{:S(2)}, u32[]{:S(2)}) collective-permute-start(bf16[4,40,640]{2,1,0:T(8,128)(2,1)} %get-tuple-element.46), channel_id=1, source_target_pairs={{0,4},{1,5},{2,6},{3,7},{4,8},{5,9},{6,10},{7,11},{8,12},{9,13},{1... | collective-permute-start | bytes 614408 | tf_op jit(solution)/shard_map/ppermute | solution.py:21
  30.3 1.5 reshape.167
  31.7 1.5 copy.206
  34.1 1.1 copy.185
  35.2 1.1 copy.186
  36.4 8.3 %collective-permute-start.3 = (bf16[4,40,640]{2,1,0:T(8,128)(2,1)S(1)}, bf16[4,40,640]{2,1,0:T(8,128)(2,1)S(1)}, u32[]{:S(2)}, u32[]{:S(2)}) collective-permute-start(bf16[4,40,640]{2,1,0:T(8,128)(2,1)S(1)} %copy-done.25), channel_id=1, source_target_pairs={{0,124},{1,125},{2,126},{3,127},{4,0},{5,1},{6,2},{7,3},{8,4},{9,5... | collective-permute-start | bytes 614408 | tf_op jit(solution)/shard_map/ppermute | solution.py:21
  44.7 1.5 pad_maximum_fusion.17
  46.3 4.2 %collective-permute-done.3 = bf16[4,40,640]{2,1,0:T(8,128)(2,1)S(1)} collective-permute-done((bf16[4,40,640]{2,1,0:T(8,128)(2,1)S(1)}, bf16[4,40,640]{2,1,0:T(8,128)(2,1)S(1)}, u32[]{:S(2)}, u32[]{:S(2)}) %collective-permute-start.3) | collective-permute-done | bytes 204832 | tf_op jit(solution)/shard_map/ppermute | solution.py:21
  50.5 1.6 pad_maximum_fusion.6
  52.3 1.7 pad_maximum_fusion.1
  56.2 3.1 %fusion.40 = (f32[36,8,5,128]{3,1,2,0:T(8,128)}, f32[36,8,5,128]{3,1,2,0:T(8,128)}, f32[36,8,5,128]{3,1,2,0:T(8,128)S(1)}) fusion(f32[128]{0:T(128)S(1)} %copy-done.27, bf16[3,3,256,128]{3,2,1,0:T(8,128)(2,1)S(1)} %copy-done, bf16[40,1,7,4,256]{4,2,3,0,1:T(8,128)(2,1)S(1)} %slice.162, bf16[40,1,8,5,256]{4,2,3,0,1:T(8,128)(2,1)S(1)} %copy.171, ...), kind=kOutput, calls=%fused_computation.54 | convolution fusion | flops 855982080 | bytes 4194856 | tf_op jit(solution)/shard_map/conv_general_dilated | solution.py:35
  61.2 1.9 %fusion.23 = f32[36,8,5,128]{3,1,2,0:T(8,128)S(1)} fusion(bf16[3,3,128,256]{3,2,1,0:T(8,128)(2,1)S(1)} %copy-done.28, bf16[40,1,7,4,256]{4,2,3,0,1:T(8,128)(2,1)S(1)} %slice.166, bf16[40,1,8,5,256]{4,2,3,0,1:T(8,128)(2,1)S(1)} %copy.179, pred[8,5]{0,1:T(8,128)(4,1)S(1)} %copy-done.31), kind=kOutput, calls=%fused_computation.31 | convolution fusion | flops 853954560 | bytes 2719784 | tf_op jit(solution)/shard_map/conv_general_dilated | solution.py:35
  67.2 1.5 fusion.86
  73.7 2.1 %collective-permute-start.4 = (f32[64,2432]{1,0:T(8,128)}, f32[64,2432]{1,0:T(8,128)}, u32[]{:S(2)}, u32[]{:S(2)}) collective-permute-start(f32[64,2432]{1,0:T(8,128)} %constant_dynamic-slice_fusion.13), channel_id=1, source_target_pairs={{0,1},{1,0},{2,3},{3,2},{4,5},{5,4},{6,7},{7,6},{8,9},{9,8},{10,11... | collective-permute-start | bytes 1867784 | tf_op jit(solution)/shard_map/ppermute | solution.py:95
  77.9 1.4 copy-done.12
  79.3 2.8 %copy.202 = bf16[1152,1024]{1,0:T(8,128)(2,1)S(1)} copy(bf16[1152,1024]{0,1:T(8,128)(2,1)} %bitcast.151) | data formatting | bytes 4718592 | tf_op jit(solution)/shard_map/dot_general | solution.py:62
  82.1 2.4 %dot_general.12 = bf16[9,2,2,2,2,2,2,2,1024]{8,7,6,5,4,3,2,1,0:T(2,128)(2,1)} reshape(bf16[1152,1024]{1,0:T(8,128)(2,1)S(1)} %copy.202) | data formatting | bytes 4718592 | tf_op jit(solution)/shard_map/dot_general | solution.py:62
  84.5 1.3 copy.172
  89.7 1.1 convolution_select_fusion
  93.6 1.7 fusion.4
  96.6 2.5 %collective-permute-start.11 = (f32[64,2432]{1,0:T(8,128)S(1)}, f32[64,2432]{1,0:T(8,128)S(1)}, u32[]{:S(2)}, u32[]{:S(2)}) collective-permute-start(f32[64,2432]{1,0:T(8,128)S(1)} %constant_dynamic-slice_fusion.6), channel_id=1, source_target_pairs={{0,1},{1,0},{2,3},{3,2},{4,5},{5,4},{6,7},{7,6},{8,9},{9,8},{10,11... | collective-permute-start | bytes 1867784 | tf_op jit(solution)/shard_map/ppermute | solution.py:95
  99.2 1.1 dynamic-slice_add_fusion.1
  100.4 1.9 %collective-permute-start.5 = (f32[32,2432]{1,0:T(8,128)S(1)}, f32[32,2432]{1,0:T(8,128)S(1)}, u32[]{:S(2)}, u32[]{:S(2)}) collective-permute-start(f32[32,2432]{1,0:T(8,128)S(1)} %constant_dynamic-slice_fusion.12), channel_id=1, source_target_pairs={{0,2},{2,0},{4,6},{6,4},{8,10},{10,8},{12,14},{14,12},{1,3},{3,1},... | collective-permute-start | bytes 933896 | tf_op jit(solution)/shard_map/ppermute | solution.py:95
  102.5 1.9 %collective-permute-start.12 = (f32[32,2432]{1,0:T(8,128)S(1)}, f32[32,2432]{1,0:T(8,128)S(1)}, u32[]{:S(2)}, u32[]{:S(2)}) collective-permute-start(f32[32,2432]{1,0:T(8,128)S(1)} %constant_dynamic-slice_fusion.5), channel_id=1, source_target_pairs={{0,16},{16,0},{32,48},{48,32},{64,80},{80,64},{96,112},{112,96},{1... | collective-permute-start | bytes 933896 | tf_op jit(solution)/shard_map/ppermute | solution.py:95
  104.4 7.2 %collective-permute-done.5 = f32[32,2432]{1,0:T(8,128)S(1)} collective-permute-done((f32[32,2432]{1,0:T(8,128)S(1)}, f32[32,2432]{1,0:T(8,128)S(1)}, u32[]{:S(2)}, u32[]{:S(2)}) %collective-permute-start.5) | collective-permute-done | bytes 311328 | tf_op jit(solution)/shard_map/ppermute | solution.py:95
  111.6 1.9 %collective-permute-start.6 = (f32[16,2432]{1,0:T(8,128)S(1)}, f32[16,2432]{1,0:T(8,128)S(1)}, u32[]{:S(2)}, u32[]{:S(2)}) collective-permute-start(f32[16,2432]{1,0:T(8,128)S(1)} %constant_dynamic-slice_fusion.11), channel_id=1, source_target_pairs={{0,4},{2,6},{4,0},{6,2},{8,12},{10,14},{12,8},{14,10},{1,5},{3,7},... | collective-permute-start | bytes 466952 | tf_op jit(solution)/shard_map/ppermute | solution.py:95
  113.7 3.4 %collective-permute-start.13 = (f32[16,2432]{1,0:T(8,128)S(1)}, f32[16,2432]{1,0:T(8,128)S(1)}, u32[]{:S(2)}, u32[]{:S(2)}) collective-permute-start(f32[16,2432]{1,0:T(8,128)S(1)} %constant_dynamic-slice_fusion.4), channel_id=1, source_target_pairs={{0,32},{16,48},{32,0},{48,16},{64,96},{80,112},{96,64},{112,80},{1... | collective-permute-start | bytes 466952 | tf_op jit(solution)/shard_map/ppermute | solution.py:95
  117.1 5.8 %collective-permute-done.6 = f32[16,2432]{1,0:T(8,128)S(1)} collective-permute-done((f32[16,2432]{1,0:T(8,128)S(1)}, f32[16,2432]{1,0:T(8,128)S(1)}, u32[]{:S(2)}, u32[]{:S(2)}) %collective-permute-start.6) | collective-permute-done | bytes 155680 | tf_op jit(solution)/shard_map/ppermute | solution.py:95
  122.9 1.9 %collective-permute-start.7 = (f32[8,2432]{1,0:T(8,128)S(1)}, f32[8,2432]{1,0:T(8,128)S(1)}, u32[]{:S(2)}, u32[]{:S(2)}) collective-permute-start(f32[8,2432]{1,0:T(8,128)S(1)} %constant_dynamic-slice_fusion.10), channel_id=1, source_target_pairs={{0,8},{2,10},{4,12},{6,14},{8,0},{10,2},{12,4},{14,6},{1,9},{3,11}... | collective-permute-start | bytes 233480 | tf_op jit(solution)/shard_map/ppermute | solution.py:95
  125.0 9.1 %collective-permute-start.14 = (f32[8,2432]{1,0:T(8,128)S(1)}, f32[8,2432]{1,0:T(8,128)S(1)}, u32[]{:S(2)}, u32[]{:S(2)}) collective-permute-start(f32[8,2432]{1,0:T(8,128)S(1)} %constant_dynamic-slice_fusion.3), channel_id=1, source_target_pairs={{0,64},{16,80},{32,96},{48,112},{64,0},{80,16},{96,32},{112,48},{1... | collective-permute-start | bytes 233480 | tf_op jit(solution)/shard_map/ppermute | solution.py:95
  134.2 3.4 %collective-permute-start.8 = (f32[4,2432]{1,0:T(4,128)S(1)}, f32[4,2432]{1,0:T(4,128)S(1)}, u32[]{:S(2)}, u32[]{:S(2)}) collective-permute-start(f32[4,2432]{1,0:T(4,128)S(1)} %constant_dynamic-slice_fusion.9), channel_id=1, source_target_pairs={{0,16},{16,0},{32,48},{48,32},{64,80},{80,64},{96,112},{112,96},{1... | collective-permute-start | bytes 116744 | tf_op jit(solution)/shard_map/ppermute | solution.py:95
  137.6 2.1 %collective-permute-start.15 = (f32[4,2432]{1,0:T(4,128)S(1)}, f32[4,2432]{1,0:T(4,128)S(1)}, u32[]{:S(2)}, u32[]{:S(2)}) collective-permute-start(f32[4,2432]{1,0:T(4,128)S(1)} %constant_dynamic-slice_fusion.2), channel_id=1, source_target_pairs={{0,2},{2,0},{4,6},{6,4},{8,10},{10,8},{12,14},{14,12},{1,3},{3,1},... | collective-permute-start | bytes 116744 | tf_op jit(solution)/shard_map/ppermute | solution.py:95
  140.5 4.0 %collective-permute-start.9 = (f32[2,2432]{1,0:T(2,128)S(1)}, f32[2,2432]{1,0:T(2,128)S(1)}, u32[]{:S(2)}, u32[]{:S(2)}) collective-permute-start(f32[2,2432]{1,0:T(2,128)S(1)} %constant_dynamic-slice_fusion.8), channel_id=1, source_target_pairs={{0,32},{16,48},{32,0},{48,16},{64,96},{80,112},{96,64},{112,80},{1... | collective-permute-start | bytes 58376 | tf_op jit(solution)/shard_map/ppermute | solution.py:95
  144.5 4.7 %collective-permute-start.16 = (f32[2,2432]{1,0:T(2,128)S(1)}, f32[2,2432]{1,0:T(2,128)S(1)}, u32[]{:S(2)}, u32[]{:S(2)}) collective-permute-start(f32[2,2432]{1,0:T(2,128)S(1)} %constant_dynamic-slice_fusion.1), channel_id=1, source_target_pairs={{0,4},{2,6},{4,0},{6,2},{8,12},{10,14},{12,8},{14,10},{1,5},{3,7},... | collective-permute-start | bytes 58376 | tf_op jit(solution)/shard_map/ppermute | solution.py:95
  149.3 7.9 %collective-permute-start.10 = (f32[1,2432]{1,0:T(1,128)S(1)}, f32[1,2432]{1,0:T(1,128)S(1)}, u32[]{:S(2)}, u32[]{:S(2)}) collective-permute-start(f32[1,2432]{1,0:T(1,128)S(1)} %constant_dynamic-slice_fusion.7), channel_id=1, source_target_pairs={{0,64},{16,80},{32,96},{48,112},{64,0},{80,16},{96,32},{112,48},{1... | collective-permute-start | bytes 29192 | tf_op jit(solution)/shard_map/ppermute | solution.py:95
  157.3 4.5 %collective-permute-start.17 = (f32[1,2432]{1,0:T(1,128)S(1)}, f32[1,2432]{1,0:T(1,128)S(1)}, u32[]{:S(2)}, u32[]{:S(2)}) collective-permute-start(f32[1,2432]{1,0:T(1,128)S(1)} %constant_dynamic-slice_fusion), channel_id=1, source_target_pairs={{0,8},{2,10},{4,12},{6,14},{8,0},{10,2},{12,4},{14,6},{1,9},{3,11}... | collective-permute-start | bytes 29192 | tf_op jit(solution)/shard_map/ppermute | solution.py:95
  161.9 4.9 %collective-permute-done.17 = f32[1,2432]{1,0:T(1,128)S(1)} collective-permute-done((f32[1,2432]{1,0:T(1,128)S(1)}, f32[1,2432]{1,0:T(1,128)S(1)}, u32[]{:S(2)}, u32[]{:S(2)}) %collective-permute-start.17) | collective-permute-done | bytes 9760 | tf_op jit(solution)/shard_map/ppermute | solution.py:95
  166.8 2.7 %collective-permute-start.18 = (f32[1,4864]{1,0:T(1,128)S(1)}, f32[1,4864]{1,0:T(1,128)S(1)}, u32[]{:S(2)}, u32[]{:S(2)}) collective-permute-start(f32[1,4864]{1,0:T(1,128)S(1)} %pad_maximum_fusion.26), channel_id=1, source_target_pairs={{0,128},{128,0},{256,384},{384,256},{1,129},{129,1},{257,385},{385... | collective-permute-start | bytes 58376 | tf_op jit(solution)/shard_map/ppermute | solution.py:95
  169.5 2.9 %collective-permute-done.18 = f32[1,4864]{1,0:T(1,128)S(1)} collective-permute-done((f32[1,4864]{1,0:T(1,128)S(1)}, f32[1,4864]{1,0:T(1,128)S(1)}, u32[]{:S(2)}, u32[]{:S(2)}) %collective-permute-start.18) | collective-permute-done | bytes 19488 | tf_op jit(solution)/shard_map/ppermute | solution.py:95
  172.5 3.3 %collective-permute-start.19 = (f32[1,4864]{1,0:T(1,128)S(1)}, f32[1,4864]{1,0:T(1,128)S(1)}, u32[]{:S(2)}, u32[]{:S(2)}) collective-permute-start(f32[1,4864]{1,0:T(1,128)S(1)} %fusion.79), channel_id=1, source_target_pairs={{0,256},{128,384},{256,0},{384,128},{1,257},{129,385},{257,1},{385... | collective-permute-start | bytes 58376 | tf_op jit(solution)/shard_map/ppermute | solution.py:95
  175.8 1.1 copy.207
  176.9 1.1 copy.208
  178.0 1.7 collective-permute-done.19
  (199 shorter events, 34.0 us)
Async XLA Ops:
  0.6 55.3 %copy-start = (bf16[3,3,256,128]{3,2,1,0:T(8,128)(2,1)S(1)}, bf16[3,3,256,128]{3,2,1,0:T(8,128)(2,1)}, u32[]{:S(2)}) copy-start(bf16[3,3,256,128]{3,2,1,0:T(8,128)(2,1)} %param.10) | copy-start | bytes 1769476
  2.9 2.5 %copy-start.7 = (bf16[1,1,32,32,256]{4,2,3,1,0:T(8,128)(2,1)}, bf16[1,1,32,32,256]{4,2,3,1,0:T(8,128)(2,1)S(1)}, u32[]{:S(2)}) copy-start(bf16[1,1,32,32,256]{4,2,3,1,0:T(8,128)(2,1)S(1)} %copy.226) | copy-start | bytes 1572868
  5.1 1.1 copy-start.5
  6.2 16.6 %collective-permute-start = (bf16[32,4,640]{2,0,1:T(8,128)(2,1)}, bf16[32,4,640]{2,0,1:T(8,128)(2,1)}, u32[]{:S(2)}, u32[]{:S(2)}) collective-permute-start(bf16[32,4,640]{2,0,1:T(8,128)(2,1)} %get-tuple-element.50), channel_id=1, source_target_pairs={{0,1},{1,2},{2,3},{3,4},{4,5},{5,6},{6,7},{7,8},{8,9},{9,10},{10,1... | collective-permute-start | bytes 491528 | tf_op jit(solution)/shard_map/ppermute | solution.py:21
  8.1 16.4 %collective-permute-start.1 = (bf16[32,4,640]{2,0,1:T(8,128)(2,1)}, bf16[32,4,640]{2,0,1:T(8,128)(2,1)}, u32[]{:S(2)}, u32[]{:S(2)}) collective-permute-start(bf16[32,4,640]{2,0,1:T(8,128)(2,1)} %get-tuple-element.51), channel_id=1, source_target_pairs={{0,127},{1,0},{2,1},{3,2},{4,3},{5,4},{6,5},{7,6},{8,7},{9,8},{10,... | collective-permute-start | bytes 491528 | tf_op jit(solution)/shard_map/ppermute | solution.py:21
  23.8 9.4 %copy-start.6 = (bf16[32,32,256]{2,0,1:T(8,128)(2,1)S(1)}, bf16[32,32,256]{2,0,1:T(8,128)(2,1)}, u32[]{:S(2)}) copy-start(bf16[32,32,256]{2,0,1:T(8,128)(2,1)} %copy-done.5) | copy-start | bytes 1572868
  23.9 9.4 %copy-start.8 = (bf16[1,1,32,32,256]{4,2,3,1,0:T(8,128)(2,1)S(1)}, bf16[1,1,32,32,256]{4,2,3,1,0:T(8,128)(2,1)}, u32[]{:S(2)}) copy-start(bf16[1,1,32,32,256]{4,2,3,1,0:T(8,128)(2,1)} %copy-done.7) | copy-start | bytes 1572868
  28.1 16.6 %collective-permute-start.2 = (bf16[4,40,640]{2,1,0:T(8,128)(2,1)}, bf16[4,40,640]{2,1,0:T(8,128)(2,1)}, u32[]{:S(2)}, u32[]{:S(2)}) collective-permute-start(bf16[4,40,640]{2,1,0:T(8,128)(2,1)} %get-tuple-element.46), channel_id=1, source_target_pairs={{0,4},{1,5},{2,6},{3,7},{4,8},{5,9},{6,10},{7,11},{8,12},{9,13},{1... | collective-permute-start | bytes 614408 | tf_op jit(solution)/shard_map/ppermute | solution.py:21
  34.1 2.3 %copy-start.25 = (bf16[4,40,640]{2,1,0:T(8,128)(2,1)S(1)}, bf16[4,40,640]{2,1,0:T(8,128)(2,1)}, u32[]{:S(2)}) copy-start(bf16[4,40,640]{2,1,0:T(8,128)(2,1)} %get-tuple-element.47) | copy-start | bytes 614404
  36.4 14.1 %collective-permute-start.3 = (bf16[4,40,640]{2,1,0:T(8,128)(2,1)S(1)}, bf16[4,40,640]{2,1,0:T(8,128)(2,1)S(1)}, u32[]{:S(2)}, u32[]{:S(2)}) collective-permute-start(bf16[4,40,640]{2,1,0:T(8,128)(2,1)S(1)} %copy-done.25), channel_id=1, source_target_pairs={{0,124},{1,125},{2,126},{3,127},{4,0},{5,1},{6,2},{7,3},{8,4},{9,5... | collective-permute-start | bytes 614408 | tf_op jit(solution)/shard_map/ppermute | solution.py:21
  54.0 1.3 copy-start.11
  60.1 1.1 copy-start.28
  60.3 4.5 %slice-start = ((s8[4718592]{0:T(1024)(128)(4,1)}), s8[4194304]{0:T(1024)(128)(4,1)S(1)}, s32[]{:S(2)}) async-start(s8[4718592]{0:T(1024)(128)(4,1)} %bitcast.137), calls=%async_computation | async-start | bytes 8388608
  61.2 3.6 %slice-start.1 = ((s8[4718592]{0:T(1024)(128)(4,1)}), s8[524288]{0:T(1024)(128)(4,1)S(1)}, s32[]{:S(2)}) async-start(s8[4718592]{0:T(1024)(128)(4,1)} %bitcast.137), calls=%async_computation.1 | async-start | bytes 1048576
  64.2 1.0 copy-start.20
  64.2 1.2 copy-start.19
  64.7 1.1 copy-start.15
  64.8 1.2 copy-start.9
  65.3 1.2 copy-start.14
  65.5 1.1 copy-start.18
  65.8 1.2 copy-start.17
  66.0 1.1 copy-start.16
  71.7 1.0 copy-start.3
  73.7 25.5 %collective-permute-start.4 = (f32[64,2432]{1,0:T(8,128)}, f32[64,2432]{1,0:T(8,128)}, u32[]{:S(2)}, u32[]{:S(2)}) collective-permute-start(f32[64,2432]{1,0:T(8,128)} %constant_dynamic-slice_fusion.13), channel_id=1, source_target_pairs={{0,1},{1,0},{2,3},{3,2},{4,5},{5,4},{6,7},{7,6},{8,9},{9,8},{10,11... | collective-permute-start | bytes 1867784 | tf_op jit(solution)/shard_map/ppermute | solution.py:95
  77.8 1.4 copy-start.12
  85.7 1.1 copy-start.29
  85.7 1.1 copy-start.30
  87.8 1.1 copy-start.23
  87.8 1.4 copy-start.2
  90.7 1.2 copy-start.21
  90.7 1.2 copy-start.26
  91.9 1.7 copy-start.13
  96.5 2.7 %copy-start.4 = (f32[128,2432]{1,0:T(8,128)S(1)}, f32[128,2432]{1,0:T(8,128)}, u32[]{:S(2)}) copy-start(f32[128,2432]{1,0:T(8,128)} %copy-done.3) | copy-start | bytes 3735556
  96.6 5.7 %collective-permute-start.11 = (f32[64,2432]{1,0:T(8,128)S(1)}, f32[64,2432]{1,0:T(8,128)S(1)}, u32[]{:S(2)}, u32[]{:S(2)}) collective-permute-start(f32[64,2432]{1,0:T(8,128)S(1)} %constant_dynamic-slice_fusion.6), channel_id=1, source_target_pairs={{0,1},{1,0},{2,3},{3,2},{4,5},{5,4},{6,7},{7,6},{8,9},{9,8},{10,11... | collective-permute-start | bytes 1867784 | tf_op jit(solution)/shard_map/ppermute | solution.py:95
  100.4 11.2 %collective-permute-start.5 = (f32[32,2432]{1,0:T(8,128)S(1)}, f32[32,2432]{1,0:T(8,128)S(1)}, u32[]{:S(2)}, u32[]{:S(2)}) collective-permute-start(f32[32,2432]{1,0:T(8,128)S(1)} %constant_dynamic-slice_fusion.12), channel_id=1, source_target_pairs={{0,2},{2,0},{4,6},{6,4},{8,10},{10,8},{12,14},{14,12},{1,3},{3,1},... | collective-permute-start | bytes 933896 | tf_op jit(solution)/shard_map/ppermute | solution.py:95
  102.5 11.2 %collective-permute-start.12 = (f32[32,2432]{1,0:T(8,128)S(1)}, f32[32,2432]{1,0:T(8,128)S(1)}, u32[]{:S(2)}, u32[]{:S(2)}) collective-permute-start(f32[32,2432]{1,0:T(8,128)S(1)} %constant_dynamic-slice_fusion.5), channel_id=1, source_target_pairs={{0,16},{16,0},{32,48},{48,32},{64,80},{80,64},{96,112},{112,96},{1... | collective-permute-start | bytes 933896 | tf_op jit(solution)/shard_map/ppermute | solution.py:95
  111.6 11.2 %collective-permute-start.6 = (f32[16,2432]{1,0:T(8,128)S(1)}, f32[16,2432]{1,0:T(8,128)S(1)}, u32[]{:S(2)}, u32[]{:S(2)}) collective-permute-start(f32[16,2432]{1,0:T(8,128)S(1)} %constant_dynamic-slice_fusion.11), channel_id=1, source_target_pairs={{0,4},{2,6},{4,0},{6,2},{8,12},{10,14},{12,8},{14,10},{1,5},{3,7},... | collective-permute-start | bytes 466952 | tf_op jit(solution)/shard_map/ppermute | solution.py:95
  113.7 11.2 %collective-permute-start.13 = (f32[16,2432]{1,0:T(8,128)S(1)}, f32[16,2432]{1,0:T(8,128)S(1)}, u32[]{:S(2)}, u32[]{:S(2)}) collective-permute-start(f32[16,2432]{1,0:T(8,128)S(1)} %constant_dynamic-slice_fusion.4), channel_id=1, source_target_pairs={{0,32},{16,48},{32,0},{48,16},{64,96},{80,112},{96,64},{112,80},{1... | collective-permute-start | bytes 466952 | tf_op jit(solution)/shard_map/ppermute | solution.py:95
  122.9 11.2 %collective-permute-start.7 = (f32[8,2432]{1,0:T(8,128)S(1)}, f32[8,2432]{1,0:T(8,128)S(1)}, u32[]{:S(2)}, u32[]{:S(2)}) collective-permute-start(f32[8,2432]{1,0:T(8,128)S(1)} %constant_dynamic-slice_fusion.10), channel_id=1, source_target_pairs={{0,8},{2,10},{4,12},{6,14},{8,0},{10,2},{12,4},{14,6},{1,9},{3,11}... | collective-permute-start | bytes 233480 | tf_op jit(solution)/shard_map/ppermute | solution.py:95
  125.0 12.6 %collective-permute-start.14 = (f32[8,2432]{1,0:T(8,128)S(1)}, f32[8,2432]{1,0:T(8,128)S(1)}, u32[]{:S(2)}, u32[]{:S(2)}) collective-permute-start(f32[8,2432]{1,0:T(8,128)S(1)} %constant_dynamic-slice_fusion.3), channel_id=1, source_target_pairs={{0,64},{16,80},{32,96},{48,112},{64,0},{80,16},{96,32},{112,48},{1... | collective-permute-start | bytes 233480 | tf_op jit(solution)/shard_map/ppermute | solution.py:95
  134.2 6.3 %collective-permute-start.8 = (f32[4,2432]{1,0:T(4,128)S(1)}, f32[4,2432]{1,0:T(4,128)S(1)}, u32[]{:S(2)}, u32[]{:S(2)}) collective-permute-start(f32[4,2432]{1,0:T(4,128)S(1)} %constant_dynamic-slice_fusion.9), channel_id=1, source_target_pairs={{0,16},{16,0},{32,48},{48,32},{64,80},{80,64},{96,112},{112,96},{1... | collective-permute-start | bytes 116744 | tf_op jit(solution)/shard_map/ppermute | solution.py:95
  137.6 6.9 %collective-permute-start.15 = (f32[4,2432]{1,0:T(4,128)S(1)}, f32[4,2432]{1,0:T(4,128)S(1)}, u32[]{:S(2)}, u32[]{:S(2)}) collective-permute-start(f32[4,2432]{1,0:T(4,128)S(1)} %constant_dynamic-slice_fusion.2), channel_id=1, source_target_pairs={{0,2},{2,0},{4,6},{6,4},{8,10},{10,8},{12,14},{14,12},{1,3},{3,1},... | collective-permute-start | bytes 116744 | tf_op jit(solution)/shard_map/ppermute | solution.py:95
  140.5 8.8 %collective-permute-start.9 = (f32[2,2432]{1,0:T(2,128)S(1)}, f32[2,2432]{1,0:T(2,128)S(1)}, u32[]{:S(2)}, u32[]{:S(2)}) collective-permute-start(f32[2,2432]{1,0:T(2,128)S(1)} %constant_dynamic-slice_fusion.8), channel_id=1, source_target_pairs={{0,32},{16,48},{32,0},{48,16},{64,96},{80,112},{96,64},{112,80},{1... | collective-permute-start | bytes 58376 | tf_op jit(solution)/shard_map/ppermute | solution.py:95
  144.5 12.7 %collective-permute-start.16 = (f32[2,2432]{1,0:T(2,128)S(1)}, f32[2,2432]{1,0:T(2,128)S(1)}, u32[]{:S(2)}, u32[]{:S(2)}) collective-permute-start(f32[2,2432]{1,0:T(2,128)S(1)} %constant_dynamic-slice_fusion.1), channel_id=1, source_target_pairs={{0,4},{2,6},{4,0},{6,2},{8,12},{10,14},{12,8},{14,10},{1,5},{3,7},... | collective-permute-start | bytes 58376 | tf_op jit(solution)/shard_map/ppermute | solution.py:95
  149.3 12.5 %collective-permute-start.10 = (f32[1,2432]{1,0:T(1,128)S(1)}, f32[1,2432]{1,0:T(1,128)S(1)}, u32[]{:S(2)}, u32[]{:S(2)}) collective-permute-start(f32[1,2432]{1,0:T(1,128)S(1)} %constant_dynamic-slice_fusion.7), channel_id=1, source_target_pairs={{0,64},{16,80},{32,96},{48,112},{64,0},{80,16},{96,32},{112,48},{1... | collective-permute-start | bytes 29192 | tf_op jit(solution)/shard_map/ppermute | solution.py:95
  157.3 9.5 %collective-permute-start.17 = (f32[1,2432]{1,0:T(1,128)S(1)}, f32[1,2432]{1,0:T(1,128)S(1)}, u32[]{:S(2)}, u32[]{:S(2)}) collective-permute-start(f32[1,2432]{1,0:T(1,128)S(1)} %constant_dynamic-slice_fusion), channel_id=1, source_target_pairs={{0,8},{2,10},{4,12},{6,14},{8,0},{10,2},{12,4},{14,6},{1,9},{3,11}... | collective-permute-start | bytes 29192 | tf_op jit(solution)/shard_map/ppermute | solution.py:95
  166.8 5.7 %collective-permute-start.18 = (f32[1,4864]{1,0:T(1,128)S(1)}, f32[1,4864]{1,0:T(1,128)S(1)}, u32[]{:S(2)}, u32[]{:S(2)}) collective-permute-start(f32[1,4864]{1,0:T(1,128)S(1)} %pad_maximum_fusion.26), channel_id=1, source_target_pairs={{0,128},{128,0},{256,384},{384,256},{1,129},{129,1},{257,385},{385... | collective-permute-start | bytes 58376 | tf_op jit(solution)/shard_map/ppermute | solution.py:95
  172.5 7.2 %collective-permute-start.19 = (f32[1,4864]{1,0:T(1,128)S(1)}, f32[1,4864]{1,0:T(1,128)S(1)}, u32[]{:S(2)}, u32[]{:S(2)}) collective-permute-start(f32[1,4864]{1,0:T(1,128)S(1)} %fusion.79), channel_id=1, source_target_pairs={{0,256},{128,384},{256,0},{384,128},{1,257},{129,385},{257,1},{385... | collective-permute-start | bytes 58376 | tf_op jit(solution)/shard_map/ppermute | solution.py:95
  (6 other events, 5.1 us)

commit v7 on v4

--- a/solution.py
+++ b/solution.py
@@ -122,8 +122,18 @@
 
 def reduce_shards(blocks, sizes):
     first, second = blocks
+    shared = 0
+    for step_a, step_b in zip(butterfly_steps(sizes, False), butterfly_steps(sizes, True)):
+        if step_a != step_b:
+            break
+        shared += 1
+    split = first.shape[1]
+    joined = jnp.concatenate([first, second], axis=1)
+    for axis, bit in butterfly_steps(sizes, False)[:shared]:
+        joined = halve(joined, axis, bit)
+    first, second = joined[:, :split], joined[:, split:]
     for (axis_a, bit_a), (axis_b, bit_b) in zip(
-        butterfly_steps(sizes, False), butterfly_steps(sizes, True)
+        butterfly_steps(sizes, False)[shared:], butterfly_steps(sizes, True)[shared:]
     ):
         first = halve(first, axis_a, bit_a)
         second = halve(second, axis_b, bit_b)

time: 171 us -> 165 us (0.965)
  starting transfers between devices: 79.8 us -> 63.7 us
  waiting for transfers between devices: 33.5 us -> 45.9 us
  other arithmetic: 15.4 us -> 12.6 us
    ppermute x16 -> x15, starting transfers between devices: 54.5 us -> 41.8 us  [swap(): return lax.ppermute(value, axis, [(i, i ^ bit) for i in range(size)])]
    ppermute x4, waiting for transfers between devices: 9.34 us -> 17.4 us  [from_behind(): lax.ppermute(array, axis, [(i, (i + by) % length) for i in range(length)])]
    unnamed x33 -> x59, local copies, waits for them, and re-layouts: 4.46 us -> 9.84 us
    another operation x6, other arithmetic: 5.47 us -> 0.35 us  [tap_sums(): return jnp.stack(tap_rows)]
    reshape x4, local copies, waits for them, and re-layouts: 7.64 us -> 3.16 us  [shard_rows(): split = grad.reshape((9,) + (2,) * bits + (per * grad.shape[-1],))]
    ppermute x16 -> x15, waiting for transfers between devices: 24.2 us -> 28.5 us  [swap(): return lax.ppermute(value, axis, [(i, i ^ bit) for i in range(size)])]
    ppermute x4, starting transfers between devices: 25.3 us -> 21.9 us  [from_behind(): lax.ppermute(array, axis, [(i, (i + by) % length) for i in range(length)])]
    conv_general_dilated x15, local copies, waits for them, and re-layouts: 4.25 us -> 2.26 us  [dilated(): lax.conv_general_dilated(padded[None], kernel, (1, 1), 'VALID', rhs_dilat...]
  transfers between devices with their start and end apart: 20 -> 19, of which waited for: 13 -> 16; matrix products, arithmetic and copies ran while one was open for 5% -> 5% of each run, Pallas kernels for 0% -> 0%
where the time goes in v7:
time: 165 us; the launch traced here: 163 us
  starting transfers between devices  63.7 us (39%)
  waiting for transfers between devices  45.9 us (28%)
  local copies, waits for them, and re-layouts  20.4 us (12%)
  matrix products  18.8 us (11%)
  other arithmetic  12.6 us (8%)
  between operations  2.01 us (1%)
    ppermute x15, starting transfers between devices, swap(): return lax.ppermute(value, axis, [(i, i ^ bit) for i in range(size)])  41.8 us
    ppermute x15, waiting for transfers between devices, swap(): return lax.ppermute(value, axis, [(i, i ^ bit) for i in range(size)])  28.5 us
    ppermute x4, starting transfers between devices, from_behind(): lax.ppermute(array, axis, [(i, (i + by) % length) for i in range(length)])  21.9 us
    ppermute x4, waiting for transfers between devices, from_behind(): lax.ppermute(array, axis, [(i, (i + by) % length) for i in range(length)])  17.4 us
    dot_general x18, matrix products, tap_sums(): lax.dot_general(window, flat_out, (((0,), (0,)), ((), ())), preferred_ele...  11.7 us
    unnamed x59, local copies, waits for them, and re-layouts  9.84 us
    conv_general_dilated x4, matrix products, dilated(): lax.conv_general_dilated(padded[None], kernel, (1, 1), 'VALID', rhs_dilat...  7.11 us
    concatenate x1, other arithmetic, grid_halo(): return jnp.concatenate([row_bands[0], widened, row_bands[1]], axis=0)  3.31 us
  transfers between devices with their start and end apart: 19, of which 16 were waited for; matrix products, arithmetic and copies ran while one was open for 5% of the time, Pallas kernels for 0%

profile of v7, /device:TPU:6, one launch (start us, length us, event | category | flops | bytes accessed | tf_op | source)
XLA Modules:
  0.0 163.4 jit_solution(4598097053141704742)
XLA Ops:
  1.5 1.3 convert_reduce_fusion
  3.1 13.3 %collective-permute-start.1 = (bf16[32,4,640]{2,1,0:T(4,128)(2,1)S(1)}, bf16[32,4,640]{2,1,0:T(4,128)(2,1)S(1)}, u32[]{:S(2)}, u32[]{:S(2)}) collective-permute-start(bf16[32,4,640]{2,1,0:T(4,128)(2,1)S(1)} %get-tuple-element.30), channel_id=1, source_target_pairs={{0,127},{1,0},{2,1},{3,2},{4,3},{5,4},{6,5},{7,6},{8,7},{9,8},{10,... | collective-permute-start | bytes 491528 | tf_op jit(solution)/shard_map/ppermute | solution.py:21
  16.4 1.9 %collective-permute-start = (bf16[32,4,640]{2,1,0:T(4,128)(2,1)S(1)}, bf16[32,4,640]{2,1,0:T(4,128)(2,1)S(1)}, u32[]{:S(2)}, u32[]{:S(2)}) collective-permute-start(bf16[32,4,640]{2,1,0:T(4,128)(2,1)S(1)} %get-tuple-element.29), channel_id=1, source_target_pairs={{0,1},{1,2},{2,3},{3,4},{4,5},{5,6},{6,7},{7,8},{8,9},{9,10},{10,1... | collective-permute-start | bytes 491528 | tf_op jit(solution)/shard_map/ppermute | solution.py:21
  19.3 7.1 %collective-permute-done = bf16[32,4,640]{2,1,0:T(4,128)(2,1)S(1)} collective-permute-done((bf16[32,4,640]{2,1,0:T(4,128)(2,1)S(1)}, bf16[32,4,640]{2,1,0:T(4,128)(2,1)S(1)}, u32[]{:S(2)}, u32[]{:S(2)}) %collective-permute-start) | collective-permute-done | bytes 163872 | tf_op jit(solution)/shard_map/ppermute | solution.py:21
  26.6 1.9 %collective-permute-start.3 = (bf16[4,40,640]{2,1,0:T(8,128)(2,1)S(1)}, bf16[4,40,640]{2,1,0:T(8,128)(2,1)S(1)}, u32[]{:S(2)}, u32[]{:S(2)}) collective-permute-start(bf16[4,40,640]{2,1,0:T(8,128)(2,1)S(1)} %get-tuple-element.28), channel_id=1, source_target_pairs={{0,124},{1,125},{2,126},{3,127},{4,0},{5,1},{6,2},{7,3},{8,4},{9,5... | collective-permute-start | bytes 614408 | tf_op jit(solution)/shard_map/ppermute | solution.py:21
  29.4 4.8 %collective-permute-start.2 = (bf16[4,40,640]{2,1,0:T(8,128)(2,1)S(1)}, bf16[4,40,640]{2,1,0:T(8,128)(2,1)S(1)}, u32[]{:S(2)}, u32[]{:S(2)}) collective-permute-start(bf16[4,40,640]{2,1,0:T(8,128)(2,1)S(1)} %get-tuple-element.27), channel_id=1, source_target_pairs={{0,4},{1,5},{2,6},{3,7},{4,8},{5,9},{6,10},{7,11},{8,12},{9,13},{1... | collective-permute-start | bytes 614408 | tf_op jit(solution)/shard_map/ppermute | solution.py:21
  34.2 1.0 collective-permute-done.3
  35.3 8.4 %collective-permute-done.2 = bf16[4,40,640]{2,1,0:T(8,128)(2,1)S(1)} collective-permute-done((bf16[4,40,640]{2,1,0:T(8,128)(2,1)S(1)}, bf16[4,40,640]{2,1,0:T(8,128)(2,1)S(1)}, u32[]{:S(2)}, u32[]{:S(2)}) %collective-permute-start.2) | collective-permute-done | bytes 204832 | tf_op jit(solution)/shard_map/ppermute | solution.py:21
  43.7 3.3 %pad_maximum_fusion.2 = (bf16[40,40,256]{2,1,0:T(8,128)(2,1)S(1)}, bf16[40,40,256]{2,1,0:T(8,128)(2,1)S(1)}) fusion(bf16[4,40,640]{2,1,0:T(8,128)(2,1)S(1)} %broadcast_select_fusion, bf16[4,40,640]{2,1,0:T(8,128)(2,1)S(1)} %broadcast_select_fusion.1, bf16[32,4,640]{2,1,0:T(4,128)(2,1)S(1)} %broadcast_select_fusion.2, ...), kind=kLoop, calls=%fused_computation.67 | loop fusion | flops 11468800 | bytes 3686400 | tf_op jit(solution)/shard_map/concatenate | solution.py:89
  49.0 1.9 %fusion.21 = f32[36,8,5,128]{3,1,2,0:T(8,128)S(1)} fusion(bf16[3,3,128,256]{3,2,1,0:T(8,128)(2,1)S(1)} %copy-done.23, bf16[40,1,7,4,256]{4,2,3,0,1:T(8,128)(2,1)S(1)} %slice.172, bf16[40,1,8,5,256]{4,2,3,0,1:T(8,128)(2,1)S(1)} %copy.62, pred[8,5]{0,1:T(8,128)(4,1)S(1)} %copy-done.26), kind=kOutput, calls=%fused_computation.33 | convolution fusion | flops 853954560 | bytes 2719784 | tf_op jit(solution)/shard_map/conv_general_dilated | solution.py:35
  51.6 3.1 %fusion.37 = (f32[36,8,5,128]{3,1,2,0:T(8,128)}, f32[36,8,5,128]{3,1,2,0:T(8,128)}, f32[36,8,5,128]{3,1,2,0:T(8,128)S(1)}) fusion(f32[128]{0:T(128)S(1)} %copy-done.22, bf16[3,3,256,128]{3,2,1,0:T(8,128)(2,1)S(1)} %copy-done, bf16[40,1,7,4,256]{4,2,3,0,1:T(8,128)(2,1)S(1)} %slice.168, bf16[40,1,8,5,256]{4,2,3,0,1:T(8,128)(2,1)S(1)} %copy.55, ...), kind=kOutput, calls=%fused_computation.77 | convolution fusion | flops 855982080 | bytes 4194856 | tf_op jit(solution)/shard_map/conv_general_dilated | solution.py:35
  59.3 0.9 convolution_bitcast_fusion
  60.2 0.9 convolution_bitcast_fusion.1
  63.9 0.9 convolution_bitcast_fusion.8
  64.9 0.9 convolution_bitcast_fusion.3
  66.7 0.9 convolution_bitcast_fusion.5
  69.0 1.0 reshape.99
  70.9 2.0 %copy.89 = f32[16,8,9,256]{3,1,2,0:T(8,128)} copy(f32[16,8,9,256]{3,2,1,0:T(8,128)S(1)} %bitcast.205) | data formatting | bytes 2359296
  74.6 0.9 copy.90
  76.6 1.1 fusion.18
  78.1 1.9 %collective-permute-start.4 = (f32[64,4864]{1,0:T(8,128)}, f32[64,4864]{1,0:T(8,128)}, u32[]{:S(2)}, u32[]{:S(2)}) collective-permute-start(f32[64,4864]{1,0:T(8,128)} %fusion.18), channel_id=1, source_target_pairs={{0,1},{1,0},{2,3},{3,2},{4,5},{5,4},{6,7},{7,6},{8,9},{9,8},{10,11... | collective-permute-start | bytes 3735560 | tf_op jit(solution)/shard_map/ppermute | solution.py:94
  81.9 1.0 convolution_select_fusion.1
  86.9 1.4 fusion.20
  88.5 1.9 %collective-permute-start.11 = (f32[32,2432]{1,0:T(8,128)S(1)}, f32[32,2432]{1,0:T(8,128)S(1)}, u32[]{:S(2)}, u32[]{:S(2)}) collective-permute-start(f32[32,2432]{1,0:T(8,128)S(1)} %constant_dynamic-slice_fusion.5), channel_id=1, source_target_pairs={{0,16},{16,0},{32,48},{48,32},{64,80},{80,64},{96,112},{112,96},{1... | collective-permute-start | bytes 933896 | tf_op jit(solution)/shard_map/ppermute | solution.py:94
  90.5 4.7 %collective-permute-start.5 = (f32[32,2432]{1,0:T(8,128)S(1)}, f32[32,2432]{1,0:T(8,128)S(1)}, u32[]{:S(2)}, u32[]{:S(2)}) collective-permute-start(f32[32,2432]{1,0:T(8,128)S(1)} %constant_dynamic-slice_fusion.11), channel_id=1, source_target_pairs={{0,2},{2,0},{4,6},{6,4},{8,10},{10,8},{12,14},{14,12},{1,3},{3,1},... | collective-permute-start | bytes 933896 | tf_op jit(solution)/shard_map/ppermute | solution.py:94
  95.2 5.0 %collective-permute-done.11 = f32[32,2432]{1,0:T(8,128)S(1)} collective-permute-done((f32[32,2432]{1,0:T(8,128)S(1)}, f32[32,2432]{1,0:T(8,128)S(1)}, u32[]{:S(2)}, u32[]{:S(2)}) %collective-permute-start.11) | collective-permute-done | bytes 311328 | tf_op jit(solution)/shard_map/ppermute | solution.py:94
  100.2 1.9 %collective-permute-start.12 = (f32[16,2432]{1,0:T(8,128)S(1)}, f32[16,2432]{1,0:T(8,128)S(1)}, u32[]{:S(2)}, u32[]{:S(2)}) collective-permute-start(f32[16,2432]{1,0:T(8,128)S(1)} %constant_dynamic-slice_fusion.4), channel_id=1, source_target_pairs={{0,32},{16,48},{32,0},{48,16},{64,96},{80,112},{96,64},{112,80},{1... | collective-permute-start | bytes 466952 | tf_op jit(solution)/shard_map/ppermute | solution.py:94
  103.1 1.9 %collective-permute-start.6 = (f32[16,2432]{1,0:T(8,128)S(1)}, f32[16,2432]{1,0:T(8,128)S(1)}, u32[]{:S(2)}, u32[]{:S(2)}) collective-permute-start(f32[16,2432]{1,0:T(8,128)S(1)} %constant_dynamic-slice_fusion.10), channel_id=1, source_target_pairs={{0,4},{2,6},{4,0},{6,2},{8,12},{10,14},{12,8},{14,10},{1,5},{3,7},... | collective-permute-start | bytes 466952 | tf_op jit(solution)/shard_map/ppermute | solution.py:94
  105.0 6.9 %collective-permute-done.12 = f32[16,2432]{1,0:T(8,128)S(1)} collective-permute-done((f32[16,2432]{1,0:T(8,128)S(1)}, f32[16,2432]{1,0:T(8,128)S(1)}, u32[]{:S(2)}, u32[]{:S(2)}) %collective-permute-start.12) | collective-permute-done | bytes 155680 | tf_op jit(solution)/shard_map/ppermute | solution.py:94
  112.0 1.9 %collective-permute-start.13 = (f32[8,2432]{1,0:T(8,128)S(1)}, f32[8,2432]{1,0:T(8,128)S(1)}, u32[]{:S(2)}, u32[]{:S(2)}) collective-permute-start(f32[8,2432]{1,0:T(8,128)S(1)} %constant_dynamic-slice_fusion.3), channel_id=1, source_target_pairs={{0,64},{16,80},{32,96},{48,112},{64,0},{80,16},{96,32},{112,48},{1... | collective-permute-start | bytes 233480 | tf_op jit(solution)/shard_map/ppermute | solution.py:94
  113.9 1.1 collective-permute-done.6
  115.0 1.9 %collective-permute-start.7 = (f32[8,2432]{1,0:T(8,128)S(1)}, f32[8,2432]{1,0:T(8,128)S(1)}, u32[]{:S(2)}, u32[]{:S(2)}) collective-permute-start(f32[8,2432]{1,0:T(8,128)S(1)} %constant_dynamic-slice_fusion.9), channel_id=1, source_target_pairs={{0,8},{2,10},{4,12},{6,14},{8,0},{10,2},{12,4},{14,6},{1,9},{3,11}... | collective-permute-start | bytes 233480 | tf_op jit(solution)/shard_map/ppermute | solution.py:94
  116.9 5.2 %collective-permute-done.13 = f32[8,2432]{1,0:T(8,128)S(1)} collective-permute-done((f32[8,2432]{1,0:T(8,128)S(1)}, f32[8,2432]{1,0:T(8,128)S(1)}, u32[]{:S(2)}, u32[]{:S(2)}) %collective-permute-start.13) | collective-permute-done | bytes 77856 | tf_op jit(solution)/shard_map/ppermute | solution.py:94
  122.2 4.4 %collective-permute-start.14 = (f32[4,2432]{1,0:T(4,128)S(1)}, f32[4,2432]{1,0:T(4,128)S(1)}, u32[]{:S(2)}, u32[]{:S(2)}) collective-permute-start(f32[4,2432]{1,0:T(4,128)S(1)} %constant_dynamic-slice_fusion.2), channel_id=1, source_target_pairs={{0,2},{2,0},{4,6},{6,4},{8,10},{10,8},{12,14},{14,12},{1,3},{3,1},... | collective-permute-start | bytes 116744 | tf_op jit(solution)/shard_map/ppermute | solution.py:94
  126.7 2.3 %collective-permute-start.8 = (f32[4,2432]{1,0:T(4,128)S(1)}, f32[4,2432]{1,0:T(4,128)S(1)}, u32[]{:S(2)}, u32[]{:S(2)}) collective-permute-start(f32[4,2432]{1,0:T(4,128)S(1)} %constant_dynamic-slice_fusion.8), channel_id=1, source_target_pairs={{0,16},{16,0},{32,48},{48,32},{64,80},{80,64},{96,112},{112,96},{1... | collective-permute-start | bytes 116744 | tf_op jit(solution)/shard_map/ppermute | solution.py:94
  129.1 1.9 %collective-permute-start.15 = (f32[2,2432]{1,0:T(2,128)S(1)}, f32[2,2432]{1,0:T(2,128)S(1)}, u32[]{:S(2)}, u32[]{:S(2)}) collective-permute-start(f32[2,2432]{1,0:T(2,128)S(1)} %constant_dynamic-slice_fusion.1), channel_id=1, source_target_pairs={{0,4},{2,6},{4,0},{6,2},{8,12},{10,14},{12,8},{14,10},{1,5},{3,7},... | collective-permute-start | bytes 58376 | tf_op jit(solution)/shard_map/ppermute | solution.py:94
  131.0 1.5 collective-permute-done.8
  132.6 2.6 %collective-permute-start.9 = (f32[2,2432]{1,0:T(2,128)S(1)}, f32[2,2432]{1,0:T(2,128)S(1)}, u32[]{:S(2)}, u32[]{:S(2)}) collective-permute-start(f32[2,2432]{1,0:T(2,128)S(1)} %constant_dynamic-slice_fusion.7), channel_id=1, source_target_pairs={{0,32},{16,48},{32,0},{48,16},{64,96},{80,112},{96,64},{112,80},{1... | collective-permute-start | bytes 58376 | tf_op jit(solution)/shard_map/ppermute | solution.py:94
  135.7 2.8 %collective-permute-start.16 = (f32[1,2432]{1,0:T(1,128)S(1)}, f32[1,2432]{1,0:T(1,128)S(1)}, u32[]{:S(2)}, u32[]{:S(2)}) collective-permute-start(f32[1,2432]{1,0:T(1,128)S(1)} %constant_dynamic-slice_fusion), channel_id=1, source_target_pairs={{0,8},{2,10},{4,12},{6,14},{8,0},{10,2},{12,4},{14,6},{1,9},{3,11}... | collective-permute-start | bytes 29192 | tf_op jit(solution)/shard_map/ppermute | solution.py:94
  139.3 5.5 %collective-permute-start.10 = (f32[1,2432]{1,0:T(1,128)S(1)}, f32[1,2432]{1,0:T(1,128)S(1)}, u32[]{:S(2)}, u32[]{:S(2)}) collective-permute-start(f32[1,2432]{1,0:T(1,128)S(1)} %constant_dynamic-slice_fusion.6), channel_id=1, source_target_pairs={{0,64},{16,80},{32,96},{48,112},{64,0},{80,16},{96,32},{112,48},{1... | collective-permute-start | bytes 29192 | tf_op jit(solution)/shard_map/ppermute | solution.py:94
  145.2 3.6 %collective-permute-done.10 = f32[1,2432]{1,0:T(1,128)S(1)} collective-permute-done((f32[1,2432]{1,0:T(1,128)S(1)}, f32[1,2432]{1,0:T(1,128)S(1)}, u32[]{:S(2)}, u32[]{:S(2)}) %collective-permute-start.10) | collective-permute-done | bytes 9760 | tf_op jit(solution)/shard_map/ppermute | solution.py:94
  148.8 2.7 %collective-permute-start.17 = (f32[1,4864]{1,0:T(1,128)S(1)}, f32[1,4864]{1,0:T(1,128)S(1)}, u32[]{:S(2)}, u32[]{:S(2)}) collective-permute-start(f32[1,4864]{1,0:T(1,128)S(1)} %pad_maximum_fusion.49), channel_id=1, source_target_pairs={{0,128},{128,0},{256,384},{384,256},{1,129},{129,1},{257,385},{385... | collective-permute-start | bytes 58376 | tf_op jit(solution)/shard_map/ppermute | solution.py:94
  151.6 1.1 convolution_select_fusion
  153.2 1.3 collective-permute-done.17
  154.5 3.3 %collective-permute-start.18 = (f32[1,4864]{1,0:T(1,128)S(1)}, f32[1,4864]{1,0:T(1,128)S(1)}, u32[]{:S(2)}, u32[]{:S(2)}) collective-permute-start(f32[1,4864]{1,0:T(1,128)S(1)} %fusion.142), channel_id=1, source_target_pairs={{0,256},{128,384},{256,0},{384,128},{1,257},{129,385},{257,1},{385... | collective-permute-start | bytes 58376 | tf_op jit(solution)/shard_map/ppermute | solution.py:94
  157.9 1.4 fusion.29
  159.3 1.1 copy.80
  160.3 1.4 collective-permute-done.18
  (164 shorter events, 29.8 us)
Async XLA Ops:
  0.6 50.6 %copy-start = (bf16[3,3,256,128]{3,2,1,0:T(8,128)(2,1)S(1)}, bf16[3,3,256,128]{3,2,1,0:T(8,128)(2,1)}, u32[]{:S(2)}) copy-start(bf16[3,3,256,128]{3,2,1,0:T(8,128)(2,1)} %param.10) | copy-start | bytes 1769476
  0.6 2.3 %copy-start.1 = (bf16[1,1,32,32,256]{4,3,2,1,0:T(8,128)(2,1)S(1)}, bf16[1,1,32,32,256]{4,3,2,1,0:T(8,128)(2,1)}, u32[]{:S(2)}) copy-start(bf16[1,1,32,32,256]{4,3,2,1,0:T(8,128)(2,1)} %param.7) | copy-start | bytes 1572868
  3.1 16.1 %collective-permute-start.1 = (bf16[32,4,640]{2,1,0:T(4,128)(2,1)S(1)}, bf16[32,4,640]{2,1,0:T(4,128)(2,1)S(1)}, u32[]{:S(2)}, u32[]{:S(2)}) collective-permute-start(bf16[32,4,640]{2,1,0:T(4,128)(2,1)S(1)} %get-tuple-element.30), channel_id=1, source_target_pairs={{0,127},{1,0},{2,1},{3,2},{4,3},{5,4},{6,5},{7,6},{8,7},{9,8},{10,... | collective-permute-start | bytes 491528 | tf_op jit(solution)/shard_map/ppermute | solution.py:21
  16.4 10.0 %collective-permute-start = (bf16[32,4,640]{2,1,0:T(4,128)(2,1)S(1)}, bf16[32,4,640]{2,1,0:T(4,128)(2,1)S(1)}, u32[]{:S(2)}, u32[]{:S(2)}) collective-permute-start(bf16[32,4,640]{2,1,0:T(4,128)(2,1)S(1)} %get-tuple-element.29), channel_id=1, source_target_pairs={{0,1},{1,2},{2,3},{3,4},{4,5},{5,6},{6,7},{7,8},{8,9},{9,10},{10,1... | collective-permute-start | bytes 491528 | tf_op jit(solution)/shard_map/ppermute | solution.py:21
  26.6 8.7 %collective-permute-start.3 = (bf16[4,40,640]{2,1,0:T(8,128)(2,1)S(1)}, bf16[4,40,640]{2,1,0:T(8,128)(2,1)S(1)}, u32[]{:S(2)}, u32[]{:S(2)}) collective-permute-start(bf16[4,40,640]{2,1,0:T(8,128)(2,1)S(1)} %get-tuple-element.28), channel_id=1, source_target_pairs={{0,124},{1,125},{2,126},{3,127},{4,0},{5,1},{6,2},{7,3},{8,4},{9,5... | collective-permute-start | bytes 614408 | tf_op jit(solution)/shard_map/ppermute | solution.py:21
  29.4 14.3 %collective-permute-start.2 = (bf16[4,40,640]{2,1,0:T(8,128)(2,1)S(1)}, bf16[4,40,640]{2,1,0:T(8,128)(2,1)S(1)}, u32[]{:S(2)}, u32[]{:S(2)}) collective-permute-start(bf16[4,40,640]{2,1,0:T(8,128)(2,1)S(1)} %get-tuple-element.27), channel_id=1, source_target_pairs={{0,4},{1,5},{2,6},{3,7},{4,8},{5,9},{6,10},{7,11},{8,12},{9,13},{1... | collective-permute-start | bytes 614408 | tf_op jit(solution)/shard_map/ppermute | solution.py:21
  48.0 1.1 copy-start.23
  48.0 1.1 copy-start.26
  51.0 0.7 copy-start.22
  51.6 3.8 %copy-start.4 = (f32[36,1,36,128]{3,0,2,1:T(8,128)}, f32[36,1,36,128]{3,0,2,1:T(8,128)S(1)}, u32[]{:S(2)}) copy-start(f32[36,1,36,128]{3,0,2,1:T(8,128)S(1)} %slice.173) | copy-start | bytes 1990660
  70.8 2.1 %copy-start.14 = (f32[1,128,256]{2,1,0:T(8,128)S(1)}, f32[1,128,256]{2,1,0:T(8,128)}, u32[]{:S(2)}) copy-start(f32[1,128,256]{2,1,0:T(8,128)} %convolution_bitcast_fusion.1) | copy-start | bytes 393220
  70.8 2.1 %copy-start.15 = (f32[1,128,256]{2,1,0:T(8,128)S(1)}, f32[1,128,256]{2,1,0:T(8,128)}, u32[]{:S(2)}) copy-start(f32[1,128,256]{2,1,0:T(8,128)} %convolution_bitcast_fusion.2) | copy-start | bytes 393220
  70.8 2.1 %copy-start.20 = (f32[1,128,256]{2,1,0:T(8,128)S(1)}, f32[1,128,256]{2,1,0:T(8,128)}, u32[]{:S(2)}) copy-start(f32[1,128,256]{2,1,0:T(8,128)} %convolution_bitcast_fusion) | copy-start | bytes 393220
  70.8 2.1 %copy-start.10 = (f32[1,128,256]{2,1,0:T(8,128)S(1)}, f32[1,128,256]{2,1,0:T(8,128)}, u32[]{:S(2)}) copy-start(f32[1,128,256]{2,1,0:T(8,128)} %convolution_bitcast_fusion.7) | copy-start | bytes 393220
  70.8 2.1 %copy-start.11 = (f32[1,128,256]{2,1,0:T(8,128)S(1)}, f32[1,128,256]{2,1,0:T(8,128)}, u32[]{:S(2)}) copy-start(f32[1,128,256]{2,1,0:T(8,128)} %convolution_bitcast_fusion.8) | copy-start | bytes 393220
  70.8 2.1 %copy-start.12 = (f32[1,128,256]{2,1,0:T(8,128)S(1)}, f32[1,128,256]{2,1,0:T(8,128)}, u32[]{:S(2)}) copy-start(f32[1,128,256]{2,1,0:T(8,128)} %convolution_bitcast_fusion.4) | copy-start | bytes 393220
  70.8 2.1 %copy-start.13 = (f32[1,128,256]{2,1,0:T(8,128)S(1)}, f32[1,128,256]{2,1,0:T(8,128)}, u32[]{:S(2)}) copy-start(f32[1,128,256]{2,1,0:T(8,128)} %convolution_bitcast_fusion.5) | copy-start | bytes 393220
  70.8 2.1 %copy-start.18 = (f32[1,128,256]{2,1,0:T(8,128)S(1)}, f32[1,128,256]{2,1,0:T(8,128)}, u32[]{:S(2)}) copy-start(f32[1,128,256]{2,1,0:T(8,128)} %convolution_bitcast_fusion.6) | copy-start | bytes 393220
  70.9 2.1 %copy-start.19 = (f32[1,128,256]{2,1,0:T(8,128)S(1)}, f32[1,128,256]{2,1,0:T(8,128)}, u32[]{:S(2)}) copy-start(f32[1,128,256]{2,1,0:T(8,128)} %convolution_bitcast_fusion.3) | copy-start | bytes 393220
  74.6 1.3 copy-start.6
  74.6 1.3 copy-start.17
  75.6 0.9 copy-start.16
  76.6 1.5 copy-start.2
  76.6 3.8 %copy-start.9 = (f32[36,8,5,128]{3,1,2,0:T(8,128)S(1)}, f32[36,8,5,128]{3,1,2,0:T(8,128)}, u32[]{:S(2)}) copy-start(f32[36,8,5,128]{3,1,2,0:T(8,128)} %get-tuple-element.34) | copy-start | bytes 2211844
  78.1 8.4 %collective-permute-start.4 = (f32[64,4864]{1,0:T(8,128)}, f32[64,4864]{1,0:T(8,128)}, u32[]{:S(2)}, u32[]{:S(2)}) collective-permute-start(f32[64,4864]{1,0:T(8,128)} %fusion.18), channel_id=1, source_target_pairs={{0,1},{1,0},{2,3},{3,2},{4,5},{5,4},{6,7},{7,6},{8,9},{9,8},{10,11... | collective-permute-start | bytes 3735560 | tf_op jit(solution)/shard_map/ppermute | solution.py:94
  80.8 1.1 copy-start.24
  80.8 1.1 copy-start.25
  82.9 1.1 copy-start.8
  84.0 1.1 copy-start.5
  85.5 0.7 copy-start.21
  85.6 1.3 copy-start.3
  88.5 11.7 %collective-permute-start.11 = (f32[32,2432]{1,0:T(8,128)S(1)}, f32[32,2432]{1,0:T(8,128)S(1)}, u32[]{:S(2)}, u32[]{:S(2)}) collective-permute-start(f32[32,2432]{1,0:T(8,128)S(1)} %constant_dynamic-slice_fusion.5), channel_id=1, source_target_pairs={{0,16},{16,0},{32,48},{48,32},{64,80},{80,64},{96,112},{112,96},{1... | collective-permute-start | bytes 933896 | tf_op jit(solution)/shard_map/ppermute | solution.py:94
  90.5 12.6 %collective-permute-start.5 = (f32[32,2432]{1,0:T(8,128)S(1)}, f32[32,2432]{1,0:T(8,128)S(1)}, u32[]{:S(2)}, u32[]{:S(2)}) collective-permute-start(f32[32,2432]{1,0:T(8,128)S(1)} %constant_dynamic-slice_fusion.11), channel_id=1, source_target_pairs={{0,2},{2,0},{4,6},{6,4},{8,10},{10,8},{12,14},{14,12},{1,3},{3,1},... | collective-permute-start | bytes 933896 | tf_op jit(solution)/shard_map/ppermute | solution.py:94
  100.2 11.7 %collective-permute-start.12 = (f32[16,2432]{1,0:T(8,128)S(1)}, f32[16,2432]{1,0:T(8,128)S(1)}, u32[]{:S(2)}, u32[]{:S(2)}) collective-permute-start(f32[16,2432]{1,0:T(8,128)S(1)} %constant_dynamic-slice_fusion.4), channel_id=1, source_target_pairs={{0,32},{16,48},{32,0},{48,16},{64,96},{80,112},{96,64},{112,80},{1... | collective-permute-start | bytes 466952 | tf_op jit(solution)/shard_map/ppermute | solution.py:94
  103.1 11.9 %collective-permute-start.6 = (f32[16,2432]{1,0:T(8,128)S(1)}, f32[16,2432]{1,0:T(8,128)S(1)}, u32[]{:S(2)}, u32[]{:S(2)}) collective-permute-start(f32[16,2432]{1,0:T(8,128)S(1)} %constant_dynamic-slice_fusion.10), channel_id=1, source_target_pairs={{0,4},{2,6},{4,0},{6,2},{8,12},{10,14},{12,8},{14,10},{1,5},{3,7},... | collective-permute-start | bytes 466952 | tf_op jit(solution)/shard_map/ppermute | solution.py:94
  112.0 10.2 %collective-permute-start.13 = (f32[8,2432]{1,0:T(8,128)S(1)}, f32[8,2432]{1,0:T(8,128)S(1)}, u32[]{:S(2)}, u32[]{:S(2)}) collective-permute-start(f32[8,2432]{1,0:T(8,128)S(1)} %constant_dynamic-slice_fusion.3), channel_id=1, source_target_pairs={{0,64},{16,80},{32,96},{48,112},{64,0},{80,16},{96,32},{112,48},{1... | collective-permute-start | bytes 233480 | tf_op jit(solution)/shard_map/ppermute | solution.py:94
  115.0 11.7 %collective-permute-start.7 = (f32[8,2432]{1,0:T(8,128)S(1)}, f32[8,2432]{1,0:T(8,128)S(1)}, u32[]{:S(2)}, u32[]{:S(2)}) collective-permute-start(f32[8,2432]{1,0:T(8,128)S(1)} %constant_dynamic-slice_fusion.9), channel_id=1, source_target_pairs={{0,8},{2,10},{4,12},{6,14},{8,0},{10,2},{12,4},{14,6},{1,9},{3,11}... | collective-permute-start | bytes 233480 | tf_op jit(solution)/shard_map/ppermute | solution.py:94
  122.2 6.9 %collective-permute-start.14 = (f32[4,2432]{1,0:T(4,128)S(1)}, f32[4,2432]{1,0:T(4,128)S(1)}, u32[]{:S(2)}, u32[]{:S(2)}) collective-permute-start(f32[4,2432]{1,0:T(4,128)S(1)} %constant_dynamic-slice_fusion.2), channel_id=1, source_target_pairs={{0,2},{2,0},{4,6},{6,4},{8,10},{10,8},{12,14},{14,12},{1,3},{3,1},... | collective-permute-start | bytes 116744 | tf_op jit(solution)/shard_map/ppermute | solution.py:94
  126.7 5.9 %collective-permute-start.8 = (f32[4,2432]{1,0:T(4,128)S(1)}, f32[4,2432]{1,0:T(4,128)S(1)}, u32[]{:S(2)}, u32[]{:S(2)}) collective-permute-start(f32[4,2432]{1,0:T(4,128)S(1)} %constant_dynamic-slice_fusion.8), channel_id=1, source_target_pairs={{0,16},{16,0},{32,48},{48,32},{64,80},{80,64},{96,112},{112,96},{1... | collective-permute-start | bytes 116744 | tf_op jit(solution)/shard_map/ppermute | solution.py:94
  129.1 6.6 %collective-permute-start.15 = (f32[2,2432]{1,0:T(2,128)S(1)}, f32[2,2432]{1,0:T(2,128)S(1)}, u32[]{:S(2)}, u32[]{:S(2)}) collective-permute-start(f32[2,2432]{1,0:T(2,128)S(1)} %constant_dynamic-slice_fusion.1), channel_id=1, source_target_pairs={{0,4},{2,6},{4,0},{6,2},{8,12},{10,14},{12,8},{14,10},{1,5},{3,7},... | collective-permute-start | bytes 58376 | tf_op jit(solution)/shard_map/ppermute | solution.py:94
  132.6 6.6 %collective-permute-start.9 = (f32[2,2432]{1,0:T(2,128)S(1)}, f32[2,2432]{1,0:T(2,128)S(1)}, u32[]{:S(2)}, u32[]{:S(2)}) collective-permute-start(f32[2,2432]{1,0:T(2,128)S(1)} %constant_dynamic-slice_fusion.7), channel_id=1, source_target_pairs={{0,32},{16,48},{32,0},{48,16},{64,96},{80,112},{96,64},{112,80},{1... | collective-permute-start | bytes 58376 | tf_op jit(solution)/shard_map/ppermute | solution.py:94
  135.7 9.5 %collective-permute-start.16 = (f32[1,2432]{1,0:T(1,128)S(1)}, f32[1,2432]{1,0:T(1,128)S(1)}, u32[]{:S(2)}, u32[]{:S(2)}) collective-permute-start(f32[1,2432]{1,0:T(1,128)S(1)} %constant_dynamic-slice_fusion), channel_id=1, source_target_pairs={{0,8},{2,10},{4,12},{6,14},{8,0},{10,2},{12,4},{14,6},{1,9},{3,11}... | collective-permute-start | bytes 29192 | tf_op jit(solution)/shard_map/ppermute | solution.py:94
  139.3 9.5 %collective-permute-start.10 = (f32[1,2432]{1,0:T(1,128)S(1)}, f32[1,2432]{1,0:T(1,128)S(1)}, u32[]{:S(2)}, u32[]{:S(2)}) collective-permute-start(f32[1,2432]{1,0:T(1,128)S(1)} %constant_dynamic-slice_fusion.6), channel_id=1, source_target_pairs={{0,64},{16,80},{32,96},{48,112},{64,0},{80,16},{96,32},{112,48},{1... | collective-permute-start | bytes 29192 | tf_op jit(solution)/shard_map/ppermute | solution.py:94
  148.8 5.7 %collective-permute-start.17 = (f32[1,4864]{1,0:T(1,128)S(1)}, f32[1,4864]{1,0:T(1,128)S(1)}, u32[]{:S(2)}, u32[]{:S(2)}) collective-permute-start(f32[1,4864]{1,0:T(1,128)S(1)} %pad_maximum_fusion.49), channel_id=1, source_target_pairs={{0,128},{128,0},{256,384},{384,256},{1,129},{129,1},{257,385},{385... | collective-permute-start | bytes 58376 | tf_op jit(solution)/shard_map/ppermute | solution.py:94
  153.1 4.8 %copy-start.7 = (bf16[1,1,32,32,256]{4,3,2,1,0:T(8,128)(2,1)S(1)}, bf16[1,1,32,32,256]{4,3,2,1,0:T(8,128)(2,1)}, u32[]{:S(2)}) copy-start(bf16[1,1,32,32,256]{4,3,2,1,0:T(8,128)(2,1)} %param.9) | copy-start | bytes 1572868
  154.5 7.2 %collective-permute-start.18 = (f32[1,4864]{1,0:T(1,128)S(1)}, f32[1,4864]{1,0:T(1,128)S(1)}, u32[]{:S(2)}, u32[]{:S(2)}) collective-permute-start(f32[1,4864]{1,0:T(1,128)S(1)} %fusion.142), channel_id=1, source_target_pairs={{0,256},{128,384},{256,0},{384,128},{1,257},{129,385},{257,1},{385... | collective-permute-start | bytes 58376 | tf_op jit(solution)/shard_map/ppermute | solution.py:94
